TPU v7x, 1024 devices: a whole 4x8x16 slice. The times are simulated.
1024 devices in a mesh: ctx: 128 (over z, y), exp: 8 (over x, core).
Axes of the slice: x: 4, y: 8, z: 16, core: 2. Of those that a mesh axis runs over, the one named last changes fastest.
Arguments:
- scan_grad: bfloat16 [32768, 8192], P('ctx', 'exp'), may hold values from -6 to 6
- step_size: bfloat16 [32768, 8192], P('ctx', 'exp'), may hold values from 0.3 to 4.5, as said below
- scan_input: bfloat16 [32768, 8192], P('ctx', 'exp'), may hold values from -6 to 6
- state_in: float32 [32768, 16], P('ctx'), may hold values from -2 to 2
- state_out: float32 [32768, 16], P('ctx'), may hold values from -0.5 to 0.5
- decay_rate: float32 [16, 8192], P(None, 'exp'), may hold values from -1 to 0, as said below
- skip_gain: float32 [8192], P('exp'), may hold values from 0.5 to 1.5
Outputs:
- scan_input_grad: bfloat16 [32768, 8192], P('ctx', 'exp')
- state_in_grad: float32 [16, 32768], P(None, ('ctx', 'exp'))
Inputs may be any that keep to these rules, and one draw needn't show every extreme that they name: `step_size`: Positive. `decay_rate`: Negative.
All inputs are finite; a program needn't handle non-finite values.
Results may differ from a plain program's by a relative error of at most 0.0015.
Values sent between devices are 32-bit elements; how exact they have to be, the bound alone decides.
No kernel may reach another device: no remote copies, remote signals or barrier semaphores. Data moves between devices by JAX's collectives and lax.ppermute only.
A program may use at most 64 MiB of HBM per device.

v0:
```python
import math

import jax
import jax.numpy as jnp
from jax import lax
from jax.sharding import PartitionSpec as P


def carried_in(array, axis, combine, identity):
    size, position = (lax.axis_size(axis), lax.axis_index(axis))
    everything = jax.tree.map(lambda part: lax.all_gather(part, axis), array)
    start = jax.tree.map(
        lambda part, zero: jnp.broadcast_to(jnp.asarray(zero, part.dtype), part.shape),
        array,
        identity,
    )

    def step(k, before):
        at = size - 1 - k
        reached = at > position
        new = combine(before, jax.tree.map(lambda part: part[at], everything))
        return jax.tree.map(lambda a, b: jnp.where(reached, a, b), new, before)

    return lax.fori_loop(0, size, step, start)


def unit_steps(incoming, row_block, decay_rate, skip_gain):
    grad_part, step_part, input_part, in_part, out_part = row_block
    results = []
    b_rows = []
    for offset in range(grad_part.shape[0] - 1, -1, -1):
        grad_row = grad_part[offset].astype(jnp.float32)
        step_row = step_part[offset].astype(jnp.float32)
        input_row = input_part[offset].astype(jnp.float32)
        adjoint = out_part[offset][:, None] * grad_row[None, :] + incoming
        results.append(
            step_row * jnp.sum(in_part[offset][:, None] * adjoint, axis=0) + skip_gain * grad_row
        )
        b_rows.append(jnp.sum(adjoint * (step_row * input_row)[None, :], axis=1))
        incoming = jnp.exp(step_row[None, :] * decay_rate) * adjoint
    return (incoming, (jnp.stack(results[::-1]), jnp.stack(b_rows[::-1])))


def local_sweep(
    scan_grad, step_size, scan_input, state_in, state_out, decay_rate, skip_gain, incoming
):
    row_count, channels = scan_grad.shape
    block_size = 32
    block_count = row_count // block_size

    def sweep_block(carry_state, row_block):
        return unit_steps(carry_state, row_block, decay_rate, skip_gain)

    stacked = (
        scan_grad.reshape(block_count, block_size, channels),
        step_size.reshape(block_count, block_size, channels),
        scan_input.reshape(block_count, block_size, channels),
        state_in.reshape(block_count, block_size, -1),
        state_out.reshape(block_count, block_size, -1),
    )
    final_state, outputs = lax.scan(sweep_block, incoming, stacked, reverse=True)
    grads_all, b_all = outputs
    return (final_state, grads_all.reshape(row_count, channels), b_all.reshape(row_count, -1))


def running_steps(step_size):
    row_count = step_size.shape[0]
    row_index = lax.broadcasted_iota(jnp.int32, (row_count, row_count), 0)
    column_index = lax.broadcasted_iota(jnp.int32, (row_count, row_count), 1)
    tri_table = column_index <= row_index
    return jnp.dot(tri_table.astype(jnp.bfloat16), step_size, preferred_element_type=jnp.float32)


def group_summary(scan_grad, reach_sum, state_out, decay_rate):
    row_count, channels = scan_grad.shape
    block_size = 32
    block_count = row_count // block_size

    def add_block(accum, pieces):
        reach_part, grad_part, out_part = pieces
        decay_weight = jnp.exp(decay_rate[None, :, :] * reach_part[:, None, :])
        term = jnp.einsum(
            "tnc,tn,tc->nc",
            decay_weight,
            out_part,
            grad_part.astype(jnp.float32),
            precision=lax.Precision.HIGHEST,
        )
        return (accum + term, None)

    pieces = (
        reach_sum.reshape(block_count, block_size, channels),
        scan_grad.reshape(block_count, block_size, channels),
        state_out.reshape(block_count, block_size, -1),
    )
    summary, _ = lax.scan(add_block, jnp.zeros(decay_rate.shape, jnp.float32), pieces)
    return summary


def carry_in(total_decay, summary):

    def combine(earlier, later):
        return (later[0] * earlier[0], later[0] * earlier[1] + later[1])

    neutral = (jnp.ones_like(total_decay), jnp.zeros_like(summary))
    return carried_in((total_decay, summary), "ctx", combine, neutral)[1]


def shards(scan_grad, step_size, scan_input, state_in, state_out, decay_rate, skip_gain):
    num_rows = scan_grad.shape[0]
    reach_sum = running_steps(step_size)
    summary = group_summary(scan_grad, reach_sum, state_out, decay_rate)
    total_decay = jnp.exp(decay_rate * reach_sum[num_rows - 1][None, :])
    carried = carry_in(total_decay, summary)
    _, input_grad, b_local = local_sweep(
        scan_grad, step_size, scan_input, state_in, state_out, decay_rate, skip_gain, carried
    )
    scan_input_grad = input_grad.astype(jnp.bfloat16)
    all_channels = scan_grad.shape[1] * lax.axis_size("exp")
    b_term = jnp.transpose(b_local) * (1.0 / math.sqrt(all_channels))
    state_in_grad = lax.psum_scatter(b_term, "exp", scatter_dimension=1, tiled=True)
    return (scan_input_grad, state_in_grad)


def solution(mesh):
    in_specs = (
        P("ctx", "exp"),
        P("ctx", "exp"),
        P("ctx", "exp"),
        P("ctx", None),
        P("ctx", None),
        P(None, "exp"),
        P("exp"),
    )
    out_specs = (P("ctx", "exp"), P(None, ("ctx", "exp")))
    return jax.shard_map(shards, mesh=mesh, in_specs=in_specs, out_specs=out_specs, check_vma=False)
```

profile of v0, /device:TPU:1, one launch (start us, length us, event | category | flops | bytes accessed | tf_op | source)
XLA Modules:
  0.0 629.1 jit_solution(13336787435839462404)
XLA Ops:
  7.2 1.3 fusion.161
  9.4 18.6 %while.46 = (s32[]{:T(128)}, f32[16,1024]{1,0:T(8,128)S(1)}, f32[16,1024]{1,0:T(8,128)}, f32[8,32,1024]{2,1,0:T(8,128)S(1)}, f32[8,32,16]{1,0,2:T(8,128)S(1)}, /...) while((s32[]{:T(128)}, f32[16,1024]{1,0:T(8,128)S(1)}, f32[16,1024]{1,0:T(8,128)}, ...), condition=%wide.region_1.2_spmd.clone, body=%wide.region_0.1_spmd.clone.sunk | while | flops 2146307 | bytes 1058923 | solution.py:96
  10.4 1.3 multiply_reduce_fusion.84
  12.7 1.3 multiply_reduce_fusion.84
  15.0 1.3 multiply_reduce_fusion.84
  17.4 1.3 multiply_reduce_fusion.84
  19.7 1.3 multiply_reduce_fusion.84
  22.0 1.3 multiply_reduce_fusion.84
  24.3 1.3 multiply_reduce_fusion.84
  26.7 1.3 multiply_reduce_fusion.84
  28.7 1.5 multiply_exponential_fusion
  30.4 157.4 %all-gather.7.cloned.1.call-done = f32[2048,1024]{1,0:T(8,128)} async-done(((f32[16,1024]{1,0:T(8,128)}), f32[2048,1024]{1,0:T(8,128)}) %all-gather.7.cloned.1.call-update) | async-done | bytes 8388624 | tf_op jit(solution)/shard_map/all_gather | solution.py:11
  187.8 156.0 %all-gather.5.cloned.1.call-done = f32[2048,1024]{1,0:T(8,128)} async-done(((f32[16,1024]{1,0:T(8,128)}), f32[2048,1024]{1,0:T(8,128)}) %all-gather.5.cloned.1.call-update) | async-done | bytes 8388624 | tf_op jit(solution)/shard_map/all_gather | solution.py:11
  343.8 121.1 %while.47 = (s32[]{:T(128)}, f32[16,1024]{1,0:T(8,128)S(1)}, s32[]{:T(128)}, f32[128,16,1024]{2,1,0:T(8,128)}, f32[128,16,1024]{2,1,0:T(8,128)}, /*index=5*/s32[]{:T(128)}, s32[]{:T(128)}, s32[]{:T(128)}, s32[]{:T(128)}) while((s32[]{:T(128)}, f32[16,1024]{1,0:T(8,128)S(1)}, s32[]{:T(128)}, f32[128,16,1024]{2,1,0:T(8,128)}, ...), condition=%wide.region_3.4_spmd.clone, body=%wide.region_2.3_spmd.clone.sunk | while | flops 65544 | bytes 262307 | solution.py:24
  465.0 113.4 %while.45 = (s32[]{:T(128)}, f32[16,1024]{1,0:T(8,128)S(1)}, bf16[8,32,1024]{2,1,0:T(8,128)(2,1)S(1)}, f32[8,32,16]{2,1,0:T(8,128)S(1)}, bf16[8,32,1024]{2,1,0:T...) while((s32[]{:T(128)}, f32[16,1024]{1,0:T(8,128)S(1)}, ...), condition=%wide.region_69.70_spmd, body=%wide.region_4.69_spmd.sunk | while | flops 5439010 | bytes 5386649 | solution.py:61
  473.4 1.3 fusion.185
  493.3 1.3 fusion.182
  508.7 1.3 fusion.179
  528.1 1.2 fusion.180
  530.2 1.2 fusion.185
  544.4 1.3 fusion.185
  564.3 1.2 fusion.182
  579.2 42.0 %reduce-scatter.4.cloned.1.call-done = f32[32,16]{1,0:T(8,128)} async-done(((f32[256,16]{1,0:T(8,128)}), f32[32,16]{1,0:T(8,128)}) %reduce-scatter.4.cloned.1.call-update) | async-done | bytes 2064
  621.1 1.4 copy.30
  (937 shorter events, 228.7 us)
Async XLA Ops:
  7.2 180.6 %all-gather.7.cloned.1.call-start = ((), (), s32[]{:S(2)}) async-start(), calls=%async_computation.2 | async-start | bytes 8454144 | tf_op jit(solution)/shard_map/all_gather | solution.py:11
  9.4 20.9 %copy-start.4 = (f32[256,16]{0,1:T(8,128)S(1)}, f32[256,16]{0,1:T(8,128)}, u32[]{:S(2)}) copy-start(f32[256,16]{0,1:T(8,128)} %param.16) | copy-start | bytes 49156
  28.0 0.6 copy-start.2
  28.0 436.9 %copy-start = (f32[16,1024]{1,0:T(8,128)S(1)}, f32[16,1024]{1,0:T(8,128)}, u32[]{:S(2)}) copy-start(f32[16,1024]{1,0:T(8,128)} %get-tuple-element.1673) | copy-start | bytes 196612
  28.0 436.9 %copy-start.1 = (f32[1024]{0:T(1024)S(1)}, f32[1024]{0:T(1024)}, u32[]{:S(2)}) copy-start(f32[1024]{0:T(1024)} %param.19) | copy-start | bytes 12292
  28.7 315.1 %all-gather.5.cloned.1.call-start = ((), (), s32[]{:S(2)}) async-start(), calls=%async_computation.1 | async-start | bytes 8454144 | tf_op jit(solution)/shard_map/all_gather | solution.py:11
  30.2 590.9 %reduce-scatter.4.cloned.1.call-start = ((), (), s32[]{:S(2)}) async-start(), calls=%async_computation.3 | async-start | bytes 147456
  578.4 44.1 %copy-start.3 = (bf16[8,32,1024]{2,1,0:T(8,128)(2,1)}, bf16[8,32,1024]{2,1,0:T(8,128)(2,1)S(1)}, u32[]{:S(2)}) copy-start(bf16[8,32,1024]{2,1,0:T(8,128)(2,1)S(1)} %get-tuple-element.386) | copy-start | bytes 1572868
Sparse Core Ops, SparseCore 0:
  28.8 158.9 all-gather.6
  192.4 151.2 all-gather.4
  579.3 41.8 reduce-scatter.3
where the time goes:
time: 640 us; the launch traced here: 629 us
  waiting for transfers between devices  355 us (55%)
  other arithmetic  217 us (34%)
  local copies, waits for them, and re-layouts  34 us (5%)
  between operations  13.9 us (2%)
  loops' own time  7.63 us (1%)
    all_gather x2, waiting for transfers between devices, carried_in(): everything = jax.tree.map(lambda part: lax.all_gather(part, axis), array)  313 us
    select_n x128, other arithmetic, step(): return jax.tree.map(lambda a, b: jnp.where(reached, a, b), new, before)  117 us
    unnamed x4, waiting for transfers between devices  42 us
    reduce_sum x72, other arithmetic, unit_steps(): b_rows.append(jnp.sum(adjoint * (step_row * input_row)[None, :], axis=1))  20.7 us
    while x256, local copies, waits for them, and re-layouts  20.3 us
    convert_element_type x16, other arithmetic, unit_steps(): input_row = input_part[offset].astype(jnp.float32)  18.7 us
    convert_element_type x16, other arithmetic, unit_steps(): grad_row = grad_part[offset].astype(jnp.float32)  18.4 us
    convert_element_type x16, other arithmetic, unit_steps(): step_row = step_part[offset].astype(jnp.float32)  18.3 us
  transfers between devices with their start and end apart: 3, of which 3 were waited for; matrix products, arithmetic and copies ran while one was open for 0% of the time, Pallas kernels for 0%

commit v1 on v0

v1 whole, which is shorter than its diff:
```python
import math

import jax
import jax.numpy as jnp
from jax import lax
from jax.experimental import pallas as pl
from jax.experimental.pallas import tpu as pltpu
from jax.sharding import PartitionSpec as P

LANES = 128


def tiled(column_block, tiles):
    return jnp.concatenate([column_block] * tiles, axis=1)


def summary_kernel(g_ref, s_ref, outb_ref, a_ref, sum_ref, tot_ref, gf, sf):
    rows, channels = g_ref.shape
    tiles = channels // LANES
    gf[...] = g_ref[...].astype(jnp.float32)
    sf[...] = s_ref[...].astype(jnp.float32)
    tot_ref[...] = jnp.sum(sf[...], axis=0, keepdims=True)
    a = a_ref[...]

    def body(i, incoming):
        t = rows - 1 - i
        g_row = gf[pl.ds(t, 1), :]
        s_row = sf[pl.ds(t, 1), :]
        adjoint = tiled(outb_ref[t], tiles) * g_row + incoming
        return jnp.exp(s_row * a) * adjoint

    sum_ref[...] = lax.fori_loop(0, rows, body, jnp.zeros(a.shape, jnp.float32), unroll=8)


def sweep_kernel(
    g_ref, s_ref, x_ref, inb_ref, outb_ref, a_ref, skip_ref, inc_ref,
    res_ref, bp_ref, gf, sf, wf, rf,
):
    rows, channels = g_ref.shape
    tiles = channels // LANES
    gf[...] = g_ref[...].astype(jnp.float32)
    sf[...] = s_ref[...].astype(jnp.float32)
    wf[...] = sf[...] * x_ref[...].astype(jnp.float32)
    a = a_ref[...]
    skip = skip_ref[...]

    def body(i, incoming):
        t = rows - 1 - i
        g_row = gf[pl.ds(t, 1), :]
        s_row = sf[pl.ds(t, 1), :]
        w_row = wf[pl.ds(t, 1), :]
        adjoint = tiled(outb_ref[t], tiles) * g_row + incoming
        mixed = jnp.sum(tiled(inb_ref[t], tiles) * adjoint, axis=0, keepdims=True)
        rf[pl.ds(t, 1), :] = s_row * mixed + skip * g_row
        weighted = adjoint * w_row
        part = weighted[:, 0:LANES]
        for k in range(1, tiles):
            part = part + weighted[:, k * LANES:(k + 1) * LANES]
        bp_ref[t] = part
        return jnp.exp(s_row * a) * adjoint

    lax.fori_loop(0, rows, body, inc_ref[...], unroll=8)
    res_ref[...] = rf[...].astype(res_ref.dtype)


def vmem_spec():
    return pl.BlockSpec(memory_space=pltpu.VMEM)


def shard_summary(scan_grad, step_size, out_b, decay_rate):
    rows, channels = scan_grad.shape
    return pl.pallas_call(
        summary_kernel,
        out_shape=(
            jax.ShapeDtypeStruct(decay_rate.shape, jnp.float32),
            jax.ShapeDtypeStruct((1, channels), jnp.float32),
        ),
        in_specs=[vmem_spec()] * 4,
        out_specs=(vmem_spec(), vmem_spec()),
        scratch_shapes=[pltpu.VMEM((rows, channels), jnp.float32)] * 2,
        cost_estimate=pl.CostEstimate(
            flops=6 * rows * decay_rate.size,
            transcendentals=rows * decay_rate.size,
            bytes_accessed=4 * rows * channels + 4 * out_b.size,
        ),
    )(scan_grad, step_size, out_b, decay_rate)


def shard_sweep(scan_grad, step_size, scan_input, in_b, out_b, decay_rate, skip_gain, incoming):
    rows, channels = scan_grad.shape
    states = decay_rate.shape[0]
    return pl.pallas_call(
        sweep_kernel,
        out_shape=(
            jax.ShapeDtypeStruct((rows, channels), jnp.bfloat16),
            jax.ShapeDtypeStruct((rows, states, LANES), jnp.float32),
        ),
        in_specs=[vmem_spec()] * 8,
        out_specs=(vmem_spec(), vmem_spec()),
        scratch_shapes=[pltpu.VMEM((rows, channels), jnp.float32)] * 4,
        cost_estimate=pl.CostEstimate(
            flops=12 * rows * decay_rate.size,
            transcendentals=rows * decay_rate.size,
            bytes_accessed=8 * rows * channels + 4 * (in_b.size + out_b.size) * 2,
        ),
    )(scan_grad, step_size, scan_input, in_b, out_b, decay_rate, skip_gain, incoming)


def carry_in(summary, total, decay_rate):
    size = lax.axis_size("ctx")
    states = summary.shape[0]
    packed = jnp.concatenate([summary, total], axis=0)
    packed = lax.ppermute(packed, "ctx", [(q, q - 1) for q in range(1, size)])
    reach = 1
    while reach < size:
        got = lax.ppermute(packed, "ctx", [(q, q - reach) for q in range(reach, size)])
        own_s, own_r = packed[:states], packed[states:]
        new_s = own_s + jnp.exp(decay_rate * own_r) * got[:states]
        packed = jnp.concatenate([new_s, own_r + got[states:]], axis=0)
        reach *= 2
    return packed[:states]


def shards(scan_grad, step_size, scan_input, state_in, state_out, decay_rate, skip_gain):
    rows = scan_grad.shape[0]
    states = state_in.shape[1]
    in_b = jnp.broadcast_to(state_in[:, :, None], (rows, states, LANES))
    out_b = jnp.broadcast_to(state_out[:, :, None], (rows, states, LANES))
    summary, total = shard_summary(scan_grad, step_size, out_b, decay_rate)
    carried = carry_in(summary, total, decay_rate)
    scan_input_grad, b_part = shard_sweep(
        scan_grad, step_size, scan_input, in_b, out_b, decay_rate, skip_gain[None, :], carried
    )
    all_channels = scan_grad.shape[1] * lax.axis_size("exp")
    b_term = jnp.transpose(jnp.sum(b_part, axis=2)) * (1.0 / math.sqrt(all_channels))
    state_in_grad = lax.psum_scatter(b_term, "exp", scatter_dimension=1, tiled=True)
    return (scan_input_grad, state_in_grad)


def solution(mesh):
    in_specs = (
        P("ctx", "exp"),
        P("ctx", "exp"),
        P("ctx", "exp"),
        P("ctx", None),
        P("ctx", None),
        P(None, "exp"),
        P("exp"),
    )
    out_specs = (P("ctx", "exp"), P(None, ("ctx", "exp")))
    return jax.shard_map(shards, mesh=mesh, in_specs=in_specs, out_specs=out_specs, check_vma=False)
```

time: 640 us -> 181 us (0.28); the launches traced: 629 us -> 180 us
  waiting for transfers between devices: 355 us -> 125 us
  other arithmetic: 217 us -> 4.63 us
  local copies, waits for them, and re-layouts: 34 us -> 6.18 us
  Pallas kernels: 0 us -> 20.2 us
  starting transfers between devices: 0.12 us -> 10.4 us
  loops' own time: 7.63 us -> 0 us
    all_gather x2 -> x0, waiting for transfers between devices: 313 us -> none  [carried_in(): everything = jax.tree.map(lambda part: lax.all_gather(part, axis), array)]
    select_n x128 -> x0, other arithmetic: 117 us -> none  [step(): return jax.tree.map(lambda a, b: jnp.where(reached, a, b), new, before)]
    ppermute x0 -> x8, waiting for transfers between devices: none -> 65.9 us  [the longest x7 61.1 us: carry_in(): lax.ppermute(packed, 'ctx', [(q, q - reach) for q in range(reach, size)])]
    convert_element_type x48 -> x0, other arithmetic: 55.5 us -> none  [the longest x16 18.7 us: unit_steps(): input_row = input_part[offset].astype(jnp.float32)]
    while x256 -> x0, local copies, waits for them, and re-layouts: 20.3 us -> none
    pallas_call x0 -> x2, Pallas kernels: none -> 20.2 us  [the longest x1 13.2 us: shard_sweep(): pl.pallas_call(sweep_kernel, out_shape=(jax.ShapeDtypeStruct((rows, chann...]
    reduce_sum x72 -> x1, other arithmetic: 20.7 us -> 2.21 us  [shards(): jnp.sum(b_part, axis=2)]
    unnamed x4 -> x2, waiting for transfers between devices: 42 us -> 58.9 us
  transfers between devices with their start and end apart: 3 -> 9, of which waited for: 3 -> 9; matrix products, arithmetic and copies ran while one was open for 0% -> 0% of each run, Pallas kernels for 0% -> 0%
where the time goes in v1:
time: 181 us; the launch traced here: 180 us
  waiting for transfers between devices  125 us (69%)
  Pallas kernels  20.2 us (11%)
  between operations  14.2 us (8%)
  starting transfers between devices  10.4 us (6%)
  local copies, waits for them, and re-layouts  6.18 us (3%)
  other arithmetic  4.63 us (3%)
    ppermute x7, waiting for transfers between devices, carry_in(): lax.ppermute(packed, 'ctx', [(q, q - reach) for q in range(reach, size)])  61.1 us
    unnamed x2, waiting for transfers between devices  58.9 us
    pallas_call x1, Pallas kernels, shard_sweep(): pl.pallas_call(sweep_kernel, out_shape=(jax.ShapeDtypeStruct((rows, chann...  13.2 us
    ppermute x7, starting transfers between devices, carry_in(): lax.ppermute(packed, 'ctx', [(q, q - reach) for q in range(reach, size)])  9.03 us
    pallas_call x1, Pallas kernels, shard_summary(): pl.pallas_call(summary_kernel, out_shape=(jax.ShapeDtypeStruct(decay_rate...  7.01 us
    ppermute x1, waiting for transfers between devices, carry_in(): packed = lax.ppermute(packed, 'ctx', [(q, q - 1) for q in range(1, size)])  4.73 us
  transfers between devices with their start and end apart: 9, of which 9 were waited for; matrix products, arithmetic and copies ran while one was open for 0% of the time, Pallas kernels for 0%

profile of v1, /device:TPU:1, one launch (start us, length us, event | category | flops | bytes accessed | tf_op | source)
XLA Modules:
  0.0 180.3 jit_solution(2552986183637213978)
XLA Ops:
  8.0 1.9 %broadcast_in_dim.7.outb_ref = f32[256,16,128]{2,1,0:T(8,128)} broadcast(f32[256,16]{1,0:T(8,128)S(1)} %copy.12), dimensions={0,1} | broadcast | bytes 2113536 | tf_op jit(solution)/shard_map/broadcast_in_dim | solution.py:128
  10.0 7.0 %shard_map.86 = (f32[16,1024]{1,0:T(8,128)}, f32[1,1024]{1,0:T(1,128)}) custom-call(bf16[256,1024]{1,0:T(8,128)(2,1)} %g_ref.3, bf16[256,1024]{1,0:T(8,128)(2,1)} %s_ref.3, f32[256,16,128]{2,1,0:T(8,128)} %broadcast_in_dim.7.outb_ref, f32[16,1024]{1,0:T(8,128)} %a_ref.3), custom_call_target="tpu_custom_call" | custom-call | flops 25165824 | bytes 3145728 | tf_op jit(solution)/shard_map/pallas_call | solution.py:72
  17.0 0.9 pad_maximum_fusion
  17.9 1.3 collective-permute-start
  19.1 4.7 %collective-permute-done = f32[17,1024]{1,0:T(8,128)S(1)} collective-permute-done((f32[17,1024]{1,0:T(8,128)S(1)}, f32[17,1024]{1,0:T(8,128)S(1)}, u32[]{:S(2)}, u32[]{:S(2)}) %collective-permute-start) | collective-permute-done | bytes 69664 | tf_op jit(solution)/shard_map/ppermute | solution.py:113
  23.9 1.3 collective-permute-start.1
  25.2 4.1 %collective-permute-done.1 = f32[17,1024]{1,0:T(8,128)S(1)} collective-permute-done((f32[17,1024]{1,0:T(8,128)S(1)}, f32[17,1024]{1,0:T(8,128)S(1)}, u32[]{:S(2)}, u32[]{:S(2)}) %collective-permute-start.1) | collective-permute-done | bytes 69664 | tf_op jit(solution)/shard_map/ppermute | solution.py:116
  29.3 1.3 collective-permute-start.2
  30.6 6.1 %collective-permute-done.2 = f32[17,1024]{1,0:T(8,128)S(1)} collective-permute-done((f32[17,1024]{1,0:T(8,128)S(1)}, f32[17,1024]{1,0:T(8,128)S(1)}, u32[]{:S(2)}, u32[]{:S(2)}) %collective-permute-start.2) | collective-permute-done | bytes 69664 | tf_op jit(solution)/shard_map/ppermute | solution.py:116
  36.8 1.3 collective-permute-start.3
  38.1 8.0 %collective-permute-done.3 = f32[17,1024]{1,0:T(8,128)S(1)} collective-permute-done((f32[17,1024]{1,0:T(8,128)S(1)}, f32[17,1024]{1,0:T(8,128)S(1)}, u32[]{:S(2)}, u32[]{:S(2)}) %collective-permute-start.3) | collective-permute-done | bytes 69664 | tf_op jit(solution)/shard_map/ppermute | solution.py:116
  46.1 1.3 collective-permute-start.4
  47.4 7.3 %collective-permute-done.4 = f32[17,1024]{1,0:T(8,128)S(1)} collective-permute-done((f32[17,1024]{1,0:T(8,128)S(1)}, f32[17,1024]{1,0:T(8,128)S(1)}, u32[]{:S(2)}, u32[]{:S(2)}) %collective-permute-start.4) | collective-permute-done | bytes 69664 | tf_op jit(solution)/shard_map/ppermute | solution.py:116
  54.8 1.3 collective-permute-start.5
  56.1 7.4 %collective-permute-done.5 = f32[17,1024]{1,0:T(8,128)S(1)} collective-permute-done((f32[17,1024]{1,0:T(8,128)S(1)}, f32[17,1024]{1,0:T(8,128)S(1)}, u32[]{:S(2)}, u32[]{:S(2)}) %collective-permute-start.5) | collective-permute-done | bytes 69664 | tf_op jit(solution)/shard_map/ppermute | solution.py:116
  63.5 1.3 collective-permute-start.6
  64.8 12.7 %collective-permute-done.6 = f32[17,1024]{1,0:T(8,128)S(1)} collective-permute-done((f32[17,1024]{1,0:T(8,128)S(1)}, f32[17,1024]{1,0:T(8,128)S(1)}, u32[]{:S(2)}, u32[]{:S(2)}) %collective-permute-start.6) | collective-permute-done | bytes 69664 | tf_op jit(solution)/shard_map/ppermute | solution.py:116
  77.5 1.3 collective-permute-start.7
  78.9 15.6 %collective-permute-done.7 = f32[17,1024]{1,0:T(8,128)S(1)} collective-permute-done((f32[17,1024]{1,0:T(8,128)S(1)}, f32[17,1024]{1,0:T(8,128)S(1)}, u32[]{:S(2)}, u32[]{:S(2)}) %collective-permute-start.7) | collective-permute-done | bytes 69664 | tf_op jit(solution)/shard_map/ppermute | solution.py:116
  95.2 1.9 %broadcast_in_dim.6.inb_ref = f32[256,16,128]{2,1,0:T(8,128)} broadcast(f32[256,16]{1,0:T(8,128)S(1)} %copy.11), dimensions={0,1} | broadcast | bytes 2113536 | tf_op jit(solution)/shard_map/broadcast_in_dim | solution.py:127
  97.1 13.2 %shard_map.87 = (bf16[256,1024]{1,0:T(8,128)(2,1)}, f32[256,16,128]{2,1,0:T(8,128)}) custom-call(bf16[256,1024]{1,0:T(8,128)(2,1)} %g_ref.3, bf16[256,1024]{1,0:T(8,128)(2,1)} %s_ref.3, bf16[256,1024]{1,0:T(8,128)(2,1)} %x_ref.1, f32[256,16,128]{2,1,0:T(8,128)} %broadcast_in_dim.6.inb_ref, f32[256,16,128]{2,1,0:T(8,128)} %broadcast_in_dim.7.outb_ref, ...), custom_call_target="tpu_custom_call" | custom-call | flops 50331648 | bytes 10485760 | tf_op jit(solution)/shard_map/pallas_call | solution.py:92
  110.3 2.2 %reduce_sum.9 = f32[256,16]{1,0:T(8,128)S(1)} reduce(f32[256,16,128]{2,1,0:T(8,128)} %get-tuple-element.9, f32[]{:T(128)} %constant.0.clone.1), dimensions={2}, to_apply=%region_0.0 | reduce | flops 520192 | bytes 2113540 | tf_op jit(solution)/shard_map/reduce_sum | solution.py:135
  113.2 58.9 %reduce-scatter.4.cloned.1.call-done = f32[32,16]{1,0:T(8,128)} async-done(((f32[256,16]{1,0:T(8,128)}), f32[32,16]{1,0:T(8,128)}) %reduce-scatter.4.cloned.1.call-update) | async-done | bytes 2064
  172.1 1.4 copy.15
  (28 shorter events, 2.5 us)
Async XLA Ops:
  7.2 164.9 %reduce-scatter.4.cloned.1.call-start = ((), (), s32[]{:S(2)}) async-start(), calls=%async_computation.1 | async-start | bytes 147456
  10.0 19.3 %copy-start = (f32[16,1024]{1,0:T(8,128)S(1)}, f32[16,1024]{1,0:T(8,128)}, u32[]{:S(2)}) copy-start(f32[16,1024]{1,0:T(8,128)} %a_ref.3) | copy-start | bytes 196612
  17.0 61.9 %copy-start.1 = (f32[256,16]{0,1:T(8,128)S(1)}, f32[256,16]{0,1:T(8,128)}, u32[]{:S(2)}) copy-start(f32[256,16]{0,1:T(8,128)} %param.10) | copy-start | bytes 49156
  17.9 6.0 %collective-permute-start = (f32[17,1024]{1,0:T(8,128)S(1)}, f32[17,1024]{1,0:T(8,128)S(1)}, u32[]{:S(2)}, u32[]{:S(2)}) collective-permute-start(f32[17,1024]{1,0:T(8,128)S(1)} %pad_maximum_fusion), channel_id=1, source_target_pairs={{8,0},{16,8},{24,16},{32,24},{40,32},{48,40},{56,48},{64,56},{72,6... | collective-permute-start | bytes 208904 | tf_op jit(solution)/shard_map/ppermute | solution.py:113
  23.9 5.3 %collective-permute-start.1 = (f32[17,1024]{1,0:T(8,128)S(1)}, f32[17,1024]{1,0:T(8,128)S(1)}, u32[]{:S(2)}, u32[]{:S(2)}) collective-permute-start(f32[17,1024]{1,0:T(8,128)S(1)} %collective-permute-done), channel_id=1, source_target_pairs={{8,0},{16,8},{24,16},{32,24},{40,32},{48,40},{56,48},{64,56},{72,6... | collective-permute-start | bytes 208904 | tf_op jit(solution)/shard_map/ppermute | solution.py:116
  29.3 7.4 %collective-permute-start.2 = (f32[17,1024]{1,0:T(8,128)S(1)}, f32[17,1024]{1,0:T(8,128)S(1)}, u32[]{:S(2)}, u32[]{:S(2)}) collective-permute-start(f32[17,1024]{1,0:T(8,128)S(1)} %pad_maximum_fusion.1), channel_id=1, source_target_pairs={{16,0},{24,8},{32,16},{40,24},{48,32},{56,40},{64,48},{72,56},{80,... | collective-permute-start | bytes 208904 | tf_op jit(solution)/shard_map/ppermute | solution.py:116
  36.8 9.3 %collective-permute-start.3 = (f32[17,1024]{1,0:T(8,128)S(1)}, f32[17,1024]{1,0:T(8,128)S(1)}, u32[]{:S(2)}, u32[]{:S(2)}) collective-permute-start(f32[17,1024]{1,0:T(8,128)S(1)} %pad_maximum_fusion.2), channel_id=1, source_target_pairs={{32,0},{40,8},{48,16},{56,24},{64,32},{72,40},{80,48},{88,56},{96,... | collective-permute-start | bytes 208904 | tf_op jit(solution)/shard_map/ppermute | solution.py:116
  46.1 8.6 %collective-permute-start.4 = (f32[17,1024]{1,0:T(8,128)S(1)}, f32[17,1024]{1,0:T(8,128)S(1)}, u32[]{:S(2)}, u32[]{:S(2)}) collective-permute-start(f32[17,1024]{1,0:T(8,128)S(1)} %pad_maximum_fusion.3), channel_id=1, source_target_pairs={{64,0},{72,8},{80,16},{88,24},{96,32},{104,40},{112,48},{120,56},{... | collective-permute-start | bytes 208904 | tf_op jit(solution)/shard_map/ppermute | solution.py:116
  54.8 8.7 %collective-permute-start.5 = (f32[17,1024]{1,0:T(8,128)S(1)}, f32[17,1024]{1,0:T(8,128)S(1)}, u32[]{:S(2)}, u32[]{:S(2)}) collective-permute-start(f32[17,1024]{1,0:T(8,128)S(1)} %pad_maximum_fusion.4), channel_id=1, source_target_pairs={{128,0},{136,8},{144,16},{152,24},{160,32},{168,40},{176,48},{184,... | collective-permute-start | bytes 208904 | tf_op jit(solution)/shard_map/ppermute | solution.py:116
  63.5 14.0 %collective-permute-start.6 = (f32[17,1024]{1,0:T(8,128)S(1)}, f32[17,1024]{1,0:T(8,128)S(1)}, u32[]{:S(2)}, u32[]{:S(2)}) collective-permute-start(f32[17,1024]{1,0:T(8,128)S(1)} %pad_maximum_fusion.5), channel_id=1, source_target_pairs={{256,0},{264,8},{272,16},{280,24},{288,32},{296,40},{304,48},{312,... | collective-permute-start | bytes 208904 | tf_op jit(solution)/shard_map/ppermute | solution.py:116
  77.5 17.0 %collective-permute-start.7 = (f32[17,1024]{1,0:T(8,128)S(1)}, f32[17,1024]{1,0:T(8,128)S(1)}, u32[]{:S(2)}, u32[]{:S(2)}) collective-permute-start(f32[17,1024]{1,0:T(8,128)S(1)} %pad_maximum_fusion.6), channel_id=1, source_target_pairs={{512,0},{520,8},{528,16},{536,24},{544,32},{552,40},{560,48},{568,... | collective-permute-start | bytes 208904 | tf_op jit(solution)/shard_map/ppermute | solution.py:116
Sparse Core Ops, SparseCore 0:
  113.3 58.6 reduce-scatter.3

commit v2 on v1

--- a/solution.py
+++ b/solution.py
@@ -121,6 +121,22 @@
     return packed[:states]
 
 
+def halving_sum(block, axis):
+    size = lax.axis_size(axis)
+    me = lax.axis_index(axis)
+    bit = size // 2
+    while bit >= 1:
+        half = block.shape[1] // 2
+        low, high = block[:, :half], block[:, half:]
+        upper = (me // bit) % 2 == 1
+        keep = jnp.where(upper, high, low)
+        send = jnp.where(upper, low, high)
+        got = lax.ppermute(send, axis, [(e, e ^ bit) for e in range(size)])
+        block = keep + got
+        bit //= 2
+    return block
+
+
 def shards(scan_grad, step_size, scan_input, state_in, state_out, decay_rate, skip_gain):
     rows = scan_grad.shape[0]
     states = state_in.shape[1]
@@ -133,7 +149,7 @@
     )
     all_channels = scan_grad.shape[1] * lax.axis_size("exp")
     b_term = jnp.transpose(jnp.sum(b_part, axis=2)) * (1.0 / math.sqrt(all_channels))
-    state_in_grad = lax.psum_scatter(b_term, "exp", scatter_dimension=1, tiled=True)
+    state_in_grad = halving_sum(b_term, "exp")
     return (scan_input_grad, state_in_grad)
 
 

time: 181 us -> 144 us (0.80)
  the two profiles are of different devices: /device:TPU:1 before, /device:TPU:127 now
where the time goes in v2:
time: 144 us
  waiting for transfers between devices  75 us (52%)
  starting transfers between devices  38 us (26%)
  Pallas kernels  20.2 us (14%)
  local copies, waits for them, and re-layouts  5.44 us (4%)
  other arithmetic  4.02 us (3%)
    ppermute x7, waiting for transfers between devices, carry_in(): lax.ppermute(packed, 'ctx', [(q, q - reach) for q in range(reach, size)])  64 us
    ppermute x3, starting transfers between devices, halving_sum(): got = lax.ppermute(send, axis, [(e, e ^ bit) for e in range(size)])  23.4 us
    pallas_call x1, Pallas kernels, shard_sweep(): pl.pallas_call(sweep_kernel, out_shape=(jax.ShapeDtypeStruct((rows, chann...  13.2 us
    ppermute x7, starting transfers between devices, carry_in(): lax.ppermute(packed, 'ctx', [(q, q - reach) for q in range(reach, size)])  11.5 us
    pallas_call x1, Pallas kernels, shard_summary(): pl.pallas_call(summary_kernel, out_shape=(jax.ShapeDtypeStruct(decay_rate...  7.01 us
    ppermute x3, waiting for transfers between devices, halving_sum(): got = lax.ppermute(send, axis, [(e, e ^ bit) for e in range(size)])  6.44 us
    ppermute x1, waiting for transfers between devices, carry_in(): packed = lax.ppermute(packed, 'ctx', [(q, q - 1) for q in range(1, size)])  4.49 us
    ppermute x1, starting transfers between devices, carry_in(): packed = lax.ppermute(packed, 'ctx', [(q, q - 1) for q in range(1, size)])  2.97 us
  transfers between devices with their start and end apart: 11, of which 11 were waited for; matrix products, arithmetic and copies ran while one was open for 0% of the time, Pallas kernels for 0%

profile of v2, /device:TPU:127, one launch (start us, length us, event | category | flops | bytes accessed | tf_op | source)
XLA Modules:
  0.0 143.5 jit_solution(12685017239775752279)
XLA Ops:
  1.4 1.9 %broadcast_in_dim.7.outb_ref = f32[256,16,128]{2,1,0:T(8,128)} broadcast(f32[256,16]{1,0:T(8,128)S(1)} %copy.12), dimensions={0,1} | broadcast | bytes 2113536 | tf_op jit(solution)/shard_map/broadcast_in_dim | solution.py:144
  3.4 7.0 %shard_map.86 = (f32[16,1024]{1,0:T(8,128)}, f32[1,1024]{1,0:T(1,128)}) custom-call(bf16[256,1024]{1,0:T(8,128)(2,1)} %g_ref.3, bf16[256,1024]{1,0:T(8,128)(2,1)} %s_ref.3, f32[256,16,128]{2,1,0:T(8,128)} %broadcast_in_dim.7.outb_ref, f32[16,1024]{1,0:T(8,128)} %a_ref.3), custom_call_target="tpu_custom_call" | custom-call | flops 25165824 | bytes 3145728 | tf_op jit(solution)/shard_map/pallas_call | solution.py:72
  11.3 3.0 %collective-permute-start = (f32[17,1024]{1,0:T(8,128)S(1)}, f32[17,1024]{1,0:T(8,128)S(1)}, u32[]{:S(2)}, u32[]{:S(2)}) collective-permute-start(f32[17,1024]{1,0:T(8,128)S(1)} %pad_maximum_fusion), channel_id=1, source_target_pairs={{8,0},{16,8},{24,16},{32,24},{40,32},{48,40},{56,48},{64,56},{72,6... | collective-permute-start | bytes 208904 | tf_op jit(solution)/shard_map/ppermute | solution.py:113
  14.2 4.5 %collective-permute-done = f32[17,1024]{1,0:T(8,128)S(1)} collective-permute-done((f32[17,1024]{1,0:T(8,128)S(1)}, f32[17,1024]{1,0:T(8,128)S(1)}, u32[]{:S(2)}, u32[]{:S(2)}) %collective-permute-start) | collective-permute-done | bytes 69664 | tf_op jit(solution)/shard_map/ppermute | solution.py:113
  18.7 1.9 %collective-permute-start.1 = (f32[17,1024]{1,0:T(8,128)S(1)}, f32[17,1024]{1,0:T(8,128)S(1)}, u32[]{:S(2)}, u32[]{:S(2)}) collective-permute-start(f32[17,1024]{1,0:T(8,128)S(1)} %collective-permute-done), channel_id=1, source_target_pairs={{8,0},{16,8},{24,16},{32,24},{40,32},{48,40},{56,48},{64,56},{72,6... | collective-permute-start | bytes 208904 | tf_op jit(solution)/shard_map/ppermute | solution.py:116
  20.6 5.5 %collective-permute-done.1 = f32[17,1024]{1,0:T(8,128)S(1)} collective-permute-done((f32[17,1024]{1,0:T(8,128)S(1)}, f32[17,1024]{1,0:T(8,128)S(1)}, u32[]{:S(2)}, u32[]{:S(2)}) %collective-permute-start.1) | collective-permute-done | bytes 69664 | tf_op jit(solution)/shard_map/ppermute | solution.py:116
  26.2 1.9 %collective-permute-start.2 = (f32[17,1024]{1,0:T(8,128)S(1)}, f32[17,1024]{1,0:T(8,128)S(1)}, u32[]{:S(2)}, u32[]{:S(2)}) collective-permute-start(f32[17,1024]{1,0:T(8,128)S(1)} %pad_maximum_fusion.1), channel_id=1, source_target_pairs={{16,0},{24,8},{32,16},{40,24},{48,32},{56,40},{64,48},{72,56},{80,... | collective-permute-start | bytes 208904 | tf_op jit(solution)/shard_map/ppermute | solution.py:116
  28.2 7.4 %collective-permute-done.2 = f32[17,1024]{1,0:T(8,128)S(1)} collective-permute-done((f32[17,1024]{1,0:T(8,128)S(1)}, f32[17,1024]{1,0:T(8,128)S(1)}, u32[]{:S(2)}, u32[]{:S(2)}) %collective-permute-start.2) | collective-permute-done | bytes 69664 | tf_op jit(solution)/shard_map/ppermute | solution.py:116
  35.6 1.9 %collective-permute-start.3 = (f32[17,1024]{1,0:T(8,128)S(1)}, f32[17,1024]{1,0:T(8,128)S(1)}, u32[]{:S(2)}, u32[]{:S(2)}) collective-permute-start(f32[17,1024]{1,0:T(8,128)S(1)} %pad_maximum_fusion.2), channel_id=1, source_target_pairs={{32,0},{40,8},{48,16},{56,24},{64,32},{72,40},{80,48},{88,56},{96,... | collective-permute-start | bytes 208904 | tf_op jit(solution)/shard_map/ppermute | solution.py:116
  37.5 9.3 %collective-permute-done.3 = f32[17,1024]{1,0:T(8,128)S(1)} collective-permute-done((f32[17,1024]{1,0:T(8,128)S(1)}, f32[17,1024]{1,0:T(8,128)S(1)}, u32[]{:S(2)}, u32[]{:S(2)}) %collective-permute-start.3) | collective-permute-done | bytes 69664 | tf_op jit(solution)/shard_map/ppermute | solution.py:116
  46.9 1.9 %collective-permute-start.4 = (f32[17,1024]{1,0:T(8,128)S(1)}, f32[17,1024]{1,0:T(8,128)S(1)}, u32[]{:S(2)}, u32[]{:S(2)}) collective-permute-start(f32[17,1024]{1,0:T(8,128)S(1)} %pad_maximum_fusion.3), channel_id=1, source_target_pairs={{64,0},{72,8},{80,16},{88,24},{96,32},{104,40},{112,48},{120,56},{... | collective-permute-start | bytes 208904 | tf_op jit(solution)/shard_map/ppermute | solution.py:116
  48.8 4.1 %collective-permute-done.4 = f32[17,1024]{1,0:T(8,128)S(1)} collective-permute-done((f32[17,1024]{1,0:T(8,128)S(1)}, f32[17,1024]{1,0:T(8,128)S(1)}, u32[]{:S(2)}, u32[]{:S(2)}) %collective-permute-start.4) | collective-permute-done | bytes 69664 | tf_op jit(solution)/shard_map/ppermute | solution.py:116
  52.9 1.3 collective-permute-start.5
  54.2 11.4 %collective-permute-done.5 = f32[17,1024]{1,0:T(8,128)S(1)} collective-permute-done((f32[17,1024]{1,0:T(8,128)S(1)}, f32[17,1024]{1,0:T(8,128)S(1)}, u32[]{:S(2)}, u32[]{:S(2)}) %collective-permute-start.5) | collective-permute-done | bytes 69664 | tf_op jit(solution)/shard_map/ppermute | solution.py:116
  67.0 11.4 %collective-permute-done.6 = f32[17,1024]{1,0:T(8,128)S(1)} collective-permute-done((f32[17,1024]{1,0:T(8,128)S(1)}, f32[17,1024]{1,0:T(8,128)S(1)}, u32[]{:S(2)}, u32[]{:S(2)}) %collective-permute-start.6) | collective-permute-done | bytes 69664 | tf_op jit(solution)/shard_map/ppermute | solution.py:116
  79.9 14.9 %collective-permute-done.7 = f32[17,1024]{1,0:T(8,128)S(1)} collective-permute-done((f32[17,1024]{1,0:T(8,128)S(1)}, f32[17,1024]{1,0:T(8,128)S(1)}, u32[]{:S(2)}, u32[]{:S(2)}) %collective-permute-start.7) | collective-permute-done | bytes 69664 | tf_op jit(solution)/shard_map/ppermute | solution.py:116
  95.5 1.9 %broadcast_in_dim.6.inb_ref = f32[256,16,128]{2,1,0:T(8,128)} broadcast(f32[256,16]{1,0:T(8,128)S(1)} %copy.11), dimensions={0,1} | broadcast | bytes 2113536 | tf_op jit(solution)/shard_map/broadcast_in_dim | solution.py:143
  97.4 13.2 %shard_map.87 = (bf16[256,1024]{1,0:T(8,128)(2,1)}, f32[256,16,128]{2,1,0:T(8,128)}) custom-call(bf16[256,1024]{1,0:T(8,128)(2,1)} %g_ref.3, bf16[256,1024]{1,0:T(8,128)(2,1)} %s_ref.3, bf16[256,1024]{1,0:T(8,128)(2,1)} %x_ref.1, f32[256,16,128]{2,1,0:T(8,128)} %broadcast_in_dim.6.inb_ref, f32[256,16,128]{2,1,0:T(8,128)} %broadcast_in_dim.7.outb_ref, ...), custom_call_target="tpu_custom_call" | custom-call | flops 50331648 | bytes 10485760 | tf_op jit(solution)/shard_map/pallas_call | solution.py:92
  110.6 2.2 %reduce_sum.9 = f32[256,16]{1,0:T(8,128)S(1)} reduce(f32[256,16,128]{2,1,0:T(8,128)} %get-tuple-element.9, f32[]{:T(128)} %constant.57.clone.1), dimensions={2}, to_apply=%region_0.0 | reduce | flops 520192 | bytes 2113540 | tf_op jit(solution)/shard_map/reduce_sum | solution.py:151
  112.8 3.0 %collective-permute-start.8 = (f32[16,128]{0,1:T(8,128)S(1)}, f32[16,128]{0,1:T(8,128)S(1)}, u32[]{:S(2)}, u32[]{:S(2)}) collective-permute-start(f32[16,128]{0,1:T(8,128)S(1)} %slice_select_fusion), channel_id=1, source_target_pairs={{0,4},{1,5},{2,6},{3,7},{4,0},{5,1},{6,2},{7,3},{8,12},{9,13},{10,... | collective-permute-start | bytes 24584 | tf_op jit(solution)/shard_map/ppermute | solution.py:134
  115.9 3.4 %collective-permute-done.8 = f32[16,128]{0,1:T(8,128)S(1)} collective-permute-done((f32[16,128]{0,1:T(8,128)S(1)}, f32[16,128]{0,1:T(8,128)S(1)}, u32[]{:S(2)}, u32[]{:S(2)}) %collective-permute-start.8) | collective-permute-done | bytes 8224 | tf_op jit(solution)/shard_map/ppermute | solution.py:134
  119.4 2.5 %collective-permute-start.9 = (f32[16,64]{0,1:T(8,128)S(1)}, f32[16,64]{0,1:T(8,128)S(1)}, u32[]{:S(2)}, u32[]{:S(2)}) collective-permute-start(f32[16,64]{0,1:T(8,128)S(1)} %slice_select_fusion.1), channel_id=1, source_target_pairs={{0,2},{1,3},{2,0},{3,1},{4,6},{5,7},{6,4},{7,5},{8,10},{9,11},{10,... | collective-permute-start | bytes 12296 | tf_op jit(solution)/shard_map/ppermute | solution.py:134
  121.9 2.2 %collective-permute-done.9 = f32[16,64]{0,1:T(8,128)S(1)} collective-permute-done((f32[16,64]{0,1:T(8,128)S(1)}, f32[16,64]{0,1:T(8,128)S(1)}, u32[]{:S(2)}, u32[]{:S(2)}) %collective-permute-start.9) | collective-permute-done | bytes 4128 | tf_op jit(solution)/shard_map/ppermute | solution.py:134
  124.0 17.9 %collective-permute-start.10 = (f32[16,32]{0,1:T(8,128)S(1)}, f32[16,32]{0,1:T(8,128)S(1)}, u32[]{:S(2)}, u32[]{:S(2)}) collective-permute-start(f32[16,32]{0,1:T(8,128)S(1)} %slice_select_fusion.2), channel_id=1, source_target_pairs={{0,1},{1,0},{2,3},{3,2},{4,5},{5,4},{6,7},{7,6},{8,9},{9,8},{10,11... | collective-permute-start | bytes 6152 | tf_op jit(solution)/shard_map/ppermute | solution.py:134
  (37 shorter events, 6.8 us)
Async XLA Ops:
  3.4 22.8 %copy-start = (f32[16,1024]{1,0:T(8,128)S(1)}, f32[16,1024]{1,0:T(8,128)}, u32[]{:S(2)}) copy-start(f32[16,1024]{1,0:T(8,128)} %a_ref.3) | copy-start | bytes 196612
  10.4 69.4 %copy-start.1 = (f32[256,16]{0,1:T(8,128)S(1)}, f32[256,16]{0,1:T(8,128)}, u32[]{:S(2)}) copy-start(f32[256,16]{0,1:T(8,128)} %param.10) | copy-start | bytes 49156
  11.3 7.5 %collective-permute-start = (f32[17,1024]{1,0:T(8,128)S(1)}, f32[17,1024]{1,0:T(8,128)S(1)}, u32[]{:S(2)}, u32[]{:S(2)}) collective-permute-start(f32[17,1024]{1,0:T(8,128)S(1)} %pad_maximum_fusion), channel_id=1, source_target_pairs={{8,0},{16,8},{24,16},{32,24},{40,32},{48,40},{56,48},{64,56},{72,6... | collective-permute-start | bytes 208904 | tf_op jit(solution)/shard_map/ppermute | solution.py:113
  18.7 7.5 %collective-permute-start.1 = (f32[17,1024]{1,0:T(8,128)S(1)}, f32[17,1024]{1,0:T(8,128)S(1)}, u32[]{:S(2)}, u32[]{:S(2)}) collective-permute-start(f32[17,1024]{1,0:T(8,128)S(1)} %collective-permute-done), channel_id=1, source_target_pairs={{8,0},{16,8},{24,16},{32,24},{40,32},{48,40},{56,48},{64,56},{72,6... | collective-permute-start | bytes 208904 | tf_op jit(solution)/shard_map/ppermute | solution.py:116
  26.2 9.3 %collective-permute-start.2 = (f32[17,1024]{1,0:T(8,128)S(1)}, f32[17,1024]{1,0:T(8,128)S(1)}, u32[]{:S(2)}, u32[]{:S(2)}) collective-permute-start(f32[17,1024]{1,0:T(8,128)S(1)} %pad_maximum_fusion.1), channel_id=1, source_target_pairs={{16,0},{24,8},{32,16},{40,24},{48,32},{56,40},{64,48},{72,56},{80,... | collective-permute-start | bytes 208904 | tf_op jit(solution)/shard_map/ppermute | solution.py:116
  35.6 11.2 %collective-permute-start.3 = (f32[17,1024]{1,0:T(8,128)S(1)}, f32[17,1024]{1,0:T(8,128)S(1)}, u32[]{:S(2)}, u32[]{:S(2)}) collective-permute-start(f32[17,1024]{1,0:T(8,128)S(1)} %pad_maximum_fusion.2), channel_id=1, source_target_pairs={{32,0},{40,8},{48,16},{56,24},{64,32},{72,40},{80,48},{88,56},{96,... | collective-permute-start | bytes 208904 | tf_op jit(solution)/shard_map/ppermute | solution.py:116
  46.9 6.0 %collective-permute-start.4 = (f32[17,1024]{1,0:T(8,128)S(1)}, f32[17,1024]{1,0:T(8,128)S(1)}, u32[]{:S(2)}, u32[]{:S(2)}) collective-permute-start(f32[17,1024]{1,0:T(8,128)S(1)} %pad_maximum_fusion.3), channel_id=1, source_target_pairs={{64,0},{72,8},{80,16},{88,24},{96,32},{104,40},{112,48},{120,56},{... | collective-permute-start | bytes 208904 | tf_op jit(solution)/shard_map/ppermute | solution.py:116
  52.9 12.7 %collective-permute-start.5 = (f32[17,1024]{1,0:T(8,128)S(1)}, f32[17,1024]{1,0:T(8,128)S(1)}, u32[]{:S(2)}, u32[]{:S(2)}) collective-permute-start(f32[17,1024]{1,0:T(8,128)S(1)} %pad_maximum_fusion.4), channel_id=1, source_target_pairs={{128,0},{136,8},{144,16},{152,24},{160,32},{168,40},{176,48},{184,... | collective-permute-start | bytes 208904 | tf_op jit(solution)/shard_map/ppermute | solution.py:116
  65.7 12.7 %collective-permute-start.6 = (f32[17,1024]{1,0:T(8,128)S(1)}, f32[17,1024]{1,0:T(8,128)S(1)}, u32[]{:S(2)}, u32[]{:S(2)}) collective-permute-start(f32[17,1024]{1,0:T(8,128)S(1)} %pad_maximum_fusion.5), channel_id=1, source_target_pairs={{256,0},{264,8},{272,16},{280,24},{288,32},{296,40},{304,48},{312,... | collective-permute-start | bytes 208904 | tf_op jit(solution)/shard_map/ppermute | solution.py:116
  78.5 16.4 %collective-permute-start.7 = (f32[17,1024]{1,0:T(8,128)S(1)}, f32[17,1024]{1,0:T(8,128)S(1)}, u32[]{:S(2)}, u32[]{:S(2)}) collective-permute-start(f32[17,1024]{1,0:T(8,128)S(1)} %pad_maximum_fusion.6), channel_id=1, source_target_pairs={{512,0},{520,8},{528,16},{536,24},{544,32},{552,40},{560,48},{568,... | collective-permute-start | bytes 208904 | tf_op jit(solution)/shard_map/ppermute | solution.py:116
  112.8 6.5 %collective-permute-start.8 = (f32[16,128]{0,1:T(8,128)S(1)}, f32[16,128]{0,1:T(8,128)S(1)}, u32[]{:S(2)}, u32[]{:S(2)}) collective-permute-start(f32[16,128]{0,1:T(8,128)S(1)} %slice_select_fusion), channel_id=1, source_target_pairs={{0,4},{1,5},{2,6},{3,7},{4,0},{5,1},{6,2},{7,3},{8,12},{9,13},{10,... | collective-permute-start | bytes 24584 | tf_op jit(solution)/shard_map/ppermute | solution.py:134
  119.4 4.7 %collective-permute-start.9 = (f32[16,64]{0,1:T(8,128)S(1)}, f32[16,64]{0,1:T(8,128)S(1)}, u32[]{:S(2)}, u32[]{:S(2)}) collective-permute-start(f32[16,64]{0,1:T(8,128)S(1)} %slice_select_fusion.1), channel_id=1, source_target_pairs={{0,2},{1,3},{2,0},{3,1},{4,6},{5,7},{6,4},{7,5},{8,10},{9,11},{10,... | collective-permute-start | bytes 12296 | tf_op jit(solution)/shard_map/ppermute | solution.py:134
  124.0 18.8 %collective-permute-start.10 = (f32[16,32]{0,1:T(8,128)S(1)}, f32[16,32]{0,1:T(8,128)S(1)}, u32[]{:S(2)}, u32[]{:S(2)}) collective-permute-start(f32[16,32]{0,1:T(8,128)S(1)} %slice_select_fusion.2), channel_id=1, source_target_pairs={{0,1},{1,0},{2,3},{3,2},{4,5},{5,4},{6,7},{7,6},{8,9},{9,8},{10,11... | collective-permute-start | bytes 6152 | tf_op jit(solution)/shard_map/ppermute | solution.py:134

commit v3 on v2

--- a/solution.py
+++ b/solution.py
@@ -106,19 +106,31 @@
     )(scan_grad, step_size, scan_input, in_b, out_b, decay_rate, skip_gain, incoming)
 
 
-def carry_in(summary, total, decay_rate):
+def carry_in(summary, total, decay_rate, radix=4):
     size = lax.axis_size("ctx")
     states = summary.shape[0]
     packed = jnp.concatenate([summary, total], axis=0)
-    packed = lax.ppermute(packed, "ctx", [(q, q - 1) for q in range(1, size)])
-    reach = 1
-    while reach < size:
-        got = lax.ppermute(packed, "ctx", [(q, q - reach) for q in range(reach, size)])
-        own_s, own_r = packed[:states], packed[states:]
-        new_s = own_s + jnp.exp(decay_rate * own_r) * got[:states]
-        packed = jnp.concatenate([new_s, own_r + got[states:]], axis=0)
-        reach *= 2
-    return packed[:states]
+    own = None
+    covered, stride, count = 0, 1, radix
+    while covered < size - 1:
+        pieces = [] if own is None else [own]
+        for j in range(1, count + 1):
+            shift = j * stride
+            if shift >= size:
+                break
+            source = packed if own is None else own
+            pieces.append(
+                lax.ppermute(source, "ctx", [(q, q - shift) for q in range(shift, size)])
+            )
+        acc_s, acc_r = pieces[-1][:states], pieces[-1][states:]
+        for piece in pieces[-2::-1]:
+            acc_s = piece[:states] + jnp.exp(decay_rate * piece[states:]) * acc_s
+            acc_r = piece[states:] + acc_r
+        own = jnp.concatenate([acc_s, acc_r], axis=0)
+        covered = covered + (len(pieces) - (0 if covered == 0 else 1)) * stride
+        stride = covered
+        count = min(radix - 1, -(-(size - 1) // covered) - 1)
+    return own[:states]
 
 
 def halving_sum(block, axis):

time: 144 us -> 150 us (1.042)
  the two profiles are of different devices: /device:TPU:127 before, /device:TPU:317 now
where the time goes in v3:
time: 150 us; the launch traced here: 149 us
  waiting for transfers between devices  65.9 us (44%)
  starting transfers between devices  51.7 us (34%)
  Pallas kernels  20.2 us (13%)
  local copies, waits for them, and re-layouts  7.08 us (5%)
  other arithmetic  3.13 us (2%)
    ppermute x11, waiting for transfers between devices, carry_in(): lax.ppermute(source, 'ctx', [(q, q - shift) for q in range(shift, size)])  58.9 us
    ppermute x11, starting transfers between devices, carry_in(): lax.ppermute(source, 'ctx', [(q, q - shift) for q in range(shift, size)])  31.2 us
    ppermute x3, starting transfers between devices, halving_sum(): got = lax.ppermute(send, axis, [(e, e ^ bit) for e in range(size)])  20.5 us
    pallas_call x1, Pallas kernels, shard_sweep(): pl.pallas_call(sweep_kernel, out_shape=(jax.ShapeDtypeStruct((rows, chann...  13.2 us
    pallas_call x1, Pallas kernels, shard_summary(): pl.pallas_call(summary_kernel, out_shape=(jax.ShapeDtypeStruct(decay_rate...  7.01 us
    ppermute x3, waiting for transfers between devices, halving_sum(): got = lax.ppermute(send, axis, [(e, e ^ bit) for e in range(size)])  6.97 us
  transfers between devices with their start and end apart: 14, of which 11 were waited for; matrix products, arithmetic and copies ran while one was open for 0% of the time, Pallas kernels for 0%

profile of v3, /device:TPU:317, one launch (start us, length us, event | category | flops | bytes accessed | tf_op | source)
XLA Modules:
  0.0 148.9 jit_solution(2279338523218447136)
XLA Ops:
  1.4 1.9 %broadcast_in_dim.7.outb_ref = f32[256,16,128]{2,1,0:T(8,128)} broadcast(f32[256,16]{1,0:T(8,128)S(1)} %copy.12), dimensions={0,1} | broadcast | bytes 2113536 | tf_op jit(solution)/shard_map/broadcast_in_dim | solution.py:156
  3.4 7.0 %shard_map.86 = (f32[16,1024]{1,0:T(8,128)}, f32[1,1024]{1,0:T(1,128)}) custom-call(bf16[256,1024]{1,0:T(8,128)(2,1)} %g_ref.3, bf16[256,1024]{1,0:T(8,128)(2,1)} %s_ref.3, f32[256,16,128]{2,1,0:T(8,128)} %broadcast_in_dim.7.outb_ref, f32[16,1024]{1,0:T(8,128)} %a_ref.3), custom_call_target="tpu_custom_call" | custom-call | flops 25165824 | bytes 3145728 | tf_op jit(solution)/shard_map/pallas_call | solution.py:72
  12.0 3.0 %collective-permute-start = (f32[17,1024]{1,0:T(8,128)S(1)}, f32[17,1024]{1,0:T(8,128)S(1)}, u32[]{:S(2)}, u32[]{:S(2)}) collective-permute-start(f32[17,1024]{1,0:T(8,128)S(1)} %dynamic-update-slice.1), channel_id=1, source_target_pairs={{8,0},{16,8},{24,16},{32,24},{40,32},{48,40},{56,48},{64,56},{72,6... | collective-permute-start | bytes 208904 | tf_op jit(solution)/shard_map/ppermute | solution.py:123
  15.0 3.8 %collective-permute-start.1 = (f32[17,1024]{1,0:T(8,128)S(1)}, f32[17,1024]{1,0:T(8,128)S(1)}, u32[]{:S(2)}, u32[]{:S(2)}) collective-permute-start(f32[17,1024]{1,0:T(8,128)S(1)} %dynamic-update-slice.1), channel_id=1, source_target_pairs={{16,0},{24,8},{32,16},{40,24},{48,32},{56,40},{64,48},{72,56},{80,... | collective-permute-start | bytes 208904 | tf_op jit(solution)/shard_map/ppermute | solution.py:123
  18.8 1.9 %collective-permute-start.2 = (f32[17,1024]{1,0:T(8,128)S(1)}, f32[17,1024]{1,0:T(8,128)S(1)}, u32[]{:S(2)}, u32[]{:S(2)}) collective-permute-start(f32[17,1024]{1,0:T(8,128)S(1)} %dynamic-update-slice.1), channel_id=1, source_target_pairs={{24,0},{32,8},{40,16},{48,24},{56,32},{64,40},{72,48},{80,56},{88,... | collective-permute-start | bytes 208904 | tf_op jit(solution)/shard_map/ppermute | solution.py:123
  20.7 5.6 %collective-permute-start.3 = (f32[17,1024]{1,0:T(8,128)S(1)}, f32[17,1024]{1,0:T(8,128)S(1)}, u32[]{:S(2)}, u32[]{:S(2)}) collective-permute-start(f32[17,1024]{1,0:T(8,128)S(1)} %dynamic-update-slice.1), channel_id=1, source_target_pairs={{32,0},{40,8},{48,16},{56,24},{64,32},{72,40},{80,48},{88,56},{96,... | collective-permute-start | bytes 208904 | tf_op jit(solution)/shard_map/ppermute | solution.py:123
  26.3 5.2 %collective-permute-done.2 = f32[17,1024]{1,0:T(8,128)S(1)} collective-permute-done((f32[17,1024]{1,0:T(8,128)S(1)}, f32[17,1024]{1,0:T(8,128)S(1)}, u32[]{:S(2)}, u32[]{:S(2)}) %collective-permute-start.2) | collective-permute-done | bytes 69664 | tf_op jit(solution)/shard_map/ppermute | solution.py:123
  31.4 3.2 %collective-permute-done.3 = f32[17,1024]{1,0:T(8,128)S(1)} collective-permute-done((f32[17,1024]{1,0:T(8,128)S(1)}, f32[17,1024]{1,0:T(8,128)S(1)}, u32[]{:S(2)}, u32[]{:S(2)}) %collective-permute-start.3) | collective-permute-done | bytes 69664 | tf_op jit(solution)/shard_map/ppermute | solution.py:123
  34.8 5.8 %collective-permute-start.4 = (f32[17,1024]{1,0:T(8,128)S(1)}, f32[17,1024]{1,0:T(8,128)S(1)}, u32[]{:S(2)}, u32[]{:S(2)}) collective-permute-start(f32[17,1024]{1,0:T(8,128)S(1)} %pad_maximum_fusion), channel_id=1, source_target_pairs={{32,0},{40,8},{48,16},{56,24},{64,32},{72,40},{80,48},{88,56},{96,... | collective-permute-start | bytes 208904 | tf_op jit(solution)/shard_map/ppermute | solution.py:123
  40.6 2.8 %collective-permute-start.5 = (f32[17,1024]{1,0:T(8,128)S(1)}, f32[17,1024]{1,0:T(8,128)S(1)}, u32[]{:S(2)}, u32[]{:S(2)}) collective-permute-start(f32[17,1024]{1,0:T(8,128)S(1)} %pad_maximum_fusion), channel_id=1, source_target_pairs={{64,0},{72,8},{80,16},{88,24},{96,32},{104,40},{112,48},{120,56},{... | collective-permute-start | bytes 208904 | tf_op jit(solution)/shard_map/ppermute | solution.py:123
  43.4 1.9 %collective-permute-start.6 = (f32[17,1024]{1,0:T(8,128)S(1)}, f32[17,1024]{1,0:T(8,128)S(1)}, u32[]{:S(2)}, u32[]{:S(2)}) collective-permute-start(f32[17,1024]{1,0:T(8,128)S(1)} %pad_maximum_fusion), channel_id=1, source_target_pairs={{96,0},{104,8},{112,16},{120,24},{128,32},{136,40},{144,48},{152,5... | collective-permute-start | bytes 208904 | tf_op jit(solution)/shard_map/ppermute | solution.py:123
  46.9 8.0 %collective-permute-done.6 = f32[17,1024]{1,0:T(8,128)S(1)} collective-permute-done((f32[17,1024]{1,0:T(8,128)S(1)}, f32[17,1024]{1,0:T(8,128)S(1)}, u32[]{:S(2)}, u32[]{:S(2)}) %collective-permute-start.6) | collective-permute-done | bytes 69664 | tf_op jit(solution)/shard_map/ppermute | solution.py:123
  55.0 1.9 %collective-permute-start.7 = (f32[17,1024]{1,0:T(8,128)S(1)}, f32[17,1024]{1,0:T(8,128)S(1)}, u32[]{:S(2)}, u32[]{:S(2)}) collective-permute-start(f32[17,1024]{1,0:T(8,128)S(1)} %pad_maximum_fusion.1), channel_id=1, source_target_pairs={{128,0},{136,8},{144,16},{152,24},{160,32},{168,40},{176,48},{184,... | collective-permute-start | bytes 208904 | tf_op jit(solution)/shard_map/ppermute | solution.py:123
  60.1 3.7 %collective-permute-done.7 = f32[17,1024]{1,0:T(8,128)S(1)} collective-permute-done((f32[17,1024]{1,0:T(8,128)S(1)}, f32[17,1024]{1,0:T(8,128)S(1)}, u32[]{:S(2)}, u32[]{:S(2)}) %collective-permute-start.7) | collective-permute-done | bytes 69664 | tf_op jit(solution)/shard_map/ppermute | solution.py:123
  63.8 16.5 %collective-permute-done.8 = f32[17,1024]{1,0:T(8,128)S(1)} collective-permute-done((f32[17,1024]{1,0:T(8,128)S(1)}, f32[17,1024]{1,0:T(8,128)S(1)}, u32[]{:S(2)}, u32[]{:S(2)}) %collective-permute-start.8) | collective-permute-done | bytes 69664 | tf_op jit(solution)/shard_map/ppermute | solution.py:123
  80.4 8.1 %collective-permute-done.9 = f32[17,1024]{1,0:T(8,128)S(1)} collective-permute-done((f32[17,1024]{1,0:T(8,128)S(1)}, f32[17,1024]{1,0:T(8,128)S(1)}, u32[]{:S(2)}, u32[]{:S(2)}) %collective-permute-start.9) | collective-permute-done | bytes 69664 | tf_op jit(solution)/shard_map/ppermute | solution.py:123
  90.0 12.6 %collective-permute-done.10 = f32[17,1024]{1,0:T(8,128)S(1)} collective-permute-done((f32[17,1024]{1,0:T(8,128)S(1)}, f32[17,1024]{1,0:T(8,128)S(1)}, u32[]{:S(2)}, u32[]{:S(2)}) %collective-permute-start.10) | collective-permute-done | bytes 69664 | tf_op jit(solution)/shard_map/ppermute | solution.py:123
  103.3 1.9 %broadcast_in_dim.6.inb_ref = f32[256,16,128]{2,1,0:T(8,128)} broadcast(f32[256,16]{1,0:T(8,128)S(1)} %copy.11), dimensions={0,1} | broadcast | bytes 2113536 | tf_op jit(solution)/shard_map/broadcast_in_dim | solution.py:155
  105.3 13.2 %shard_map.87 = (bf16[256,1024]{1,0:T(8,128)(2,1)}, f32[256,16,128]{2,1,0:T(8,128)}) custom-call(bf16[256,1024]{1,0:T(8,128)(2,1)} %g_ref.3, bf16[256,1024]{1,0:T(8,128)(2,1)} %s_ref.3, bf16[256,1024]{1,0:T(8,128)(2,1)} %x_ref.1, f32[256,16,128]{2,1,0:T(8,128)} %broadcast_in_dim.6.inb_ref, f32[256,16,128]{2,1,0:T(8,128)} %broadcast_in_dim.7.outb_ref, ...), custom_call_target="tpu_custom_call" | custom-call | flops 50331648 | bytes 10485760 | tf_op jit(solution)/shard_map/pallas_call | solution.py:92
  118.4 2.2 %reduce_sum.9 = f32[256,16]{1,0:T(8,128)S(1)} reduce(f32[256,16,128]{2,1,0:T(8,128)} %get-tuple-element.9, f32[]{:T(128)} %constant.57.clone.1), dimensions={2}, to_apply=%region_0.0 | reduce | flops 520192 | bytes 2113540 | tf_op jit(solution)/shard_map/reduce_sum | solution.py:163
  120.7 2.1 %collective-permute-start.11 = (f32[16,128]{0,1:T(8,128)S(1)}, f32[16,128]{0,1:T(8,128)S(1)}, u32[]{:S(2)}, u32[]{:S(2)}) collective-permute-start(f32[16,128]{0,1:T(8,128)S(1)} %slice_select_fusion), channel_id=1, source_target_pairs={{0,4},{1,5},{2,6},{3,7},{4,0},{5,1},{6,2},{7,3},{8,12},{9,13},{10,... | collective-permute-start | bytes 24584 | tf_op jit(solution)/shard_map/ppermute | solution.py:146
  122.9 4.3 %collective-permute-done.11 = f32[16,128]{0,1:T(8,128)S(1)} collective-permute-done((f32[16,128]{0,1:T(8,128)S(1)}, f32[16,128]{0,1:T(8,128)S(1)}, u32[]{:S(2)}, u32[]{:S(2)}) %collective-permute-start.11) | collective-permute-done | bytes 8224 | tf_op jit(solution)/shard_map/ppermute | solution.py:146
  127.2 2.8 %collective-permute-start.12 = (f32[16,64]{0,1:T(8,128)S(1)}, f32[16,64]{0,1:T(8,128)S(1)}, u32[]{:S(2)}, u32[]{:S(2)}) collective-permute-start(f32[16,64]{0,1:T(8,128)S(1)} %slice_select_fusion.1), channel_id=1, source_target_pairs={{0,2},{1,3},{2,0},{3,1},{4,6},{5,7},{6,4},{7,5},{8,10},{9,11},{10,... | collective-permute-start | bytes 12296 | tf_op jit(solution)/shard_map/ppermute | solution.py:146
  131.9 15.5 %collective-permute-start.13 = (f32[16,32]{0,1:T(8,128)S(1)}, f32[16,32]{0,1:T(8,128)S(1)}, u32[]{:S(2)}, u32[]{:S(2)}) collective-permute-start(f32[16,32]{0,1:T(8,128)S(1)} %slice_select_fusion.2), channel_id=1, source_target_pairs={{0,1},{1,0},{2,3},{3,2},{4,5},{5,4},{6,7},{7,6},{8,9},{9,8},{10,11... | collective-permute-start | bytes 6152 | tf_op jit(solution)/shard_map/ppermute | solution.py:146
  (35 shorter events, 12.8 us)
Async XLA Ops:
  3.4 31.3 %copy-start = (f32[16,1024]{1,0:T(8,128)S(1)}, f32[16,1024]{1,0:T(8,128)}, u32[]{:S(2)}) copy-start(f32[16,1024]{1,0:T(8,128)} %a_ref.3) | copy-start | bytes 196612
  3.4 86.6 %copy-start.1 = (f32[256,16]{0,1:T(8,128)S(1)}, f32[256,16]{0,1:T(8,128)}, u32[]{:S(2)}) copy-start(f32[256,16]{0,1:T(8,128)} %param.10) | copy-start | bytes 49156
  12.0 14.3 %collective-permute-start = (f32[17,1024]{1,0:T(8,128)S(1)}, f32[17,1024]{1,0:T(8,128)S(1)}, u32[]{:S(2)}, u32[]{:S(2)}) collective-permute-start(f32[17,1024]{1,0:T(8,128)S(1)} %dynamic-update-slice.1), channel_id=1, source_target_pairs={{8,0},{16,8},{24,16},{32,24},{40,32},{48,40},{56,48},{64,56},{72,6... | collective-permute-start | bytes 208904 | tf_op jit(solution)/shard_map/ppermute | solution.py:123
  15.0 11.3 %collective-permute-start.1 = (f32[17,1024]{1,0:T(8,128)S(1)}, f32[17,1024]{1,0:T(8,128)S(1)}, u32[]{:S(2)}, u32[]{:S(2)}) collective-permute-start(f32[17,1024]{1,0:T(8,128)S(1)} %dynamic-update-slice.1), channel_id=1, source_target_pairs={{16,0},{24,8},{32,16},{40,24},{48,32},{56,40},{64,48},{72,56},{80,... | collective-permute-start | bytes 208904 | tf_op jit(solution)/shard_map/ppermute | solution.py:123
  18.8 12.7 %collective-permute-start.2 = (f32[17,1024]{1,0:T(8,128)S(1)}, f32[17,1024]{1,0:T(8,128)S(1)}, u32[]{:S(2)}, u32[]{:S(2)}) collective-permute-start(f32[17,1024]{1,0:T(8,128)S(1)} %dynamic-update-slice.1), channel_id=1, source_target_pairs={{24,0},{32,8},{40,16},{48,24},{56,32},{64,40},{72,48},{80,56},{88,... | collective-permute-start | bytes 208904 | tf_op jit(solution)/shard_map/ppermute | solution.py:123
  20.7 14.0 %collective-permute-start.3 = (f32[17,1024]{1,0:T(8,128)S(1)}, f32[17,1024]{1,0:T(8,128)S(1)}, u32[]{:S(2)}, u32[]{:S(2)}) collective-permute-start(f32[17,1024]{1,0:T(8,128)S(1)} %dynamic-update-slice.1), channel_id=1, source_target_pairs={{32,0},{40,8},{48,16},{56,24},{64,32},{72,40},{80,48},{88,56},{96,... | collective-permute-start | bytes 208904 | tf_op jit(solution)/shard_map/ppermute | solution.py:123
  34.8 10.6 %collective-permute-start.4 = (f32[17,1024]{1,0:T(8,128)S(1)}, f32[17,1024]{1,0:T(8,128)S(1)}, u32[]{:S(2)}, u32[]{:S(2)}) collective-permute-start(f32[17,1024]{1,0:T(8,128)S(1)} %pad_maximum_fusion), channel_id=1, source_target_pairs={{32,0},{40,8},{48,16},{56,24},{64,32},{72,40},{80,48},{88,56},{96,... | collective-permute-start | bytes 208904 | tf_op jit(solution)/shard_map/ppermute | solution.py:123
  40.6 6.3 %collective-permute-start.5 = (f32[17,1024]{1,0:T(8,128)S(1)}, f32[17,1024]{1,0:T(8,128)S(1)}, u32[]{:S(2)}, u32[]{:S(2)}) collective-permute-start(f32[17,1024]{1,0:T(8,128)S(1)} %pad_maximum_fusion), channel_id=1, source_target_pairs={{64,0},{72,8},{80,16},{88,24},{96,32},{104,40},{112,48},{120,56},{... | collective-permute-start | bytes 208904 | tf_op jit(solution)/shard_map/ppermute | solution.py:123
  43.4 11.5 %collective-permute-start.6 = (f32[17,1024]{1,0:T(8,128)S(1)}, f32[17,1024]{1,0:T(8,128)S(1)}, u32[]{:S(2)}, u32[]{:S(2)}) collective-permute-start(f32[17,1024]{1,0:T(8,128)S(1)} %pad_maximum_fusion), channel_id=1, source_target_pairs={{96,0},{104,8},{112,16},{120,24},{128,32},{136,40},{144,48},{152,5... | collective-permute-start | bytes 208904 | tf_op jit(solution)/shard_map/ppermute | solution.py:123
  55.0 8.9 %collective-permute-start.7 = (f32[17,1024]{1,0:T(8,128)S(1)}, f32[17,1024]{1,0:T(8,128)S(1)}, u32[]{:S(2)}, u32[]{:S(2)}) collective-permute-start(f32[17,1024]{1,0:T(8,128)S(1)} %pad_maximum_fusion.1), channel_id=1, source_target_pairs={{128,0},{136,8},{144,16},{152,24},{160,32},{168,40},{176,48},{184,... | collective-permute-start | bytes 208904 | tf_op jit(solution)/shard_map/ppermute | solution.py:123
  56.9 23.5 %collective-permute-start.8 = (f32[17,1024]{1,0:T(8,128)S(1)}, f32[17,1024]{1,0:T(8,128)S(1)}, u32[]{:S(2)}, u32[]{:S(2)}) collective-permute-start(f32[17,1024]{1,0:T(8,128)S(1)} %pad_maximum_fusion.1), channel_id=1, source_target_pairs={{256,0},{264,8},{272,16},{280,24},{288,32},{296,40},{304,48},{312,... | collective-permute-start | bytes 208904 | tf_op jit(solution)/shard_map/ppermute | solution.py:123
  58.8 29.7 %collective-permute-start.9 = (f32[17,1024]{1,0:T(8,128)S(1)}, f32[17,1024]{1,0:T(8,128)S(1)}, u32[]{:S(2)}, u32[]{:S(2)}) collective-permute-start(f32[17,1024]{1,0:T(8,128)S(1)} %pad_maximum_fusion.1), channel_id=1, source_target_pairs={{384,0},{392,8},{400,16},{408,24},{416,32},{424,40},{432,48},{440,... | collective-permute-start | bytes 208904 | tf_op jit(solution)/shard_map/ppermute | solution.py:123
  88.6 14.1 %collective-permute-start.10 = (f32[17,1024]{1,0:T(8,128)S(1)}, f32[17,1024]{1,0:T(8,128)S(1)}, u32[]{:S(2)}, u32[]{:S(2)}) collective-permute-start(f32[17,1024]{1,0:T(8,128)S(1)} %pad_maximum_fusion.2), channel_id=1, source_target_pairs={{512,0},{520,8},{528,16},{536,24},{544,32},{552,40},{560,48},{568,... | collective-permute-start | bytes 208904 | tf_op jit(solution)/shard_map/ppermute | solution.py:123
  120.7 6.5 %collective-permute-start.11 = (f32[16,128]{0,1:T(8,128)S(1)}, f32[16,128]{0,1:T(8,128)S(1)}, u32[]{:S(2)}, u32[]{:S(2)}) collective-permute-start(f32[16,128]{0,1:T(8,128)S(1)} %slice_select_fusion), channel_id=1, source_target_pairs={{0,4},{1,5},{2,6},{3,7},{4,0},{5,1},{6,2},{7,3},{8,12},{9,13},{10,... | collective-permute-start | bytes 24584 | tf_op jit(solution)/shard_map/ppermute | solution.py:146
  127.2 4.7 %collective-permute-start.12 = (f32[16,64]{0,1:T(8,128)S(1)}, f32[16,64]{0,1:T(8,128)S(1)}, u32[]{:S(2)}, u32[]{:S(2)}) collective-permute-start(f32[16,64]{0,1:T(8,128)S(1)} %slice_select_fusion.1), channel_id=1, source_target_pairs={{0,2},{1,3},{2,0},{3,1},{4,6},{5,7},{6,4},{7,5},{8,10},{9,11},{10,... | collective-permute-start | bytes 12296 | tf_op jit(solution)/shard_map/ppermute | solution.py:146
  131.9 16.3 %collective-permute-start.13 = (f32[16,32]{0,1:T(8,128)S(1)}, f32[16,32]{0,1:T(8,128)S(1)}, u32[]{:S(2)}, u32[]{:S(2)}) collective-permute-start(f32[16,32]{0,1:T(8,128)S(1)} %slice_select_fusion.2), channel_id=1, source_target_pairs={{0,1},{1,0},{2,3},{3,2},{4,5},{5,4},{6,7},{7,6},{8,9},{9,8},{10,11... | collective-permute-start | bytes 6152 | tf_op jit(solution)/shard_map/ppermute | solution.py:146

commit v4 on v2

--- a/solution.py
+++ b/solution.py
@@ -106,19 +106,35 @@
     )(scan_grad, step_size, scan_input, in_b, out_b, decay_rate, skip_gain, incoming)
 
 
+def gathered_suffix(pieces, me, decay_rate):
+    count, packed_rows, _ = pieces.shape
+    states = packed_rows - 1
+    summaries, totals = pieces[:, :states], pieces[:, states:]
+    index = lax.broadcasted_iota(jnp.int32, (count, count, 1, 1), 0)
+    inner = lax.broadcasted_iota(jnp.int32, (count, count, 1, 1), 1)
+    between = jnp.where((inner > me) & (inner < index), totals[None], 0.0)
+    before = jnp.where(inner < index, totals[None], 0.0)
+    reach_after = jnp.sum(between, axis=1)
+    reach_all = jnp.sum(before, axis=1)
+    later = (lax.broadcasted_iota(jnp.int32, (count, 1, 1), 0) > me)
+    after_s = jnp.sum(
+        jnp.where(later, jnp.exp(decay_rate[None] * reach_after) * summaries, 0.0), axis=0
+    )
+    after_r = jnp.sum(jnp.where(later, totals, 0.0), axis=0)
+    all_s = jnp.sum(jnp.exp(decay_rate[None] * reach_all) * summaries, axis=0)
+    all_r = jnp.sum(totals, axis=0)
+    return (after_s, after_r), (all_s, all_r)
+
+
 def carry_in(summary, total, decay_rate):
-    size = lax.axis_size("ctx")
-    states = summary.shape[0]
     packed = jnp.concatenate([summary, total], axis=0)
-    packed = lax.ppermute(packed, "ctx", [(q, q - 1) for q in range(1, size)])
-    reach = 1
-    while reach < size:
-        got = lax.ppermute(packed, "ctx", [(q, q - reach) for q in range(reach, size)])
-        own_s, own_r = packed[:states], packed[states:]
-        new_s = own_s + jnp.exp(decay_rate * own_r) * got[:states]
-        packed = jnp.concatenate([new_s, own_r + got[states:]], axis=0)
-        reach *= 2
-    return packed[:states]
+    near = lax.all_gather(packed, "ctx_in")
+    (near_s, near_r), (group_s, group_r) = gathered_suffix(
+        near, lax.axis_index("ctx_in"), decay_rate
+    )
+    far = lax.all_gather(jnp.concatenate([group_s, group_r], axis=0), "ctx_out")
+    (far_s, _), _ = gathered_suffix(far, lax.axis_index("ctx_out"), decay_rate)
+    return near_s + jnp.exp(decay_rate * near_r) * far_s
 
 
 def halving_sum(block, axis):
@@ -154,14 +170,21 @@
 
 
 def solution(mesh):
+    ctx_size = mesh.shape["ctx"]
+    inner = 8 if ctx_size % 8 == 0 else 1
+    split = jax.sharding.Mesh(
+        mesh.devices.reshape(ctx_size // inner, inner, mesh.shape["exp"]),
+        ("ctx_out", "ctx_in", "exp"),
+    )
+    ctx = ("ctx_out", "ctx_in")
     in_specs = (
-        P("ctx", "exp"),
-        P("ctx", "exp"),
-        P("ctx", "exp"),
-        P("ctx", None),
-        P("ctx", None),
+        P(ctx, "exp"),
+        P(ctx, "exp"),
+        P(ctx, "exp"),
+        P(ctx, None),
+        P(ctx, None),
         P(None, "exp"),
         P("exp"),
     )
-    out_specs = (P("ctx", "exp"), P(None, ("ctx", "exp")))
-    return jax.shard_map(shards, mesh=mesh, in_specs=in_specs, out_specs=out_specs, check_vma=False)
+    out_specs = (P(ctx, "exp"), P(None, ctx + ("exp",)))
+    return jax.shard_map(shards, mesh=split, in_specs=in_specs, out_specs=out_specs, check_vma=False)

time: 144 us -> 176 us (1.22)
  the two profiles are of different devices: /device:TPU:127 before, /device:TPU:1 now
where the time goes in v4:
time: 176 us; the launch traced here: 175 us
  waiting for transfers between devices  83.4 us (47%)
  starting transfers between devices  22.4 us (13%)
  blocking collectives  21.8 us (12%)
  Pallas kernels  20.2 us (11%)
  between operations  14.2 us (8%)
  other arithmetic  6.7 us (4%)
  local copies, waits for them, and re-layouts  6.55 us (4%)
    all_gather x1, waiting for transfers between devices, carry_in(): far = lax.all_gather(jnp.concatenate([group_s, group_r], axis=0), 'ctx_out')  79.1 us
    ppermute x3, starting transfers between devices, halving_sum(): got = lax.ppermute(send, axis, [(e, e ^ bit) for e in range(size)])  22.4 us
    all_gather x1, blocking collectives, carry_in(): near = lax.all_gather(packed, 'ctx_in')  21.8 us
    pallas_call x1, Pallas kernels, shard_sweep(): pl.pallas_call(sweep_kernel, out_shape=(jax.ShapeDtypeStruct((rows, chann...  13.2 us
    pallas_call x1, Pallas kernels, shard_summary(): pl.pallas_call(summary_kernel, out_shape=(jax.ShapeDtypeStruct(decay_rate...  7.01 us
    ppermute x3, waiting for transfers between devices, halving_sum(): got = lax.ppermute(send, axis, [(e, e ^ bit) for e in range(size)])  4.23 us
  transfers between devices with their start and end apart: 4, of which 4 were waited for; matrix products, arithmetic and copies ran while one was open for 0% of the time, Pallas kernels for 0%

profile of v4, /device:TPU:1, one launch (start us, length us, event | category | flops | bytes accessed | tf_op | source)
XLA Modules:
  0.0 175.2 jit_solution(2747008133625815285)
XLA Ops:
  7.2 0.8 copy.15
  8.0 2.0 %broadcast_in_dim.111.outb_ref = f32[256,16,128]{2,1,0:T(8,128)} broadcast(f32[256,16]{1,0:T(8,128)S(1)} %copy.15), dimensions={0,1} | broadcast | bytes 2113536 | tf_op jit(solution)/shard_map/broadcast_in_dim | solution.py:160
  10.0 7.0 %shard_map.86 = (f32[16,1024]{1,0:T(8,128)}, f32[1,1024]{1,0:T(1,128)}) custom-call(bf16[256,1024]{1,0:T(8,128)(2,1)} %g_ref.3, bf16[256,1024]{1,0:T(8,128)(2,1)} %s_ref.3, f32[256,16,128]{2,1,0:T(8,128)} %broadcast_in_dim.111.outb_ref, f32[16,1024]{1,0:T(8,128)} %a_ref.3), custom_call_target="tpu_custom_call" | custom-call | flops 25165824 | bytes 3145728 | tf_op jit(solution)/shard_map/pallas_call | solution.py:72
  17.0 0.9 maximum_bitcast_fusion
  17.9 21.8 %all-gather.2 = f32[8,17,1024]{2,1,0:T(8,128)S(1)} all-gather(f32[1,17,1024]{2,1,0:T(8,128)S(1)} %maximum_bitcast_fusion), channel_id=2, replica_groups=mesh['ctx_out'=16,'ctx_in'=8,'exp'=8] {'ctx_in'}, dimensions={0}, use_global_device_ids=true | all-gather | bytes 626688 | tf_op jit(solution)/shard_map/all_gather | solution.py:131
  39.7 0.1 fusion.2
  39.8 0.2 select_reduce_fusion.2
  40.1 0.2 multiply_reduce_fusion
  40.3 0.6 maximum_bitcast_fusion.1
  41.1 79.1 %all-gather.6.cloned.1.call-done = f32[16,17,1024]{2,1,0:T(8,128)} async-done(((f32[1,17,1024]{2,1,0:T(8,128)}), f32[16,17,1024]{2,1,0:T(8,128)}) %all-gather.6.cloned.1.call-update) | async-done | bytes 1114128 | tf_op jit(solution)/shard_map/all_gather | solution.py:135
  120.2 1.1 slice.42
  121.3 0.3 select_reduce_fusion
  121.6 1.5 fusion.1
  123.1 0.6 multiply_add_fusion.inc_ref
  123.7 1.9 %broadcast_in_dim.110.inb_ref = f32[256,16,128]{2,1,0:T(8,128)} broadcast(f32[256,16]{1,0:T(8,128)S(1)} %copy.14), dimensions={0,1} | broadcast | bytes 2113536 | tf_op jit(solution)/shard_map/broadcast_in_dim | solution.py:159
  125.6 13.2 %shard_map.87 = (bf16[256,1024]{1,0:T(8,128)(2,1)}, f32[256,16,128]{2,1,0:T(8,128)}) custom-call(bf16[256,1024]{1,0:T(8,128)(2,1)} %g_ref.3, bf16[256,1024]{1,0:T(8,128)(2,1)} %s_ref.3, bf16[256,1024]{1,0:T(8,128)(2,1)} %x_ref.1, f32[256,16,128]{2,1,0:T(8,128)} %broadcast_in_dim.110.inb_ref, f32[256,16,128]{2,1,0:T(8,128)} %broadcast_in_dim.111.outb_ref, ...), custom_call_target="tpu_custom_call" | custom-call | flops 50331648 | bytes 10485760 | tf_op jit(solution)/shard_map/pallas_call | solution.py:92
  138.8 2.2 %reduce_sum.92 = f32[256,16]{1,0:T(8,128)S(1)} reduce(f32[256,16,128]{2,1,0:T(8,128)} %get-tuple-element.9, f32[]{:T(128)} %constant.59.clone.1), dimensions={2}, to_apply=%region_8.9 | reduce | flops 520192 | bytes 2113540 | tf_op jit(solution)/shard_map/reduce_sum | solution.py:167
  141.0 4.6 %collective-permute-start = (f32[16,128]{0,1:T(8,128)S(1)}, f32[16,128]{0,1:T(8,128)S(1)}, u32[]{:S(2)}, u32[]{:S(2)}) collective-permute-start(f32[16,128]{0,1:T(8,128)S(1)} %slice_select_fusion), channel_id=1, source_target_pairs={{0,4},{1,5},{2,6},{3,7},{4,0},{5,1},{6,2},{7,3},{8,12},{9,13},{10,... | collective-permute-start | bytes 24584 | tf_op jit(solution)/shard_map/ppermute | solution.py:150
  145.7 1.9 %collective-permute-done = f32[16,128]{0,1:T(8,128)S(1)} collective-permute-done((f32[16,128]{0,1:T(8,128)S(1)}, f32[16,128]{0,1:T(8,128)S(1)}, u32[]{:S(2)}, u32[]{:S(2)}) %collective-permute-start) | collective-permute-done | bytes 8224 | tf_op jit(solution)/shard_map/ppermute | solution.py:150
  147.6 3.1 %collective-permute-start.1 = (f32[16,64]{0,1:T(8,128)S(1)}, f32[16,64]{0,1:T(8,128)S(1)}, u32[]{:S(2)}, u32[]{:S(2)}) collective-permute-start(f32[16,64]{0,1:T(8,128)S(1)} %slice_select_fusion.1), channel_id=1, source_target_pairs={{0,2},{1,3},{2,0},{3,1},{4,6},{5,7},{6,4},{7,5},{8,10},{9,11},{10,... | collective-permute-start | bytes 12296 | tf_op jit(solution)/shard_map/ppermute | solution.py:150
  150.7 1.5 collective-permute-done.1
  152.2 14.7 %collective-permute-start.2 = (f32[16,32]{0,1:T(8,128)S(1)}, f32[16,32]{0,1:T(8,128)S(1)}, u32[]{:S(2)}, u32[]{:S(2)}) collective-permute-start(f32[16,32]{0,1:T(8,128)S(1)} %slice_select_fusion.2), channel_id=1, source_target_pairs={{0,1},{1,0},{2,3},{3,2},{4,5},{5,4},{6,7},{7,6},{8,9},{9,8},{10,11... | collective-permute-start | bytes 6152 | tf_op jit(solution)/shard_map/ppermute | solution.py:150
  166.9 0.8 collective-permute-done.2
  167.7 0.7 copy.16
  (20 shorter events, 0.3 us)
Async XLA Ops:
  7.2 113.1 %all-gather.6.cloned.1.call-start = ((), (), s32[]{:S(2)}) async-start(), calls=%async_computation | async-start | bytes 1671168 | tf_op jit(solution)/shard_map/all_gather | solution.py:135
  10.0 30.1 %copy-start = (f32[16,1024]{1,0:T(8,128)S(1)}, f32[16,1024]{1,0:T(8,128)}, u32[]{:S(2)}) copy-start(f32[16,1024]{1,0:T(8,128)} %a_ref.3) | copy-start | bytes 196612
  17.0 24.0 %copy-start.1 = (f32[256,16]{0,1:T(8,128)S(1)}, f32[256,16]{0,1:T(8,128)}, u32[]{:S(2)}) copy-start(f32[256,16]{0,1:T(8,128)} %param.10) | copy-start | bytes 49156
  141.0 6.5 %collective-permute-start = (f32[16,128]{0,1:T(8,128)S(1)}, f32[16,128]{0,1:T(8,128)S(1)}, u32[]{:S(2)}, u32[]{:S(2)}) collective-permute-start(f32[16,128]{0,1:T(8,128)S(1)} %slice_select_fusion), channel_id=1, source_target_pairs={{0,4},{1,5},{2,6},{3,7},{4,0},{5,1},{6,2},{7,3},{8,12},{9,13},{10,... | collective-permute-start | bytes 24584 | tf_op jit(solution)/shard_map/ppermute | solution.py:150
  147.6 4.7 %collective-permute-start.1 = (f32[16,64]{0,1:T(8,128)S(1)}, f32[16,64]{0,1:T(8,128)S(1)}, u32[]{:S(2)}, u32[]{:S(2)}) collective-permute-start(f32[16,64]{0,1:T(8,128)S(1)} %slice_select_fusion.1), channel_id=1, source_target_pairs={{0,2},{1,3},{2,0},{3,1},{4,6},{5,7},{6,4},{7,5},{8,10},{9,11},{10,... | collective-permute-start | bytes 12296 | tf_op jit(solution)/shard_map/ppermute | solution.py:150
  152.2 15.5 %collective-permute-start.2 = (f32[16,32]{0,1:T(8,128)S(1)}, f32[16,32]{0,1:T(8,128)S(1)}, u32[]{:S(2)}, u32[]{:S(2)}) collective-permute-start(f32[16,32]{0,1:T(8,128)S(1)} %slice_select_fusion.2), channel_id=1, source_target_pairs={{0,1},{1,0},{2,3},{3,2},{4,5},{5,4},{6,7},{7,6},{8,9},{9,8},{10,11... | collective-permute-start | bytes 6152 | tf_op jit(solution)/shard_map/ppermute | solution.py:150
Sparse Core Ops, SparseCore 0:
  41.1 79.1 all-gather.5

commit v5 on v1

--- a/solution.py
+++ b/solution.py
@@ -121,6 +121,14 @@
     return packed[:states]
 
 
+def exchange_sum(block, axis):
+    size = lax.axis_size(axis)
+    rows, columns = block.shape
+    pieces = jnp.transpose(block.reshape(rows, size, columns // size), (1, 0, 2))
+    got = lax.all_to_all(pieces, axis, 0, 0, tiled=True)
+    return jnp.sum(got, axis=0)
+
+
 def shards(scan_grad, step_size, scan_input, state_in, state_out, decay_rate, skip_gain):
     rows = scan_grad.shape[0]
     states = state_in.shape[1]
@@ -133,7 +141,7 @@
     )
     all_channels = scan_grad.shape[1] * lax.axis_size("exp")
     b_term = jnp.transpose(jnp.sum(b_part, axis=2)) * (1.0 / math.sqrt(all_channels))
-    state_in_grad = lax.psum_scatter(b_term, "exp", scatter_dimension=1, tiled=True)
+    state_in_grad = exchange_sum(b_term, "exp")
     return (scan_input_grad, state_in_grad)
 
 

time: 181 us -> 138 us (0.76)
  the two profiles are of different devices: /device:TPU:1 before, /device:TPU:120 now
where the time goes in v5:
time: 138 us; the launch traced here: 137 us
  waiting for transfers between devices  81.3 us (59%)
  Pallas kernels  20.2 us (15%)
  starting transfers between devices  14.9 us (11%)
  blocking collectives  9.46 us (7%)
  local copies, waits for them, and re-layouts  5.55 us (4%)
  other arithmetic  5.29 us (4%)
    ppermute x7, waiting for transfers between devices, carry_in(): lax.ppermute(packed, 'ctx', [(q, q - reach) for q in range(reach, size)])  75.9 us
    pallas_call x1, Pallas kernels, shard_sweep(): pl.pallas_call(sweep_kernel, out_shape=(jax.ShapeDtypeStruct((rows, chann...  13.2 us
    ppermute x7, starting transfers between devices, carry_in(): lax.ppermute(packed, 'ctx', [(q, q - reach) for q in range(reach, size)])  11.6 us
    all_to_all x1, blocking collectives, exchange_sum(): got = lax.all_to_all(pieces, axis, 0, 0, tiled=True)  9.46 us
    pallas_call x1, Pallas kernels, shard_summary(): pl.pallas_call(summary_kernel, out_shape=(jax.ShapeDtypeStruct(decay_rate...  7.01 us
    ppermute x1, waiting for transfers between devices, carry_in(): packed = lax.ppermute(packed, 'ctx', [(q, q - 1) for q in range(1, size)])  5.36 us
    ppermute x1, starting transfers between devices, carry_in(): packed = lax.ppermute(packed, 'ctx', [(q, q - 1) for q in range(1, size)])  3.25 us
  transfers between devices with their start and end apart: 8, of which 8 were waited for; matrix products, arithmetic and copies ran while one was open for 0% of the time, Pallas kernels for 0%

profile of v5, /device:TPU:120, one launch (start us, length us, event | category | flops | bytes accessed | tf_op | source)
XLA Modules:
  0.0 137.5 jit_solution(11819396844656051966)
XLA Ops:
  0.6 0.8 copy.17
  1.4 1.9 %broadcast_in_dim.7.outb_ref = f32[256,16,128]{2,1,0:T(8,128)} broadcast(f32[256,16]{1,0:T(8,128)S(1)} %copy.17), dimensions={0,1} | broadcast | bytes 2113536 | tf_op jit(solution)/shard_map/broadcast_in_dim | solution.py:136
  3.4 7.0 %shard_map.86 = (f32[16,1024]{1,0:T(8,128)}, f32[1,1024]{1,0:T(1,128)}) custom-call(bf16[256,1024]{1,0:T(8,128)(2,1)} %g_ref.3, bf16[256,1024]{1,0:T(8,128)(2,1)} %s_ref.3, f32[256,16,128]{2,1,0:T(8,128)} %broadcast_in_dim.7.outb_ref, f32[16,1024]{1,0:T(8,128)} %a_ref.3), custom_call_target="tpu_custom_call" | custom-call | flops 25165824 | bytes 3145728 | tf_op jit(solution)/shard_map/pallas_call | solution.py:72
  10.4 0.9 pad_maximum_fusion
  11.3 3.3 %collective-permute-start = (f32[17,1024]{1,0:T(8,128)S(1)}, f32[17,1024]{1,0:T(8,128)S(1)}, u32[]{:S(2)}, u32[]{:S(2)}) collective-permute-start(f32[17,1024]{1,0:T(8,128)S(1)} %pad_maximum_fusion), channel_id=1, source_target_pairs={{8,0},{16,8},{24,16},{32,24},{40,32},{48,40},{56,48},{64,56},{72,6... | collective-permute-start | bytes 208904 | tf_op jit(solution)/shard_map/ppermute | solution.py:113
  14.5 5.4 %collective-permute-done = f32[17,1024]{1,0:T(8,128)S(1)} collective-permute-done((f32[17,1024]{1,0:T(8,128)S(1)}, f32[17,1024]{1,0:T(8,128)S(1)}, u32[]{:S(2)}, u32[]{:S(2)}) %collective-permute-start) | collective-permute-done | bytes 69664 | tf_op jit(solution)/shard_map/ppermute | solution.py:113
  19.9 1.9 %collective-permute-start.1 = (f32[17,1024]{1,0:T(8,128)S(1)}, f32[17,1024]{1,0:T(8,128)S(1)}, u32[]{:S(2)}, u32[]{:S(2)}) collective-permute-start(f32[17,1024]{1,0:T(8,128)S(1)} %collective-permute-done), channel_id=1, source_target_pairs={{8,0},{16,8},{24,16},{32,24},{40,32},{48,40},{56,48},{64,56},{72,6... | collective-permute-start | bytes 208904 | tf_op jit(solution)/shard_map/ppermute | solution.py:116
  21.8 6.7 %collective-permute-done.1 = f32[17,1024]{1,0:T(8,128)S(1)} collective-permute-done((f32[17,1024]{1,0:T(8,128)S(1)}, f32[17,1024]{1,0:T(8,128)S(1)}, u32[]{:S(2)}, u32[]{:S(2)}) %collective-permute-start.1) | collective-permute-done | bytes 69664 | tf_op jit(solution)/shard_map/ppermute | solution.py:116
  28.5 1.9 %collective-permute-start.2 = (f32[17,1024]{1,0:T(8,128)S(1)}, f32[17,1024]{1,0:T(8,128)S(1)}, u32[]{:S(2)}, u32[]{:S(2)}) collective-permute-start(f32[17,1024]{1,0:T(8,128)S(1)} %pad_maximum_fusion.1), channel_id=1, source_target_pairs={{16,0},{24,8},{32,16},{40,24},{48,32},{56,40},{64,48},{72,56},{80,... | collective-permute-start | bytes 208904 | tf_op jit(solution)/shard_map/ppermute | solution.py:116
  30.5 7.6 %collective-permute-done.2 = f32[17,1024]{1,0:T(8,128)S(1)} collective-permute-done((f32[17,1024]{1,0:T(8,128)S(1)}, f32[17,1024]{1,0:T(8,128)S(1)}, u32[]{:S(2)}, u32[]{:S(2)}) %collective-permute-start.2) | collective-permute-done | bytes 69664 | tf_op jit(solution)/shard_map/ppermute | solution.py:116
  38.1 2.0 %collective-permute-start.3 = (f32[17,1024]{1,0:T(8,128)S(1)}, f32[17,1024]{1,0:T(8,128)S(1)}, u32[]{:S(2)}, u32[]{:S(2)}) collective-permute-start(f32[17,1024]{1,0:T(8,128)S(1)} %pad_maximum_fusion.2), channel_id=1, source_target_pairs={{32,0},{40,8},{48,16},{56,24},{64,32},{72,40},{80,48},{88,56},{96,... | collective-permute-start | bytes 208904 | tf_op jit(solution)/shard_map/ppermute | solution.py:116
  40.1 9.3 %collective-permute-done.3 = f32[17,1024]{1,0:T(8,128)S(1)} collective-permute-done((f32[17,1024]{1,0:T(8,128)S(1)}, f32[17,1024]{1,0:T(8,128)S(1)}, u32[]{:S(2)}, u32[]{:S(2)}) %collective-permute-start.3) | collective-permute-done | bytes 69664 | tf_op jit(solution)/shard_map/ppermute | solution.py:116
  49.5 1.9 %collective-permute-start.4 = (f32[17,1024]{1,0:T(8,128)S(1)}, f32[17,1024]{1,0:T(8,128)S(1)}, u32[]{:S(2)}, u32[]{:S(2)}) collective-permute-start(f32[17,1024]{1,0:T(8,128)S(1)} %pad_maximum_fusion.3), channel_id=1, source_target_pairs={{64,0},{72,8},{80,16},{88,24},{96,32},{104,40},{112,48},{120,56},{... | collective-permute-start | bytes 208904 | tf_op jit(solution)/shard_map/ppermute | solution.py:116
  51.4 4.9 %collective-permute-done.4 = f32[17,1024]{1,0:T(8,128)S(1)} collective-permute-done((f32[17,1024]{1,0:T(8,128)S(1)}, f32[17,1024]{1,0:T(8,128)S(1)}, u32[]{:S(2)}, u32[]{:S(2)}) %collective-permute-start.4) | collective-permute-done | bytes 69664 | tf_op jit(solution)/shard_map/ppermute | solution.py:116
  56.4 1.3 collective-permute-start.5
  57.7 15.6 %collective-permute-done.5 = f32[17,1024]{1,0:T(8,128)S(1)} collective-permute-done((f32[17,1024]{1,0:T(8,128)S(1)}, f32[17,1024]{1,0:T(8,128)S(1)}, u32[]{:S(2)}, u32[]{:S(2)}) %collective-permute-start.5) | collective-permute-done | bytes 69664 | tf_op jit(solution)/shard_map/ppermute | solution.py:116
  73.4 1.3 collective-permute-start.6
  74.7 15.0 %collective-permute-done.6 = f32[17,1024]{1,0:T(8,128)S(1)} collective-permute-done((f32[17,1024]{1,0:T(8,128)S(1)}, f32[17,1024]{1,0:T(8,128)S(1)}, u32[]{:S(2)}, u32[]{:S(2)}) %collective-permute-start.6) | collective-permute-done | bytes 69664 | tf_op jit(solution)/shard_map/ppermute | solution.py:116
  89.7 1.3 collective-permute-start.7
  91.1 16.8 %collective-permute-done.7 = f32[17,1024]{1,0:T(8,128)S(1)} collective-permute-done((f32[17,1024]{1,0:T(8,128)S(1)}, f32[17,1024]{1,0:T(8,128)S(1)}, u32[]{:S(2)}, u32[]{:S(2)}) %collective-permute-start.7) | collective-permute-done | bytes 69664 | tf_op jit(solution)/shard_map/ppermute | solution.py:116
  108.6 1.9 %broadcast_in_dim.6.inb_ref = f32[256,16,128]{2,1,0:T(8,128)} broadcast(f32[256,16]{1,0:T(8,128)S(1)} %copy.16), dimensions={0,1} | broadcast | bytes 2113536 | tf_op jit(solution)/shard_map/broadcast_in_dim | solution.py:135
  110.5 13.2 %shard_map.87 = (bf16[256,1024]{1,0:T(8,128)(2,1)}, f32[256,16,128]{2,1,0:T(8,128)}) custom-call(bf16[256,1024]{1,0:T(8,128)(2,1)} %g_ref.3, bf16[256,1024]{1,0:T(8,128)(2,1)} %s_ref.3, bf16[256,1024]{1,0:T(8,128)(2,1)} %x_ref.1, f32[256,16,128]{2,1,0:T(8,128)} %broadcast_in_dim.6.inb_ref, f32[256,16,128]{2,1,0:T(8,128)} %broadcast_in_dim.7.outb_ref, ...), custom_call_target="tpu_custom_call" | custom-call | flops 50331648 | bytes 10485760 | tf_op jit(solution)/shard_map/pallas_call | solution.py:92
  123.7 2.2 %reduce_sum.18 = f32[256,16]{1,0:T(8,128)S(1)} reduce(f32[256,16,128]{2,1,0:T(8,128)} %get-tuple-element.9, f32[]{:T(128)} %constant.0.clone.1), dimensions={2}, to_apply=%region_0.0 | reduce | flops 520192 | bytes 2113540 | tf_op jit(solution)/shard_map/reduce_sum | solution.py:143
  126.1 9.5 %all_to_all.5 = f32[8,1,512]{2,1,0:T(1,128)S(1)} all-to-all(f32[8,1,512]{2,1,0:T(1,128)S(1)} %reshape.10), channel_id=1, replica_groups=mesh['ctx'=128,'exp'=8] {'exp'}, dimensions={0} | all-to-all | bytes 32768 | tf_op jit(solution)/shard_map/all_to_all | solution.py:128
  (31 shorter events, 3.1 us)
Async XLA Ops:
  3.4 25.1 %copy-start = (f32[16,1024]{1,0:T(8,128)S(1)}, f32[16,1024]{1,0:T(8,128)}, u32[]{:S(2)}) copy-start(f32[16,1024]{1,0:T(8,128)} %a_ref.3) | copy-start | bytes 196612
  10.4 80.6 %copy-start.1 = (f32[256,16]{0,1:T(8,128)S(1)}, f32[256,16]{0,1:T(8,128)}, u32[]{:S(2)}) copy-start(f32[256,16]{0,1:T(8,128)} %param.10) | copy-start | bytes 49156
  11.3 8.6 %collective-permute-start = (f32[17,1024]{1,0:T(8,128)S(1)}, f32[17,1024]{1,0:T(8,128)S(1)}, u32[]{:S(2)}, u32[]{:S(2)}) collective-permute-start(f32[17,1024]{1,0:T(8,128)S(1)} %pad_maximum_fusion), channel_id=1, source_target_pairs={{8,0},{16,8},{24,16},{32,24},{40,32},{48,40},{56,48},{64,56},{72,6... | collective-permute-start | bytes 208904 | tf_op jit(solution)/shard_map/ppermute | solution.py:113
  19.9 8.6 %collective-permute-start.1 = (f32[17,1024]{1,0:T(8,128)S(1)}, f32[17,1024]{1,0:T(8,128)S(1)}, u32[]{:S(2)}, u32[]{:S(2)}) collective-permute-start(f32[17,1024]{1,0:T(8,128)S(1)} %collective-permute-done), channel_id=1, source_target_pairs={{8,0},{16,8},{24,16},{32,24},{40,32},{48,40},{56,48},{64,56},{72,6... | collective-permute-start | bytes 208904 | tf_op jit(solution)/shard_map/ppermute | solution.py:116
  28.5 9.5 %collective-permute-start.2 = (f32[17,1024]{1,0:T(8,128)S(1)}, f32[17,1024]{1,0:T(8,128)S(1)}, u32[]{:S(2)}, u32[]{:S(2)}) collective-permute-start(f32[17,1024]{1,0:T(8,128)S(1)} %pad_maximum_fusion.1), channel_id=1, source_target_pairs={{16,0},{24,8},{32,16},{40,24},{48,32},{56,40},{64,48},{72,56},{80,... | collective-permute-start | bytes 208904 | tf_op jit(solution)/shard_map/ppermute | solution.py:116
  38.1 11.3 %collective-permute-start.3 = (f32[17,1024]{1,0:T(8,128)S(1)}, f32[17,1024]{1,0:T(8,128)S(1)}, u32[]{:S(2)}, u32[]{:S(2)}) collective-permute-start(f32[17,1024]{1,0:T(8,128)S(1)} %pad_maximum_fusion.2), channel_id=1, source_target_pairs={{32,0},{40,8},{48,16},{56,24},{64,32},{72,40},{80,48},{88,56},{96,... | collective-permute-start | bytes 208904 | tf_op jit(solution)/shard_map/ppermute | solution.py:116
  49.5 6.9 %collective-permute-start.4 = (f32[17,1024]{1,0:T(8,128)S(1)}, f32[17,1024]{1,0:T(8,128)S(1)}, u32[]{:S(2)}, u32[]{:S(2)}) collective-permute-start(f32[17,1024]{1,0:T(8,128)S(1)} %pad_maximum_fusion.3), channel_id=1, source_target_pairs={{64,0},{72,8},{80,16},{88,24},{96,32},{104,40},{112,48},{120,56},{... | collective-permute-start | bytes 208904 | tf_op jit(solution)/shard_map/ppermute | solution.py:116
  56.4 16.9 %collective-permute-start.5 = (f32[17,1024]{1,0:T(8,128)S(1)}, f32[17,1024]{1,0:T(8,128)S(1)}, u32[]{:S(2)}, u32[]{:S(2)}) collective-permute-start(f32[17,1024]{1,0:T(8,128)S(1)} %pad_maximum_fusion.4), channel_id=1, source_target_pairs={{128,0},{136,8},{144,16},{152,24},{160,32},{168,40},{176,48},{184,... | collective-permute-start | bytes 208904 | tf_op jit(solution)/shard_map/ppermute | solution.py:116
  73.4 16.3 %collective-permute-start.6 = (f32[17,1024]{1,0:T(8,128)S(1)}, f32[17,1024]{1,0:T(8,128)S(1)}, u32[]{:S(2)}, u32[]{:S(2)}) collective-permute-start(f32[17,1024]{1,0:T(8,128)S(1)} %pad_maximum_fusion.5), channel_id=1, source_target_pairs={{256,0},{264,8},{272,16},{280,24},{288,32},{296,40},{304,48},{312,... | collective-permute-start | bytes 208904 | tf_op jit(solution)/shard_map/ppermute | solution.py:116
  89.7 18.2 %collective-permute-start.7 = (f32[17,1024]{1,0:T(8,128)S(1)}, f32[17,1024]{1,0:T(8,128)S(1)}, u32[]{:S(2)}, u32[]{:S(2)}) collective-permute-start(f32[17,1024]{1,0:T(8,128)S(1)} %pad_maximum_fusion.6), channel_id=1, source_target_pairs={{512,0},{520,8},{528,16},{536,24},{544,32},{552,40},{560,48},{568,... | collective-permute-start | bytes 208904 | tf_op jit(solution)/shard_map/ppermute | solution.py:116

commit v6 on v5

--- a/solution.py
+++ b/solution.py
@@ -106,7 +106,7 @@
     )(scan_grad, step_size, scan_input, in_b, out_b, decay_rate, skip_gain, incoming)
 
 
-def carry_in(summary, total, decay_rate):
+def doubling_carry(summary, total, decay_rate):
     size = lax.axis_size("ctx")
     states = summary.shape[0]
     packed = jnp.concatenate([summary, total], axis=0)
@@ -119,6 +119,31 @@
         packed = jnp.concatenate([new_s, own_r + got[states:]], axis=0)
         reach *= 2
     return packed[:states]
+
+
+def carry_in(summary, total, decay_rate):
+    size = lax.axis_size("ctx")
+    if size & (size - 1):
+        return doubling_carry(summary, total, decay_rate)
+    me = lax.axis_index("ctx")
+    states = summary.shape[0]
+    block_s, block_r = summary, total
+    after_s, after_r = jnp.zeros_like(summary), jnp.zeros_like(total)
+    bit = 1
+    while bit < size:
+        packed = jnp.concatenate([block_s, block_r], axis=0)
+        got = lax.ppermute(packed, "ctx", [(q, q ^ bit) for q in range(size)])
+        got_s, got_r = got[:states], got[states:]
+        lower = (me // bit) % 2 == 0
+        after_s = jnp.where(lower, after_s + jnp.exp(decay_rate * after_r) * got_s, after_s)
+        after_r = jnp.where(lower, after_r + got_r, after_r)
+        first_s = jnp.where(lower, block_s, got_s)
+        first_r = jnp.where(lower, block_r, got_r)
+        second_s = jnp.where(lower, got_s, block_s)
+        block_s = first_s + jnp.exp(decay_rate * first_r) * second_s
+        block_r = block_r + got_r
+        bit *= 2
+    return after_s
 
 
 def exchange_sum(block, axis):

time: 138 us -> 123 us (0.89)
  the two profiles are of different devices: /device:TPU:120 before, /device:TPU:1 now
where the time goes in v6:
time: 123 us; the launch traced here: 122 us
  starting transfers between devices  50.3 us (41%)
  blocking collectives  23.6 us (19%)
  Pallas kernels  20.2 us (16%)
  waiting for transfers between devices  14.7 us (12%)
  other arithmetic  6.92 us (6%)
  local copies, waits for them, and re-layouts  5.56 us (5%)
    ppermute x7, starting transfers between devices, carry_in(): got = lax.ppermute(packed, 'ctx', [(q, q ^ bit) for q in range(size)])  50.3 us
    all_to_all x1, blocking collectives, exchange_sum(): got = lax.all_to_all(pieces, axis, 0, 0, tiled=True)  23.6 us
    ppermute x7, waiting for transfers between devices, carry_in(): got = lax.ppermute(packed, 'ctx', [(q, q ^ bit) for q in range(size)])  14.7 us
    pallas_call x1, Pallas kernels, shard_sweep(): pl.pallas_call(sweep_kernel, out_shape=(jax.ShapeDtypeStruct((rows, chann...  13.2 us
    pallas_call x1, Pallas kernels, shard_summary(): pl.pallas_call(summary_kernel, out_shape=(jax.ShapeDtypeStruct(decay_rate...  7.01 us
  transfers between devices with their start and end apart: 7, of which 7 were waited for; matrix products, arithmetic and copies ran while one was open for 0% of the time, Pallas kernels for 0%

profile of v6, /device:TPU:1, one launch (start us, length us, event | category | flops | bytes accessed | tf_op | source)
XLA Modules:
  0.0 122.3 jit_solution(14594629340458721370)
XLA Ops:
  0.6 0.8 copy.17
  1.4 1.9 %broadcast_in_dim.9.outb_ref = f32[256,16,128]{2,1,0:T(8,128)} broadcast(f32[256,16]{1,0:T(8,128)S(1)} %copy.17), dimensions={0,1} | broadcast | bytes 2113536 | tf_op jit(solution)/shard_map/broadcast_in_dim | solution.py:161
  3.4 7.0 %shard_map.86 = (f32[16,1024]{1,0:T(8,128)}, f32[1,1024]{1,0:T(1,128)}) custom-call(bf16[256,1024]{1,0:T(8,128)(2,1)} %g_ref.3, bf16[256,1024]{1,0:T(8,128)(2,1)} %s_ref.3, f32[256,16,128]{2,1,0:T(8,128)} %broadcast_in_dim.9.outb_ref, f32[16,1024]{1,0:T(8,128)} %a_ref.3), custom_call_target="tpu_custom_call" | custom-call | flops 25165824 | bytes 3145728 | tf_op jit(solution)/shard_map/pallas_call | solution.py:72
  10.4 0.9 pad_maximum_fusion
  11.3 4.0 %collective-permute-start = (f32[17,1024]{1,0:T(8,128)S(1)}, f32[17,1024]{1,0:T(8,128)S(1)}, u32[]{:S(2)}, u32[]{:S(2)}) collective-permute-start(f32[17,1024]{1,0:T(8,128)S(1)} %pad_maximum_fusion), channel_id=1, source_target_pairs={{0,8},{8,0},{16,24},{24,16},{32,40},{40,32},{48,56},{56,48},{64,72... | collective-permute-start | bytes 208904 | tf_op jit(solution)/shard_map/ppermute | solution.py:135
  15.3 2.0 %collective-permute-done = f32[17,1024]{1,0:T(8,128)S(1)} collective-permute-done((f32[17,1024]{1,0:T(8,128)S(1)}, f32[17,1024]{1,0:T(8,128)S(1)}, u32[]{:S(2)}, u32[]{:S(2)}) %collective-permute-start) | collective-permute-done | bytes 69664 | tf_op jit(solution)/shard_map/ppermute | solution.py:135
  18.0 0.9 multiply_add_fusion.5
  18.9 4.4 %collective-permute-start.1 = (f32[17,1024]{1,0:T(8,128)S(1)}, f32[17,1024]{1,0:T(8,128)S(1)}, u32[]{:S(2)}, u32[]{:S(2)}) collective-permute-start(f32[17,1024]{1,0:T(8,128)S(1)} %pad_maximum_fusion.1), channel_id=1, source_target_pairs={{0,16},{8,24},{16,0},{24,8},{32,48},{40,56},{48,32},{56,40},{64,80... | collective-permute-start | bytes 208904 | tf_op jit(solution)/shard_map/ppermute | solution.py:135
  23.3 2.0 %collective-permute-done.1 = f32[17,1024]{1,0:T(8,128)S(1)} collective-permute-done((f32[17,1024]{1,0:T(8,128)S(1)}, f32[17,1024]{1,0:T(8,128)S(1)}, u32[]{:S(2)}, u32[]{:S(2)}) %collective-permute-start.1) | collective-permute-done | bytes 69664 | tf_op jit(solution)/shard_map/ppermute | solution.py:135
  25.3 8.6 %collective-permute-start.2 = (f32[17,1024]{1,0:T(8,128)S(1)}, f32[17,1024]{1,0:T(8,128)S(1)}, u32[]{:S(2)}, u32[]{:S(2)}) collective-permute-start(f32[17,1024]{1,0:T(8,128)S(1)} %pad_maximum_fusion.2), channel_id=1, source_target_pairs={{0,32},{8,40},{16,48},{24,56},{32,0},{40,8},{48,16},{56,24},{64,96... | collective-permute-start | bytes 208904 | tf_op jit(solution)/shard_map/ppermute | solution.py:135
  33.9 2.1 %collective-permute-done.2 = f32[17,1024]{1,0:T(8,128)S(1)} collective-permute-done((f32[17,1024]{1,0:T(8,128)S(1)}, f32[17,1024]{1,0:T(8,128)S(1)}, u32[]{:S(2)}, u32[]{:S(2)}) %collective-permute-start.2) | collective-permute-done | bytes 69664 | tf_op jit(solution)/shard_map/ppermute | solution.py:135
  36.0 4.0 %collective-permute-start.3 = (f32[17,1024]{1,0:T(8,128)S(1)}, f32[17,1024]{1,0:T(8,128)S(1)}, u32[]{:S(2)}, u32[]{:S(2)}) collective-permute-start(f32[17,1024]{1,0:T(8,128)S(1)} %pad_maximum_fusion.3), channel_id=1, source_target_pairs={{0,64},{8,72},{16,80},{24,88},{32,96},{40,104},{48,112},{56,120},{... | collective-permute-start | bytes 208904 | tf_op jit(solution)/shard_map/ppermute | solution.py:135
  40.0 2.0 %collective-permute-done.3 = f32[17,1024]{1,0:T(8,128)S(1)} collective-permute-done((f32[17,1024]{1,0:T(8,128)S(1)}, f32[17,1024]{1,0:T(8,128)S(1)}, u32[]{:S(2)}, u32[]{:S(2)}) %collective-permute-start.3) | collective-permute-done | bytes 69664 | tf_op jit(solution)/shard_map/ppermute | solution.py:135
  42.1 5.8 %collective-permute-start.4 = (f32[17,1024]{1,0:T(8,128)S(1)}, f32[17,1024]{1,0:T(8,128)S(1)}, u32[]{:S(2)}, u32[]{:S(2)}) collective-permute-start(f32[17,1024]{1,0:T(8,128)S(1)} %pad_maximum_fusion.4), channel_id=1, source_target_pairs={{0,128},{8,136},{16,144},{24,152},{32,160},{40,168},{48,176},{56,1... | collective-permute-start | bytes 208904 | tf_op jit(solution)/shard_map/ppermute | solution.py:135
  47.9 2.3 %collective-permute-done.4 = f32[17,1024]{1,0:T(8,128)S(1)} collective-permute-done((f32[17,1024]{1,0:T(8,128)S(1)}, f32[17,1024]{1,0:T(8,128)S(1)}, u32[]{:S(2)}, u32[]{:S(2)}) %collective-permute-start.4) | collective-permute-done | bytes 69664 | tf_op jit(solution)/shard_map/ppermute | solution.py:135
  50.2 10.3 %collective-permute-start.5 = (f32[17,1024]{1,0:T(8,128)S(1)}, f32[17,1024]{1,0:T(8,128)S(1)}, u32[]{:S(2)}, u32[]{:S(2)}) collective-permute-start(f32[17,1024]{1,0:T(8,128)S(1)} %pad_maximum_fusion.5), channel_id=1, source_target_pairs={{0,256},{8,264},{16,272},{24,280},{32,288},{40,296},{48,304},{56,3... | collective-permute-start | bytes 208904 | tf_op jit(solution)/shard_map/ppermute | solution.py:135
  60.6 2.5 %collective-permute-done.5 = f32[17,1024]{1,0:T(8,128)S(1)} collective-permute-done((f32[17,1024]{1,0:T(8,128)S(1)}, f32[17,1024]{1,0:T(8,128)S(1)}, u32[]{:S(2)}, u32[]{:S(2)}) %collective-permute-start.5) | collective-permute-done | bytes 69664 | tf_op jit(solution)/shard_map/ppermute | solution.py:135
  63.2 13.2 %collective-permute-start.6 = (f32[17,1024]{1,0:T(8,128)S(1)}, f32[17,1024]{1,0:T(8,128)S(1)}, u32[]{:S(2)}, u32[]{:S(2)}) collective-permute-start(f32[17,1024]{1,0:T(8,128)S(1)} %pad_maximum_fusion.6), channel_id=1, source_target_pairs={{0,512},{8,520},{16,528},{24,536},{32,544},{40,552},{48,560},{56,5... | collective-permute-start | bytes 208904 | tf_op jit(solution)/shard_map/ppermute | solution.py:135
  76.5 2.0 %collective-permute-done.6 = f32[17,1024]{1,0:T(8,128)S(1)} collective-permute-done((f32[17,1024]{1,0:T(8,128)S(1)}, f32[17,1024]{1,0:T(8,128)S(1)}, u32[]{:S(2)}, u32[]{:S(2)}) %collective-permute-start.6) | collective-permute-done | bytes 69664 | tf_op jit(solution)/shard_map/ppermute | solution.py:135
  78.5 0.7 add_select_fusion.inc_ref
  79.2 1.9 %broadcast_in_dim.8.inb_ref = f32[256,16,128]{2,1,0:T(8,128)} broadcast(f32[256,16]{1,0:T(8,128)S(1)} %copy.16), dimensions={0,1} | broadcast | bytes 2113536 | tf_op jit(solution)/shard_map/broadcast_in_dim | solution.py:160
  81.2 13.2 %shard_map.87 = (bf16[256,1024]{1,0:T(8,128)(2,1)}, f32[256,16,128]{2,1,0:T(8,128)}) custom-call(bf16[256,1024]{1,0:T(8,128)(2,1)} %g_ref.3, bf16[256,1024]{1,0:T(8,128)(2,1)} %s_ref.3, bf16[256,1024]{1,0:T(8,128)(2,1)} %x_ref.1, f32[256,16,128]{2,1,0:T(8,128)} %broadcast_in_dim.8.inb_ref, f32[256,16,128]{2,1,0:T(8,128)} %broadcast_in_dim.9.outb_ref, ...), custom_call_target="tpu_custom_call" | custom-call | flops 50331648 | bytes 10485760 | tf_op jit(solution)/shard_map/pallas_call | solution.py:92
  94.3 2.2 %reduce_sum.18 = f32[256,16]{1,0:T(8,128)S(1)} reduce(f32[256,16,128]{2,1,0:T(8,128)} %get-tuple-element.9, f32[]{:T(128)} %constant.121.clone.1), dimensions={2}, to_apply=%region_0.1 | reduce | flops 520192 | bytes 2113540 | tf_op jit(solution)/shard_map/reduce_sum | solution.py:168
  96.8 23.6 %all_to_all.5 = f32[8,1,512]{2,1,0:T(1,128)S(1)} all-to-all(f32[8,1,512]{2,1,0:T(1,128)S(1)} %reshape.10), channel_id=1, replica_groups=mesh['ctx'=128,'exp'=8] {'exp'}, dimensions={0} | all-to-all | bytes 32768 | tf_op jit(solution)/shard_map/all_to_all | solution.py:153
  (29 shorter events, 3.1 us)
Async XLA Ops:
  3.4 14.6 %copy-start = (f32[16,1024]{1,0:T(8,128)S(1)}, f32[16,1024]{1,0:T(8,128)}, u32[]{:S(2)}) copy-start(f32[16,1024]{1,0:T(8,128)} %a_ref.3) | copy-start | bytes 196612
  10.4 66.0 %copy-start.1 = (f32[256,16]{0,1:T(8,128)S(1)}, f32[256,16]{0,1:T(8,128)}, u32[]{:S(2)}) copy-start(f32[256,16]{0,1:T(8,128)} %param.10) | copy-start | bytes 49156
  11.3 6.0 %collective-permute-start = (f32[17,1024]{1,0:T(8,128)S(1)}, f32[17,1024]{1,0:T(8,128)S(1)}, u32[]{:S(2)}, u32[]{:S(2)}) collective-permute-start(f32[17,1024]{1,0:T(8,128)S(1)} %pad_maximum_fusion), channel_id=1, source_target_pairs={{0,8},{8,0},{16,24},{24,16},{32,40},{40,32},{48,56},{56,48},{64,72... | collective-permute-start | bytes 208904 | tf_op jit(solution)/shard_map/ppermute | solution.py:135
  18.9 6.4 %collective-permute-start.1 = (f32[17,1024]{1,0:T(8,128)S(1)}, f32[17,1024]{1,0:T(8,128)S(1)}, u32[]{:S(2)}, u32[]{:S(2)}) collective-permute-start(f32[17,1024]{1,0:T(8,128)S(1)} %pad_maximum_fusion.1), channel_id=1, source_target_pairs={{0,16},{8,24},{16,0},{24,8},{32,48},{40,56},{48,32},{56,40},{64,80... | collective-permute-start | bytes 208904 | tf_op jit(solution)/shard_map/ppermute | solution.py:135
  25.3 10.7 %collective-permute-start.2 = (f32[17,1024]{1,0:T(8,128)S(1)}, f32[17,1024]{1,0:T(8,128)S(1)}, u32[]{:S(2)}, u32[]{:S(2)}) collective-permute-start(f32[17,1024]{1,0:T(8,128)S(1)} %pad_maximum_fusion.2), channel_id=1, source_target_pairs={{0,32},{8,40},{16,48},{24,56},{32,0},{40,8},{48,16},{56,24},{64,96... | collective-permute-start | bytes 208904 | tf_op jit(solution)/shard_map/ppermute | solution.py:135
  36.0 6.0 %collective-permute-start.3 = (f32[17,1024]{1,0:T(8,128)S(1)}, f32[17,1024]{1,0:T(8,128)S(1)}, u32[]{:S(2)}, u32[]{:S(2)}) collective-permute-start(f32[17,1024]{1,0:T(8,128)S(1)} %pad_maximum_fusion.3), channel_id=1, source_target_pairs={{0,64},{8,72},{16,80},{24,88},{32,96},{40,104},{48,112},{56,120},{... | collective-permute-start | bytes 208904 | tf_op jit(solution)/shard_map/ppermute | solution.py:135
  42.1 8.1 %collective-permute-start.4 = (f32[17,1024]{1,0:T(8,128)S(1)}, f32[17,1024]{1,0:T(8,128)S(1)}, u32[]{:S(2)}, u32[]{:S(2)}) collective-permute-start(f32[17,1024]{1,0:T(8,128)S(1)} %pad_maximum_fusion.4), channel_id=1, source_target_pairs={{0,128},{8,136},{16,144},{24,152},{32,160},{40,168},{48,176},{56,1... | collective-permute-start | bytes 208904 | tf_op jit(solution)/shard_map/ppermute | solution.py:135
  50.2 12.9 %collective-permute-start.5 = (f32[17,1024]{1,0:T(8,128)S(1)}, f32[17,1024]{1,0:T(8,128)S(1)}, u32[]{:S(2)}, u32[]{:S(2)}) collective-permute-start(f32[17,1024]{1,0:T(8,128)S(1)} %pad_maximum_fusion.5), channel_id=1, source_target_pairs={{0,256},{8,264},{16,272},{24,280},{32,288},{40,296},{48,304},{56,3... | collective-permute-start | bytes 208904 | tf_op jit(solution)/shard_map/ppermute | solution.py:135
  63.2 15.3 %collective-permute-start.6 = (f32[17,1024]{1,0:T(8,128)S(1)}, f32[17,1024]{1,0:T(8,128)S(1)}, u32[]{:S(2)}, u32[]{:S(2)}) collective-permute-start(f32[17,1024]{1,0:T(8,128)S(1)} %pad_maximum_fusion.6), channel_id=1, source_target_pairs={{0,512},{8,520},{16,528},{24,536},{32,544},{40,552},{48,560},{56,5... | collective-permute-start | bytes 208904 | tf_op jit(solution)/shard_map/ppermute | solution.py:135

commit v7 on v5

--- a/solution.py
+++ b/solution.py
@@ -14,22 +14,27 @@
     return jnp.concatenate([column_block] * tiles, axis=1)
 
 
-def summary_kernel(g_ref, s_ref, outb_ref, a_ref, sum_ref, tot_ref, gf, sf):
+def summary_kernel(g_ref, s_ref, outb_ref, a_ref, out_ref, gf, sf):
     rows, channels = g_ref.shape
+    states = a_ref.shape[0]
     tiles = channels // LANES
     gf[...] = g_ref[...].astype(jnp.float32)
     sf[...] = s_ref[...].astype(jnp.float32)
-    tot_ref[...] = jnp.sum(sf[...], axis=0, keepdims=True)
     a = a_ref[...]
 
-    def body(i, incoming):
+    def body(i, carry):
+        incoming, decay = carry
         t = rows - 1 - i
         g_row = gf[pl.ds(t, 1), :]
         s_row = sf[pl.ds(t, 1), :]
         adjoint = tiled(outb_ref[t], tiles) * g_row + incoming
-        return jnp.exp(s_row * a) * adjoint
+        step_decay = jnp.exp(s_row * a)
+        return (step_decay * adjoint, step_decay * decay)
 
-    sum_ref[...] = lax.fori_loop(0, rows, body, jnp.zeros(a.shape, jnp.float32), unroll=8)
+    start = (jnp.zeros(a.shape, jnp.float32), jnp.ones(a.shape, jnp.float32))
+    summary, decay = lax.fori_loop(0, rows, body, start, unroll=8)
+    out_ref[0:states, :] = summary
+    out_ref[states:, :] = decay
 
 
 def sweep_kernel(
@@ -69,17 +74,15 @@
 
 def shard_summary(scan_grad, step_size, out_b, decay_rate):
     rows, channels = scan_grad.shape
+    states = decay_rate.shape[0]
     return pl.pallas_call(
         summary_kernel,
-        out_shape=(
-            jax.ShapeDtypeStruct(decay_rate.shape, jnp.float32),
-            jax.ShapeDtypeStruct((1, channels), jnp.float32),
-        ),
+        out_shape=jax.ShapeDtypeStruct((2 * states, channels), jnp.float32),
         in_specs=[vmem_spec()] * 4,
-        out_specs=(vmem_spec(), vmem_spec()),
+        out_specs=vmem_spec(),
         scratch_shapes=[pltpu.VMEM((rows, channels), jnp.float32)] * 2,
         cost_estimate=pl.CostEstimate(
-            flops=6 * rows * decay_rate.size,
+            flops=7 * rows * decay_rate.size,
             transcendentals=rows * decay_rate.size,
             bytes_accessed=4 * rows * channels + 4 * out_b.size,
         ),
@@ -106,19 +109,44 @@
     )(scan_grad, step_size, scan_input, in_b, out_b, decay_rate, skip_gain, incoming)
 
 
-def carry_in(summary, total, decay_rate):
+def doubling_carry(packed, states):
     size = lax.axis_size("ctx")
-    states = summary.shape[0]
-    packed = jnp.concatenate([summary, total], axis=0)
+    ones = jnp.concatenate([jnp.zeros_like(packed[:states]), jnp.ones_like(packed[states:])])
     packed = lax.ppermute(packed, "ctx", [(q, q - 1) for q in range(1, size)])
+    packed = jnp.where(lax.axis_index("ctx") == size - 1, ones, packed)
     reach = 1
     while reach < size:
         got = lax.ppermute(packed, "ctx", [(q, q - reach) for q in range(reach, size)])
-        own_s, own_r = packed[:states], packed[states:]
-        new_s = own_s + jnp.exp(decay_rate * own_r) * got[:states]
-        packed = jnp.concatenate([new_s, own_r + got[states:]], axis=0)
+        beyond = lax.axis_index("ctx") + reach >= size
+        got = jnp.where(beyond, ones, got)
+        new_s = packed[:states] + packed[states:] * got[:states]
+        packed = jnp.concatenate([new_s, packed[states:] * got[states:]], axis=0)
         reach *= 2
     return packed[:states]
+
+
+def carry_in(packed, states):
+    size = lax.axis_size("ctx")
+    if size & (size - 1):
+        return doubling_carry(packed, states)
+    me = lax.axis_index("ctx")
+    block_s, block_d = packed[:states], packed[states:]
+    after_s, after_d = jnp.zeros_like(block_s), jnp.ones_like(block_d)
+    bit = 1
+    while bit < size:
+        got = lax.ppermute(packed, "ctx", [(q, q ^ bit) for q in range(size)])
+        got_s, got_d = got[:states], got[states:]
+        lower = (me // bit) % 2 == 0
+        after_s = jnp.where(lower, after_s + after_d * got_s, after_s)
+        after_d = jnp.where(lower, after_d * got_d, after_d)
+        first_s = jnp.where(lower, block_s, got_s)
+        first_d = jnp.where(lower, block_d, got_d)
+        second_s = jnp.where(lower, got_s, block_s)
+        block_s = first_s + first_d * second_s
+        block_d = block_d * got_d
+        packed = jnp.concatenate([block_s, block_d], axis=0)
+        bit *= 2
+    return after_s
 
 
 def exchange_sum(block, axis):
@@ -134,8 +162,8 @@
     states = state_in.shape[1]
     in_b = jnp.broadcast_to(state_in[:, :, None], (rows, states, LANES))
     out_b = jnp.broadcast_to(state_out[:, :, None], (rows, states, LANES))
-    summary, total = shard_summary(scan_grad, step_size, out_b, decay_rate)
-    carried = carry_in(summary, total, decay_rate)
+    packed = shard_summary(scan_grad, step_size, out_b, decay_rate)
+    carried = carry_in(packed, states)
     scan_input_grad, b_part = shard_sweep(
         scan_grad, step_size, scan_input, in_b, out_b, decay_rate, skip_gain[None, :], carried
     )

time: 138 us -> 136 us (0.986)
  the two profiles are of different devices: /device:TPU:120 before, /device:TPU:24 now
where the time goes in v7:
time: 136 us; the launch traced here: 135 us
  waiting for transfers between devices  54.1 us (40%)
  starting transfers between devices  39.5 us (29%)
  Pallas kernels  20.8 us (15%)
  blocking collectives  9.23 us (7%)
  local copies, waits for them, and re-layouts  5.58 us (4%)
  other arithmetic  5.27 us (4%)
    ppermute x7, waiting for transfers between devices, carry_in(): got = lax.ppermute(packed, 'ctx', [(q, q ^ bit) for q in range(size)])  54.1 us
    ppermute x7, starting transfers between devices, carry_in(): got = lax.ppermute(packed, 'ctx', [(q, q ^ bit) for q in range(size)])  39.5 us
    pallas_call x1, Pallas kernels, shard_sweep(): pl.pallas_call(sweep_kernel, out_shape=(jax.ShapeDtypeStruct((rows, chann...  13.2 us
    all_to_all x1, blocking collectives, exchange_sum(): got = lax.all_to_all(pieces, axis, 0, 0, tiled=True)  9.23 us
    pallas_call x1, Pallas kernels, shard_summary(): pl.pallas_call(summary_kernel, out_shape=jax.ShapeDtypeStruct((2 * states...  7.61 us
  transfers between devices with their start and end apart: 7, of which 7 were waited for; matrix products, arithmetic and copies ran while one was open for 0% of the time, Pallas kernels for 0%

profile of v7, /device:TPU:24, one launch (start us, length us, event | category | flops | bytes accessed | tf_op | source)
XLA Modules:
  0.0 135.5 jit_solution(7583408580467932137)
XLA Ops:
  0.6 0.8 copy.17
  1.4 1.9 %broadcast_in_dim.22.outb_ref = f32[256,16,128]{2,1,0:T(8,128)} broadcast(f32[256,16]{1,0:T(8,128)S(1)} %copy.17), dimensions={0,1} | broadcast | bytes 2113536 | tf_op jit(solution)/shard_map/broadcast_in_dim | solution.py:164
  3.4 7.6 %shard_map.86 = f32[32,1024]{1,0:T(8,128)} custom-call(bf16[256,1024]{1,0:T(8,128)(2,1)} %g_ref.3, bf16[256,1024]{1,0:T(8,128)(2,1)} %s_ref.3, f32[256,16,128]{2,1,0:T(8,128)} %broadcast_in_dim.22.outb_ref, f32[16,1024]{1,0:T(8,128)} %a_ref.3), custom_call_target="tpu_custom_call" | custom-call | flops 29360128 | bytes 3145728 | tf_op jit(solution)/shard_map/pallas_call | solution.py:78
  11.0 2.3 %collective-permute-start = (f32[32,1024]{1,0:T(8,128)}, f32[32,1024]{1,0:T(8,128)S(1)}, u32[]{:S(2)}, u32[]{:S(2)}) collective-permute-start(f32[32,1024]{1,0:T(8,128)} %shard_map.86), channel_id=1, source_target_pairs={{0,8},{8,0},{16,24},{24,16},{32,40},{40,32},{48,56},{56,48},{64,72... | collective-permute-start | bytes 393224 | tf_op jit(solution)/shard_map/ppermute | solution.py:137
  13.4 4.9 %collective-permute-done = f32[32,1024]{1,0:T(8,128)S(1)} collective-permute-done((f32[32,1024]{1,0:T(8,128)}, f32[32,1024]{1,0:T(8,128)S(1)}, u32[]{:S(2)}, u32[]{:S(2)}) %collective-permute-start) | collective-permute-done | bytes 131104 | tf_op jit(solution)/shard_map/ppermute | solution.py:137
  18.3 0.9 multiply_add_fusion.5
  19.2 13.1 %collective-permute-start.1 = (f32[32,1024]{1,0:T(8,128)S(1)}, f32[32,1024]{1,0:T(8,128)S(1)}, u32[]{:S(2)}, u32[]{:S(2)}) collective-permute-start(f32[32,1024]{1,0:T(8,128)S(1)} %pad_maximum_fusion), channel_id=1, source_target_pairs={{0,16},{8,24},{16,0},{24,8},{32,48},{40,56},{48,32},{56,40},{64,80... | collective-permute-start | bytes 393224 | tf_op jit(solution)/shard_map/ppermute | solution.py:137
  32.3 7.1 %collective-permute-done.1 = f32[32,1024]{1,0:T(8,128)S(1)} collective-permute-done((f32[32,1024]{1,0:T(8,128)S(1)}, f32[32,1024]{1,0:T(8,128)S(1)}, u32[]{:S(2)}, u32[]{:S(2)}) %collective-permute-start.1) | collective-permute-done | bytes 131104 | tf_op jit(solution)/shard_map/ppermute | solution.py:137
  39.5 1.9 %collective-permute-start.2 = (f32[32,1024]{1,0:T(8,128)S(1)}, f32[32,1024]{1,0:T(8,128)S(1)}, u32[]{:S(2)}, u32[]{:S(2)}) collective-permute-start(f32[32,1024]{1,0:T(8,128)S(1)} %pad_maximum_fusion.1), channel_id=1, source_target_pairs={{0,32},{8,40},{16,48},{24,56},{32,0},{40,8},{48,16},{56,24},{64,96... | collective-permute-start | bytes 393224 | tf_op jit(solution)/shard_map/ppermute | solution.py:137
  41.4 8.8 %collective-permute-done.2 = f32[32,1024]{1,0:T(8,128)S(1)} collective-permute-done((f32[32,1024]{1,0:T(8,128)S(1)}, f32[32,1024]{1,0:T(8,128)S(1)}, u32[]{:S(2)}, u32[]{:S(2)}) %collective-permute-start.2) | collective-permute-done | bytes 131104 | tf_op jit(solution)/shard_map/ppermute | solution.py:137
  50.3 1.9 %collective-permute-start.3 = (f32[32,1024]{1,0:T(8,128)S(1)}, f32[32,1024]{1,0:T(8,128)S(1)}, u32[]{:S(2)}, u32[]{:S(2)}) collective-permute-start(f32[32,1024]{1,0:T(8,128)S(1)} %pad_maximum_fusion.2), channel_id=1, source_target_pairs={{0,64},{8,72},{16,80},{24,88},{32,96},{40,104},{48,112},{56,120},{... | collective-permute-start | bytes 393224 | tf_op jit(solution)/shard_map/ppermute | solution.py:137
  52.2 5.2 %collective-permute-done.3 = f32[32,1024]{1,0:T(8,128)S(1)} collective-permute-done((f32[32,1024]{1,0:T(8,128)S(1)}, f32[32,1024]{1,0:T(8,128)S(1)}, u32[]{:S(2)}, u32[]{:S(2)}) %collective-permute-start.3) | collective-permute-done | bytes 131104 | tf_op jit(solution)/shard_map/ppermute | solution.py:137
  57.4 1.9 %collective-permute-start.4 = (f32[32,1024]{1,0:T(8,128)S(1)}, f32[32,1024]{1,0:T(8,128)S(1)}, u32[]{:S(2)}, u32[]{:S(2)}) collective-permute-start(f32[32,1024]{1,0:T(8,128)S(1)} %pad_maximum_fusion.3), channel_id=1, source_target_pairs={{0,128},{8,136},{16,144},{24,152},{32,160},{40,168},{48,176},{56,1... | collective-permute-start | bytes 393224 | tf_op jit(solution)/shard_map/ppermute | solution.py:137
  59.4 6.7 %collective-permute-done.4 = f32[32,1024]{1,0:T(8,128)S(1)} collective-permute-done((f32[32,1024]{1,0:T(8,128)S(1)}, f32[32,1024]{1,0:T(8,128)S(1)}, u32[]{:S(2)}, u32[]{:S(2)}) %collective-permute-start.4) | collective-permute-done | bytes 131104 | tf_op jit(solution)/shard_map/ppermute | solution.py:137
  66.2 5.4 %collective-permute-start.5 = (f32[32,1024]{1,0:T(8,128)S(1)}, f32[32,1024]{1,0:T(8,128)S(1)}, u32[]{:S(2)}, u32[]{:S(2)}) collective-permute-start(f32[32,1024]{1,0:T(8,128)S(1)} %pad_maximum_fusion.4), channel_id=1, source_target_pairs={{0,256},{8,264},{16,272},{24,280},{32,288},{40,296},{48,304},{56,3... | collective-permute-start | bytes 393224 | tf_op jit(solution)/shard_map/ppermute | solution.py:137
  71.7 9.7 %collective-permute-done.5 = f32[32,1024]{1,0:T(8,128)S(1)} collective-permute-done((f32[32,1024]{1,0:T(8,128)S(1)}, f32[32,1024]{1,0:T(8,128)S(1)}, u32[]{:S(2)}, u32[]{:S(2)}) %collective-permute-start.5) | collective-permute-done | bytes 131104 | tf_op jit(solution)/shard_map/ppermute | solution.py:137
  81.5 12.9 %collective-permute-start.6 = (f32[32,1024]{1,0:T(8,128)S(1)}, f32[32,1024]{1,0:T(8,128)S(1)}, u32[]{:S(2)}, u32[]{:S(2)}) collective-permute-start(f32[32,1024]{1,0:T(8,128)S(1)} %pad_maximum_fusion.5), channel_id=1, source_target_pairs={{0,512},{8,520},{16,528},{24,536},{32,544},{40,552},{48,560},{56,5... | collective-permute-start | bytes 393224 | tf_op jit(solution)/shard_map/ppermute | solution.py:137
  94.5 11.6 %collective-permute-done.6 = f32[32,1024]{1,0:T(8,128)S(1)} collective-permute-done((f32[32,1024]{1,0:T(8,128)S(1)}, f32[32,1024]{1,0:T(8,128)S(1)}, u32[]{:S(2)}, u32[]{:S(2)}) %collective-permute-start.6) | collective-permute-done | bytes 131104 | tf_op jit(solution)/shard_map/ppermute | solution.py:137
  106.1 0.7 add_select_fusion.inc_ref
  106.8 2.0 %broadcast_in_dim.10.inb_ref = f32[256,16,128]{2,1,0:T(8,128)} broadcast(f32[256,16]{1,0:T(8,128)S(1)} %copy.16), dimensions={0,1} | broadcast | bytes 2113536 | tf_op jit(solution)/shard_map/broadcast_in_dim | solution.py:163
  108.7 13.2 %shard_map.87 = (bf16[256,1024]{1,0:T(8,128)(2,1)}, f32[256,16,128]{2,1,0:T(8,128)}) custom-call(bf16[256,1024]{1,0:T(8,128)(2,1)} %g_ref.3, bf16[256,1024]{1,0:T(8,128)(2,1)} %s_ref.3, bf16[256,1024]{1,0:T(8,128)(2,1)} %x_ref.1, f32[256,16,128]{2,1,0:T(8,128)} %broadcast_in_dim.10.inb_ref, f32[256,16,128]{2,1,0:T(8,128)} %broadcast_in_dim.22.outb_ref, ...), custom_call_target="tpu_custom_call" | custom-call | flops 50331648 | bytes 10485760 | tf_op jit(solution)/shard_map/pallas_call | solution.py:95
  121.9 2.2 %reduce_sum.18 = f32[256,16]{1,0:T(8,128)S(1)} reduce(f32[256,16,128]{2,1,0:T(8,128)} %get-tuple-element.5, f32[]{:T(128)} %constant.121.clone.1), dimensions={2}, to_apply=%region_0.1 | reduce | flops 520192 | bytes 2113540 | tf_op jit(solution)/shard_map/reduce_sum | solution.py:171
  124.3 9.2 %all_to_all.5 = f32[8,1,512]{2,1,0:T(1,128)S(1)} all-to-all(f32[8,1,512]{2,1,0:T(1,128)S(1)} %reshape.10), channel_id=1, replica_groups=mesh['ctx'=128,'exp'=8] {'exp'}, dimensions={0} | all-to-all | bytes 32768 | tf_op jit(solution)/shard_map/all_to_all | solution.py:156
  134.1 0.7 reduce
  (20 shorter events, 1.7 us)
Async XLA Ops:
  11.0 7.3 %collective-permute-start = (f32[32,1024]{1,0:T(8,128)}, f32[32,1024]{1,0:T(8,128)S(1)}, u32[]{:S(2)}, u32[]{:S(2)}) collective-permute-start(f32[32,1024]{1,0:T(8,128)} %shard_map.86), channel_id=1, source_target_pairs={{0,8},{8,0},{16,24},{24,16},{32,40},{40,32},{48,56},{56,48},{64,72... | collective-permute-start | bytes 393224 | tf_op jit(solution)/shard_map/ppermute | solution.py:137
  13.3 81.0 %copy-start = (f32[256,16]{0,1:T(8,128)S(1)}, f32[256,16]{0,1:T(8,128)}, u32[]{:S(2)}) copy-start(f32[256,16]{0,1:T(8,128)} %param.10) | copy-start | bytes 49156
  19.2 20.2 %collective-permute-start.1 = (f32[32,1024]{1,0:T(8,128)S(1)}, f32[32,1024]{1,0:T(8,128)S(1)}, u32[]{:S(2)}, u32[]{:S(2)}) collective-permute-start(f32[32,1024]{1,0:T(8,128)S(1)} %pad_maximum_fusion), channel_id=1, source_target_pairs={{0,16},{8,24},{16,0},{24,8},{32,48},{40,56},{48,32},{56,40},{64,80... | collective-permute-start | bytes 393224 | tf_op jit(solution)/shard_map/ppermute | solution.py:137
  39.5 10.8 %collective-permute-start.2 = (f32[32,1024]{1,0:T(8,128)S(1)}, f32[32,1024]{1,0:T(8,128)S(1)}, u32[]{:S(2)}, u32[]{:S(2)}) collective-permute-start(f32[32,1024]{1,0:T(8,128)S(1)} %pad_maximum_fusion.1), channel_id=1, source_target_pairs={{0,32},{8,40},{16,48},{24,56},{32,0},{40,8},{48,16},{56,24},{64,96... | collective-permute-start | bytes 393224 | tf_op jit(solution)/shard_map/ppermute | solution.py:137
  50.3 7.1 %collective-permute-start.3 = (f32[32,1024]{1,0:T(8,128)S(1)}, f32[32,1024]{1,0:T(8,128)S(1)}, u32[]{:S(2)}, u32[]{:S(2)}) collective-permute-start(f32[32,1024]{1,0:T(8,128)S(1)} %pad_maximum_fusion.2), channel_id=1, source_target_pairs={{0,64},{8,72},{16,80},{24,88},{32,96},{40,104},{48,112},{56,120},{... | collective-permute-start | bytes 393224 | tf_op jit(solution)/shard_map/ppermute | solution.py:137
  57.4 8.7 %collective-permute-start.4 = (f32[32,1024]{1,0:T(8,128)S(1)}, f32[32,1024]{1,0:T(8,128)S(1)}, u32[]{:S(2)}, u32[]{:S(2)}) collective-permute-start(f32[32,1024]{1,0:T(8,128)S(1)} %pad_maximum_fusion.3), channel_id=1, source_target_pairs={{0,128},{8,136},{16,144},{24,152},{32,160},{40,168},{48,176},{56,1... | collective-permute-start | bytes 393224 | tf_op jit(solution)/shard_map/ppermute | solution.py:137
  66.2 15.2 %collective-permute-start.5 = (f32[32,1024]{1,0:T(8,128)S(1)}, f32[32,1024]{1,0:T(8,128)S(1)}, u32[]{:S(2)}, u32[]{:S(2)}) collective-permute-start(f32[32,1024]{1,0:T(8,128)S(1)} %pad_maximum_fusion.4), channel_id=1, source_target_pairs={{0,256},{8,264},{16,272},{24,280},{32,288},{40,296},{48,304},{56,3... | collective-permute-start | bytes 393224 | tf_op jit(solution)/shard_map/ppermute | solution.py:137
  81.5 24.6 %collective-permute-start.6 = (f32[32,1024]{1,0:T(8,128)S(1)}, f32[32,1024]{1,0:T(8,128)S(1)}, u32[]{:S(2)}, u32[]{:S(2)}) collective-permute-start(f32[32,1024]{1,0:T(8,128)S(1)} %pad_maximum_fusion.5), channel_id=1, source_target_pairs={{0,512},{8,520},{16,528},{24,536},{32,544},{40,552},{48,560},{56,5... | collective-permute-start | bytes 393224 | tf_op jit(solution)/shard_map/ppermute | solution.py:137

commit v8 on v6

--- a/solution.py
+++ b/solution.py
@@ -8,28 +8,32 @@
 from jax.sharding import PartitionSpec as P
 
 LANES = 128
+LOG2_E = 1.4426950408889634
 
 
 def tiled(column_block, tiles):
     return jnp.concatenate([column_block] * tiles, axis=1)
 
 
-def summary_kernel(g_ref, s_ref, outb_ref, a_ref, sum_ref, tot_ref, gf, sf):
+def summary_kernel(g_ref, s_ref, outb_ref, a_ref, out_ref, gf, sf):
     rows, channels = g_ref.shape
+    states = a_ref.shape[0]
     tiles = channels // LANES
     gf[...] = g_ref[...].astype(jnp.float32)
     sf[...] = s_ref[...].astype(jnp.float32)
-    tot_ref[...] = jnp.sum(sf[...], axis=0, keepdims=True)
-    a = a_ref[...]
+    out_ref[states:, :] = jnp.sum(sf[...], axis=0, keepdims=True)
+    a = a_ref[...] * LOG2_E
 
     def body(i, incoming):
         t = rows - 1 - i
         g_row = gf[pl.ds(t, 1), :]
         s_row = sf[pl.ds(t, 1), :]
         adjoint = tiled(outb_ref[t], tiles) * g_row + incoming
-        return jnp.exp(s_row * a) * adjoint
+        return jnp.exp2(s_row * a) * adjoint
 
-    sum_ref[...] = lax.fori_loop(0, rows, body, jnp.zeros(a.shape, jnp.float32), unroll=8)
+    out_ref[0:states, :] = lax.fori_loop(
+        0, rows, body, jnp.zeros(a.shape, jnp.float32), unroll=8
+    )
 
 
 def sweep_kernel(
@@ -41,7 +45,7 @@
     gf[...] = g_ref[...].astype(jnp.float32)
     sf[...] = s_ref[...].astype(jnp.float32)
     wf[...] = sf[...] * x_ref[...].astype(jnp.float32)
-    a = a_ref[...]
+    a = a_ref[...] * LOG2_E
     skip = skip_ref[...]
 
     def body(i, incoming):
@@ -57,7 +61,7 @@
         for k in range(1, tiles):
             part = part + weighted[:, k * LANES:(k + 1) * LANES]
         bp_ref[t] = part
-        return jnp.exp(s_row * a) * adjoint
+        return jnp.exp2(s_row * a) * adjoint
 
     lax.fori_loop(0, rows, body, inc_ref[...], unroll=8)
     res_ref[...] = rf[...].astype(res_ref.dtype)
@@ -69,14 +73,12 @@
 
 def shard_summary(scan_grad, step_size, out_b, decay_rate):
     rows, channels = scan_grad.shape
+    states = decay_rate.shape[0]
     return pl.pallas_call(
         summary_kernel,
-        out_shape=(
-            jax.ShapeDtypeStruct(decay_rate.shape, jnp.float32),
-            jax.ShapeDtypeStruct((1, channels), jnp.float32),
-        ),
+        out_shape=jax.ShapeDtypeStruct((states + 1, channels), jnp.float32),
         in_specs=[vmem_spec()] * 4,
-        out_specs=(vmem_spec(), vmem_spec()),
+        out_specs=vmem_spec(),
         scratch_shapes=[pltpu.VMEM((rows, channels), jnp.float32)] * 2,
         cost_estimate=pl.CostEstimate(
             flops=6 * rows * decay_rate.size,
@@ -121,17 +123,18 @@
     return packed[:states]
 
 
-def carry_in(summary, total, decay_rate):
+def carry_in(packed, decay_rate):
     size = lax.axis_size("ctx")
+    states = packed.shape[0] - 1
     if size & (size - 1):
-        return doubling_carry(summary, total, decay_rate)
+        return doubling_carry(packed[:states], packed[states:], decay_rate)
     me = lax.axis_index("ctx")
-    states = summary.shape[0]
-    block_s, block_r = summary, total
-    after_s, after_r = jnp.zeros_like(summary), jnp.zeros_like(total)
+    block_s, block_r = packed[:states], packed[states:]
+    after_s, after_r = jnp.zeros_like(block_s), jnp.zeros_like(block_r)
     bit = 1
     while bit < size:
-        packed = jnp.concatenate([block_s, block_r], axis=0)
+        if bit > 1:
+            packed = jnp.concatenate([block_s, block_r], axis=0)
         got = lax.ppermute(packed, "ctx", [(q, q ^ bit) for q in range(size)])
         got_s, got_r = got[:states], got[states:]
         lower = (me // bit) % 2 == 0
@@ -159,8 +162,8 @@
     states = state_in.shape[1]
     in_b = jnp.broadcast_to(state_in[:, :, None], (rows, states, LANES))
     out_b = jnp.broadcast_to(state_out[:, :, None], (rows, states, LANES))
-    summary, total = shard_summary(scan_grad, step_size, out_b, decay_rate)
-    carried = carry_in(summary, total, decay_rate)
+    packed = shard_summary(scan_grad, step_size, out_b, decay_rate)
+    carried = carry_in(packed, decay_rate)
     scan_input_grad, b_part = shard_sweep(
         scan_grad, step_size, scan_input, in_b, out_b, decay_rate, skip_gain[None, :], carried
     )

time: 123 us -> 122 us (level)
  no operation moved by 1% of the time
where the time goes in v8:
time: 122 us
  starting transfers between devices  50.4 us (41%)
  blocking collectives  23.6 us (19%)
  Pallas kernels  20 us (16%)
  waiting for transfers between devices  14.9 us (12%)
  other arithmetic  6.1 us (5%)
  local copies, waits for them, and re-layouts  5.57 us (5%)
    ppermute x7, starting transfers between devices, carry_in(): got = lax.ppermute(packed, 'ctx', [(q, q ^ bit) for q in range(size)])  50.4 us
    all_to_all x1, blocking collectives, exchange_sum(): got = lax.all_to_all(pieces, axis, 0, 0, tiled=True)  23.6 us
    ppermute x7, waiting for transfers between devices, carry_in(): got = lax.ppermute(packed, 'ctx', [(q, q ^ bit) for q in range(size)])  14.9 us
    pallas_call x1, Pallas kernels, shard_sweep(): pl.pallas_call(sweep_kernel, out_shape=(jax.ShapeDtypeStruct((rows, chann...  13.1 us
    pallas_call x1, Pallas kernels, shard_summary(): pl.pallas_call(summary_kernel, out_shape=jax.ShapeDtypeStruct((states + 1...  6.95 us
  transfers between devices with their start and end apart: 7, of which 7 were waited for; matrix products, arithmetic and copies ran while one was open for 0% of the time, Pallas kernels for 0%

profile of v8, /device:TPU:1, one launch (start us, length us, event | category | flops | bytes accessed | tf_op | source)
XLA Modules:
  0.0 121.6 jit_solution(8551651183685170928)
XLA Ops:
  0.6 0.8 copy.17
  1.4 1.9 %broadcast_in_dim.9.outb_ref = f32[256,16,128]{2,1,0:T(8,128)} broadcast(f32[256,16]{1,0:T(8,128)S(1)} %copy.17), dimensions={0,1} | broadcast | bytes 2113536 | tf_op jit(solution)/shard_map/broadcast_in_dim | solution.py:164
  3.4 7.0 %shard_map.86 = f32[17,1024]{1,0:T(8,128)} custom-call(bf16[256,1024]{1,0:T(8,128)(2,1)} %g_ref.3, bf16[256,1024]{1,0:T(8,128)(2,1)} %s_ref.3, f32[256,16,128]{2,1,0:T(8,128)} %broadcast_in_dim.9.outb_ref, f32[16,1024]{1,0:T(8,128)} %a_ref.3), custom_call_target="tpu_custom_call" | custom-call | flops 25165824 | bytes 3145728 | tf_op jit(solution)/shard_map/pallas_call | solution.py:77
  10.3 4.2 %collective-permute-start = (f32[17,1024]{1,0:T(8,128)}, f32[17,1024]{1,0:T(8,128)S(1)}, u32[]{:S(2)}, u32[]{:S(2)}) collective-permute-start(f32[17,1024]{1,0:T(8,128)} %shard_map.86), channel_id=1, source_target_pairs={{0,8},{8,0},{16,24},{24,16},{32,40},{40,32},{48,56},{56,48},{64,72... | collective-permute-start | bytes 208904 | tf_op jit(solution)/shard_map/ppermute | solution.py:138
  14.5 2.2 %collective-permute-done = f32[17,1024]{1,0:T(8,128)S(1)} collective-permute-done((f32[17,1024]{1,0:T(8,128)}, f32[17,1024]{1,0:T(8,128)S(1)}, u32[]{:S(2)}, u32[]{:S(2)}) %collective-permute-start) | collective-permute-done | bytes 69664 | tf_op jit(solution)/shard_map/ppermute | solution.py:138
  16.7 0.8 broadcast_select_fusion.10
  17.5 0.9 multiply_add_fusion.5
  18.3 4.4 %collective-permute-start.1 = (f32[17,1024]{1,0:T(8,128)S(1)}, f32[17,1024]{1,0:T(8,128)S(1)}, u32[]{:S(2)}, u32[]{:S(2)}) collective-permute-start(f32[17,1024]{1,0:T(8,128)S(1)} %pad_maximum_fusion), channel_id=1, source_target_pairs={{0,16},{8,24},{16,0},{24,8},{32,48},{40,56},{48,32},{56,40},{64,80... | collective-permute-start | bytes 208904 | tf_op jit(solution)/shard_map/ppermute | solution.py:138
  22.8 2.0 %collective-permute-done.1 = f32[17,1024]{1,0:T(8,128)S(1)} collective-permute-done((f32[17,1024]{1,0:T(8,128)S(1)}, f32[17,1024]{1,0:T(8,128)S(1)}, u32[]{:S(2)}, u32[]{:S(2)}) %collective-permute-start.1) | collective-permute-done | bytes 69664 | tf_op jit(solution)/shard_map/ppermute | solution.py:138
  24.8 8.6 %collective-permute-start.2 = (f32[17,1024]{1,0:T(8,128)S(1)}, f32[17,1024]{1,0:T(8,128)S(1)}, u32[]{:S(2)}, u32[]{:S(2)}) collective-permute-start(f32[17,1024]{1,0:T(8,128)S(1)} %pad_maximum_fusion.1), channel_id=1, source_target_pairs={{0,32},{8,40},{16,48},{24,56},{32,0},{40,8},{48,16},{56,24},{64,96... | collective-permute-start | bytes 208904 | tf_op jit(solution)/shard_map/ppermute | solution.py:138
  33.4 2.1 %collective-permute-done.2 = f32[17,1024]{1,0:T(8,128)S(1)} collective-permute-done((f32[17,1024]{1,0:T(8,128)S(1)}, f32[17,1024]{1,0:T(8,128)S(1)}, u32[]{:S(2)}, u32[]{:S(2)}) %collective-permute-start.2) | collective-permute-done | bytes 69664 | tf_op jit(solution)/shard_map/ppermute | solution.py:138
  35.5 4.0 %collective-permute-start.3 = (f32[17,1024]{1,0:T(8,128)S(1)}, f32[17,1024]{1,0:T(8,128)S(1)}, u32[]{:S(2)}, u32[]{:S(2)}) collective-permute-start(f32[17,1024]{1,0:T(8,128)S(1)} %pad_maximum_fusion.2), channel_id=1, source_target_pairs={{0,64},{8,72},{16,80},{24,88},{32,96},{40,104},{48,112},{56,120},{... | collective-permute-start | bytes 208904 | tf_op jit(solution)/shard_map/ppermute | solution.py:138
  39.5 2.0 %collective-permute-done.3 = f32[17,1024]{1,0:T(8,128)S(1)} collective-permute-done((f32[17,1024]{1,0:T(8,128)S(1)}, f32[17,1024]{1,0:T(8,128)S(1)}, u32[]{:S(2)}, u32[]{:S(2)}) %collective-permute-start.3) | collective-permute-done | bytes 69664 | tf_op jit(solution)/shard_map/ppermute | solution.py:138
  41.5 5.8 %collective-permute-start.4 = (f32[17,1024]{1,0:T(8,128)S(1)}, f32[17,1024]{1,0:T(8,128)S(1)}, u32[]{:S(2)}, u32[]{:S(2)}) collective-permute-start(f32[17,1024]{1,0:T(8,128)S(1)} %pad_maximum_fusion.3), channel_id=1, source_target_pairs={{0,128},{8,136},{16,144},{24,152},{32,160},{40,168},{48,176},{56,1... | collective-permute-start | bytes 208904 | tf_op jit(solution)/shard_map/ppermute | solution.py:138
  47.4 2.3 %collective-permute-done.4 = f32[17,1024]{1,0:T(8,128)S(1)} collective-permute-done((f32[17,1024]{1,0:T(8,128)S(1)}, f32[17,1024]{1,0:T(8,128)S(1)}, u32[]{:S(2)}, u32[]{:S(2)}) %collective-permute-start.4) | collective-permute-done | bytes 69664 | tf_op jit(solution)/shard_map/ppermute | solution.py:138
  49.7 10.3 %collective-permute-start.5 = (f32[17,1024]{1,0:T(8,128)S(1)}, f32[17,1024]{1,0:T(8,128)S(1)}, u32[]{:S(2)}, u32[]{:S(2)}) collective-permute-start(f32[17,1024]{1,0:T(8,128)S(1)} %pad_maximum_fusion.4), channel_id=1, source_target_pairs={{0,256},{8,264},{16,272},{24,280},{32,288},{40,296},{48,304},{56,3... | collective-permute-start | bytes 208904 | tf_op jit(solution)/shard_map/ppermute | solution.py:138
  60.1 2.5 %collective-permute-done.5 = f32[17,1024]{1,0:T(8,128)S(1)} collective-permute-done((f32[17,1024]{1,0:T(8,128)S(1)}, f32[17,1024]{1,0:T(8,128)S(1)}, u32[]{:S(2)}, u32[]{:S(2)}) %collective-permute-start.5) | collective-permute-done | bytes 69664 | tf_op jit(solution)/shard_map/ppermute | solution.py:138
  62.7 13.2 %collective-permute-start.6 = (f32[17,1024]{1,0:T(8,128)S(1)}, f32[17,1024]{1,0:T(8,128)S(1)}, u32[]{:S(2)}, u32[]{:S(2)}) collective-permute-start(f32[17,1024]{1,0:T(8,128)S(1)} %pad_maximum_fusion.5), channel_id=1, source_target_pairs={{0,512},{8,520},{16,528},{24,536},{32,544},{40,552},{48,560},{56,5... | collective-permute-start | bytes 208904 | tf_op jit(solution)/shard_map/ppermute | solution.py:138
  76.0 2.0 %collective-permute-done.6 = f32[17,1024]{1,0:T(8,128)S(1)} collective-permute-done((f32[17,1024]{1,0:T(8,128)S(1)}, f32[17,1024]{1,0:T(8,128)S(1)}, u32[]{:S(2)}, u32[]{:S(2)}) %collective-permute-start.6) | collective-permute-done | bytes 69664 | tf_op jit(solution)/shard_map/ppermute | solution.py:138
  77.9 0.7 add_select_fusion.inc_ref
  78.7 2.0 %broadcast_in_dim.8.inb_ref = f32[256,16,128]{2,1,0:T(8,128)} broadcast(f32[256,16]{1,0:T(8,128)S(1)} %copy.16), dimensions={0,1} | broadcast | bytes 2113536 | tf_op jit(solution)/shard_map/broadcast_in_dim | solution.py:163
  80.6 13.1 %shard_map.87 = (bf16[256,1024]{1,0:T(8,128)(2,1)}, f32[256,16,128]{2,1,0:T(8,128)}) custom-call(bf16[256,1024]{1,0:T(8,128)(2,1)} %g_ref.3, bf16[256,1024]{1,0:T(8,128)(2,1)} %s_ref.3, bf16[256,1024]{1,0:T(8,128)(2,1)} %x_ref.1, f32[256,16,128]{2,1,0:T(8,128)} %broadcast_in_dim.8.inb_ref, f32[256,16,128]{2,1,0:T(8,128)} %broadcast_in_dim.9.outb_ref, ...), custom_call_target="tpu_custom_call" | custom-call | flops 50331648 | bytes 10485760 | tf_op jit(solution)/shard_map/pallas_call | solution.py:94
  93.7 2.2 %reduce_sum.18 = f32[256,16]{1,0:T(8,128)S(1)} reduce(f32[256,16,128]{2,1,0:T(8,128)} %get-tuple-element.5, f32[]{:T(128)} %constant.121.clone.1), dimensions={2}, to_apply=%region_0.1 | reduce | flops 520192 | bytes 2113540 | tf_op jit(solution)/shard_map/reduce_sum | solution.py:171
  96.1 23.6 %all_to_all.5 = f32[8,1,512]{2,1,0:T(1,128)S(1)} all-to-all(f32[8,1,512]{2,1,0:T(1,128)S(1)} %reshape.10), channel_id=1, replica_groups=mesh['ctx'=128,'exp'=8] {'exp'}, dimensions={0} | all-to-all | bytes 32768 | tf_op jit(solution)/shard_map/all_to_all | solution.py:156
  (28 shorter events, 2.4 us)
Async XLA Ops:
  3.4 14.1 %copy-start = (f32[16,1024]{1,0:T(8,128)S(1)}, f32[16,1024]{1,0:T(8,128)}, u32[]{:S(2)}) copy-start(f32[16,1024]{1,0:T(8,128)} %a_ref.3) | copy-start | bytes 196612
  10.3 65.5 %copy-start.1 = (f32[256,16]{0,1:T(8,128)S(1)}, f32[256,16]{0,1:T(8,128)}, u32[]{:S(2)}) copy-start(f32[256,16]{0,1:T(8,128)} %param.10) | copy-start | bytes 49156
  10.3 6.4 %collective-permute-start = (f32[17,1024]{1,0:T(8,128)}, f32[17,1024]{1,0:T(8,128)S(1)}, u32[]{:S(2)}, u32[]{:S(2)}) collective-permute-start(f32[17,1024]{1,0:T(8,128)} %shard_map.86), channel_id=1, source_target_pairs={{0,8},{8,0},{16,24},{24,16},{32,40},{40,32},{48,56},{56,48},{64,72... | collective-permute-start | bytes 208904 | tf_op jit(solution)/shard_map/ppermute | solution.py:138
  18.3 6.4 %collective-permute-start.1 = (f32[17,1024]{1,0:T(8,128)S(1)}, f32[17,1024]{1,0:T(8,128)S(1)}, u32[]{:S(2)}, u32[]{:S(2)}) collective-permute-start(f32[17,1024]{1,0:T(8,128)S(1)} %pad_maximum_fusion), channel_id=1, source_target_pairs={{0,16},{8,24},{16,0},{24,8},{32,48},{40,56},{48,32},{56,40},{64,80... | collective-permute-start | bytes 208904 | tf_op jit(solution)/shard_map/ppermute | solution.py:138
  24.8 10.7 %collective-permute-start.2 = (f32[17,1024]{1,0:T(8,128)S(1)}, f32[17,1024]{1,0:T(8,128)S(1)}, u32[]{:S(2)}, u32[]{:S(2)}) collective-permute-start(f32[17,1024]{1,0:T(8,128)S(1)} %pad_maximum_fusion.1), channel_id=1, source_target_pairs={{0,32},{8,40},{16,48},{24,56},{32,0},{40,8},{48,16},{56,24},{64,96... | collective-permute-start | bytes 208904 | tf_op jit(solution)/shard_map/ppermute | solution.py:138
  35.5 6.0 %collective-permute-start.3 = (f32[17,1024]{1,0:T(8,128)S(1)}, f32[17,1024]{1,0:T(8,128)S(1)}, u32[]{:S(2)}, u32[]{:S(2)}) collective-permute-start(f32[17,1024]{1,0:T(8,128)S(1)} %pad_maximum_fusion.2), channel_id=1, source_target_pairs={{0,64},{8,72},{16,80},{24,88},{32,96},{40,104},{48,112},{56,120},{... | collective-permute-start | bytes 208904 | tf_op jit(solution)/shard_map/ppermute | solution.py:138
  41.5 8.1 %collective-permute-start.4 = (f32[17,1024]{1,0:T(8,128)S(1)}, f32[17,1024]{1,0:T(8,128)S(1)}, u32[]{:S(2)}, u32[]{:S(2)}) collective-permute-start(f32[17,1024]{1,0:T(8,128)S(1)} %pad_maximum_fusion.3), channel_id=1, source_target_pairs={{0,128},{8,136},{16,144},{24,152},{32,160},{40,168},{48,176},{56,1... | collective-permute-start | bytes 208904 | tf_op jit(solution)/shard_map/ppermute | solution.py:138
  49.7 12.9 %collective-permute-start.5 = (f32[17,1024]{1,0:T(8,128)S(1)}, f32[17,1024]{1,0:T(8,128)S(1)}, u32[]{:S(2)}, u32[]{:S(2)}) collective-permute-start(f32[17,1024]{1,0:T(8,128)S(1)} %pad_maximum_fusion.4), channel_id=1, source_target_pairs={{0,256},{8,264},{16,272},{24,280},{32,288},{40,296},{48,304},{56,3... | collective-permute-start | bytes 208904 | tf_op jit(solution)/shard_map/ppermute | solution.py:138
  62.7 15.3 %collective-permute-start.6 = (f32[17,1024]{1,0:T(8,128)S(1)}, f32[17,1024]{1,0:T(8,128)S(1)}, u32[]{:S(2)}, u32[]{:S(2)}) collective-permute-start(f32[17,1024]{1,0:T(8,128)S(1)} %pad_maximum_fusion.5), channel_id=1, source_target_pairs={{0,512},{8,520},{16,528},{24,536},{32,544},{40,552},{48,560},{56,5... | collective-permute-start | bytes 208904 | tf_op jit(solution)/shard_map/ppermute | solution.py:138

commit v9 on v8

--- a/solution.py
+++ b/solution.py
@@ -38,32 +38,44 @@
 
 def sweep_kernel(
     g_ref, s_ref, x_ref, inb_ref, outb_ref, a_ref, skip_ref, inc_ref,
-    res_ref, bp_ref, gf, sf, wf, rf,
+    res_ref, bt_ref, gf, sf, wf, rf,
 ):
     rows, channels = g_ref.shape
+    states = a_ref.shape[0]
     tiles = channels // LANES
     gf[...] = g_ref[...].astype(jnp.float32)
     sf[...] = s_ref[...].astype(jnp.float32)
     wf[...] = sf[...] * x_ref[...].astype(jnp.float32)
     a = a_ref[...] * LOG2_E
     skip = skip_ref[...]
+    lane = lax.broadcasted_iota(jnp.int32, (states, LANES), 1)
 
-    def body(i, incoming):
-        t = rows - 1 - i
-        g_row = gf[pl.ds(t, 1), :]
-        s_row = sf[pl.ds(t, 1), :]
-        w_row = wf[pl.ds(t, 1), :]
-        adjoint = tiled(outb_ref[t], tiles) * g_row + incoming
-        mixed = jnp.sum(tiled(inb_ref[t], tiles) * adjoint, axis=0, keepdims=True)
-        rf[pl.ds(t, 1), :] = s_row * mixed + skip * g_row
-        weighted = adjoint * w_row
-        part = weighted[:, 0:LANES]
-        for k in range(1, tiles):
-            part = part + weighted[:, k * LANES:(k + 1) * LANES]
-        bp_ref[t] = part
-        return jnp.exp2(s_row * a) * adjoint
+    def run_block(base, incoming):
+        def body(i, carry):
+            incoming, gathered = carry
+            t = base + LANES - 1 - i
+            g_row = gf[pl.ds(t, 1), :]
+            s_row = sf[pl.ds(t, 1), :]
+            w_row = wf[pl.ds(t, 1), :]
+            adjoint = tiled(outb_ref[t], tiles) * g_row + incoming
+            mixed = jnp.sum(tiled(inb_ref[t], tiles) * adjoint, axis=0, keepdims=True)
+            rf[pl.ds(t, 1), :] = s_row * mixed + skip * g_row
+            weighted = adjoint * w_row
+            part = weighted[:, 0:LANES]
+            for k in range(1, tiles):
+                part = part + weighted[:, k * LANES:(k + 1) * LANES]
+            column = jnp.sum(part, axis=1, keepdims=True)
+            gathered = jnp.where(lane == LANES - 1 - i, column, gathered)
+            return (jnp.exp2(s_row * a) * adjoint, gathered)
 
-    lax.fori_loop(0, rows, body, inc_ref[...], unroll=8)
+        start = (incoming, jnp.zeros((states, LANES), jnp.float32))
+        incoming, gathered = lax.fori_loop(0, LANES, body, start, unroll=8)
+        bt_ref[:, base:base + LANES] = gathered
+        return incoming
+
+    incoming = inc_ref[...]
+    for block in range(rows // LANES - 1, -1, -1):
+        incoming = run_block(block * LANES, incoming)
     res_ref[...] = rf[...].astype(res_ref.dtype)
 
 
@@ -95,7 +107,7 @@
         sweep_kernel,
         out_shape=(
             jax.ShapeDtypeStruct((rows, channels), jnp.bfloat16),
-            jax.ShapeDtypeStruct((rows, states, LANES), jnp.float32),
+            jax.ShapeDtypeStruct((states, rows), jnp.float32),
         ),
         in_specs=[vmem_spec()] * 8,
         out_specs=(vmem_spec(), vmem_spec()),
@@ -164,11 +176,11 @@
     out_b = jnp.broadcast_to(state_out[:, :, None], (rows, states, LANES))
     packed = shard_summary(scan_grad, step_size, out_b, decay_rate)
     carried = carry_in(packed, decay_rate)
-    scan_input_grad, b_part = shard_sweep(
+    scan_input_grad, b_t = shard_sweep(
         scan_grad, step_size, scan_input, in_b, out_b, decay_rate, skip_gain[None, :], carried
     )
     all_channels = scan_grad.shape[1] * lax.axis_size("exp")
-    b_term = jnp.transpose(jnp.sum(b_part, axis=2)) * (1.0 / math.sqrt(all_channels))
+    b_term = b_t * (1.0 / math.sqrt(all_channels))
     state_in_grad = exchange_sum(b_term, "exp")
     return (scan_input_grad, state_in_grad)
 

time: 122 us -> 121 us (level)
  other arithmetic: 6.1 us -> 4.6 us
    reduce_sum x1 -> x0, other arithmetic: 2.21 us -> none  [shards(): jnp.sum(b_part, axis=2)]
where the time goes in v9:
time: 121 us; the launch traced here: 120 us
  starting transfers between devices  50.4 us (42%)
  blocking collectives  23.6 us (20%)
  Pallas kernels  20.3 us (17%)
  waiting for transfers between devices  14.9 us (12%)
  local copies, waits for them, and re-layouts  5.57 us (5%)
  other arithmetic  4.6 us (4%)
    ppermute x7, starting transfers between devices, carry_in(): got = lax.ppermute(packed, 'ctx', [(q, q ^ bit) for q in range(size)])  50.4 us
    all_to_all x1, blocking collectives, exchange_sum(): got = lax.all_to_all(pieces, axis, 0, 0, tiled=True)  23.6 us
    ppermute x7, waiting for transfers between devices, carry_in(): got = lax.ppermute(packed, 'ctx', [(q, q ^ bit) for q in range(size)])  14.9 us
    pallas_call x1, Pallas kernels, shard_sweep(): pl.pallas_call(sweep_kernel, out_shape=(jax.ShapeDtypeStruct((rows, chann...  13.3 us
    pallas_call x1, Pallas kernels, shard_summary(): pl.pallas_call(summary_kernel, out_shape=jax.ShapeDtypeStruct((states + 1...  6.95 us
  transfers between devices with their start and end apart: 7, of which 7 were waited for; matrix products, arithmetic and copies ran while one was open for 0% of the time, Pallas kernels for 0%

profile of v9, /device:TPU:1, one launch (start us, length us, event | category | flops | bytes accessed | tf_op | source)
XLA Modules:
  0.0 120.4 jit_solution(9870869013169396770)
XLA Ops:
  0.6 0.8 copy.12
  1.4 1.9 %broadcast_in_dim.9.outb_ref = f32[256,16,128]{2,1,0:T(8,128)} broadcast(f32[256,16]{1,0:T(8,128)S(1)} %copy.12), dimensions={0,1} | broadcast | bytes 2113536 | tf_op jit(solution)/shard_map/broadcast_in_dim | solution.py:176
  3.4 7.0 %shard_map.86 = f32[17,1024]{1,0:T(8,128)} custom-call(bf16[256,1024]{1,0:T(8,128)(2,1)} %g_ref.3, bf16[256,1024]{1,0:T(8,128)(2,1)} %s_ref.3, f32[256,16,128]{2,1,0:T(8,128)} %broadcast_in_dim.9.outb_ref, f32[16,1024]{1,0:T(8,128)} %a_ref.3), custom_call_target="tpu_custom_call" | custom-call | flops 25165824 | bytes 3145728 | tf_op jit(solution)/shard_map/pallas_call | solution.py:89
  10.3 4.2 %collective-permute-start = (f32[17,1024]{1,0:T(8,128)}, f32[17,1024]{1,0:T(8,128)S(1)}, u32[]{:S(2)}, u32[]{:S(2)}) collective-permute-start(f32[17,1024]{1,0:T(8,128)} %shard_map.86), channel_id=1, source_target_pairs={{0,8},{8,0},{16,24},{24,16},{32,40},{40,32},{48,56},{56,48},{64,72... | collective-permute-start | bytes 208904 | tf_op jit(solution)/shard_map/ppermute | solution.py:150
  14.5 2.2 %collective-permute-done = f32[17,1024]{1,0:T(8,128)S(1)} collective-permute-done((f32[17,1024]{1,0:T(8,128)}, f32[17,1024]{1,0:T(8,128)S(1)}, u32[]{:S(2)}, u32[]{:S(2)}) %collective-permute-start) | collective-permute-done | bytes 69664 | tf_op jit(solution)/shard_map/ppermute | solution.py:150
  16.7 0.8 broadcast_select_fusion.10
  17.5 0.9 multiply_add_fusion.5
  18.4 4.4 %collective-permute-start.1 = (f32[17,1024]{1,0:T(8,128)S(1)}, f32[17,1024]{1,0:T(8,128)S(1)}, u32[]{:S(2)}, u32[]{:S(2)}) collective-permute-start(f32[17,1024]{1,0:T(8,128)S(1)} %pad_maximum_fusion), channel_id=1, source_target_pairs={{0,16},{8,24},{16,0},{24,8},{32,48},{40,56},{48,32},{56,40},{64,80... | collective-permute-start | bytes 208904 | tf_op jit(solution)/shard_map/ppermute | solution.py:150
  22.8 2.0 %collective-permute-done.1 = f32[17,1024]{1,0:T(8,128)S(1)} collective-permute-done((f32[17,1024]{1,0:T(8,128)S(1)}, f32[17,1024]{1,0:T(8,128)S(1)}, u32[]{:S(2)}, u32[]{:S(2)}) %collective-permute-start.1) | collective-permute-done | bytes 69664 | tf_op jit(solution)/shard_map/ppermute | solution.py:150
  24.8 8.6 %collective-permute-start.2 = (f32[17,1024]{1,0:T(8,128)S(1)}, f32[17,1024]{1,0:T(8,128)S(1)}, u32[]{:S(2)}, u32[]{:S(2)}) collective-permute-start(f32[17,1024]{1,0:T(8,128)S(1)} %pad_maximum_fusion.1), channel_id=1, source_target_pairs={{0,32},{8,40},{16,48},{24,56},{32,0},{40,8},{48,16},{56,24},{64,96... | collective-permute-start | bytes 208904 | tf_op jit(solution)/shard_map/ppermute | solution.py:150
  33.4 2.1 %collective-permute-done.2 = f32[17,1024]{1,0:T(8,128)S(1)} collective-permute-done((f32[17,1024]{1,0:T(8,128)S(1)}, f32[17,1024]{1,0:T(8,128)S(1)}, u32[]{:S(2)}, u32[]{:S(2)}) %collective-permute-start.2) | collective-permute-done | bytes 69664 | tf_op jit(solution)/shard_map/ppermute | solution.py:150
  35.5 4.0 %collective-permute-start.3 = (f32[17,1024]{1,0:T(8,128)S(1)}, f32[17,1024]{1,0:T(8,128)S(1)}, u32[]{:S(2)}, u32[]{:S(2)}) collective-permute-start(f32[17,1024]{1,0:T(8,128)S(1)} %pad_maximum_fusion.2), channel_id=1, source_target_pairs={{0,64},{8,72},{16,80},{24,88},{32,96},{40,104},{48,112},{56,120},{... | collective-permute-start | bytes 208904 | tf_op jit(solution)/shard_map/ppermute | solution.py:150
  39.5 2.0 %collective-permute-done.3 = f32[17,1024]{1,0:T(8,128)S(1)} collective-permute-done((f32[17,1024]{1,0:T(8,128)S(1)}, f32[17,1024]{1,0:T(8,128)S(1)}, u32[]{:S(2)}, u32[]{:S(2)}) %collective-permute-start.3) | collective-permute-done | bytes 69664 | tf_op jit(solution)/shard_map/ppermute | solution.py:150
  41.5 5.8 %collective-permute-start.4 = (f32[17,1024]{1,0:T(8,128)S(1)}, f32[17,1024]{1,0:T(8,128)S(1)}, u32[]{:S(2)}, u32[]{:S(2)}) collective-permute-start(f32[17,1024]{1,0:T(8,128)S(1)} %pad_maximum_fusion.3), channel_id=1, source_target_pairs={{0,128},{8,136},{16,144},{24,152},{32,160},{40,168},{48,176},{56,1... | collective-permute-start | bytes 208904 | tf_op jit(solution)/shard_map/ppermute | solution.py:150
  47.4 2.3 %collective-permute-done.4 = f32[17,1024]{1,0:T(8,128)S(1)} collective-permute-done((f32[17,1024]{1,0:T(8,128)S(1)}, f32[17,1024]{1,0:T(8,128)S(1)}, u32[]{:S(2)}, u32[]{:S(2)}) %collective-permute-start.4) | collective-permute-done | bytes 69664 | tf_op jit(solution)/shard_map/ppermute | solution.py:150
  49.7 10.3 %collective-permute-start.5 = (f32[17,1024]{1,0:T(8,128)S(1)}, f32[17,1024]{1,0:T(8,128)S(1)}, u32[]{:S(2)}, u32[]{:S(2)}) collective-permute-start(f32[17,1024]{1,0:T(8,128)S(1)} %pad_maximum_fusion.4), channel_id=1, source_target_pairs={{0,256},{8,264},{16,272},{24,280},{32,288},{40,296},{48,304},{56,3... | collective-permute-start | bytes 208904 | tf_op jit(solution)/shard_map/ppermute | solution.py:150
  60.1 2.5 %collective-permute-done.5 = f32[17,1024]{1,0:T(8,128)S(1)} collective-permute-done((f32[17,1024]{1,0:T(8,128)S(1)}, f32[17,1024]{1,0:T(8,128)S(1)}, u32[]{:S(2)}, u32[]{:S(2)}) %collective-permute-start.5) | collective-permute-done | bytes 69664 | tf_op jit(solution)/shard_map/ppermute | solution.py:150
  62.7 13.2 %collective-permute-start.6 = (f32[17,1024]{1,0:T(8,128)S(1)}, f32[17,1024]{1,0:T(8,128)S(1)}, u32[]{:S(2)}, u32[]{:S(2)}) collective-permute-start(f32[17,1024]{1,0:T(8,128)S(1)} %pad_maximum_fusion.5), channel_id=1, source_target_pairs={{0,512},{8,520},{16,528},{24,536},{32,544},{40,552},{48,560},{56,5... | collective-permute-start | bytes 208904 | tf_op jit(solution)/shard_map/ppermute | solution.py:150
  76.0 2.0 %collective-permute-done.6 = f32[17,1024]{1,0:T(8,128)S(1)} collective-permute-done((f32[17,1024]{1,0:T(8,128)S(1)}, f32[17,1024]{1,0:T(8,128)S(1)}, u32[]{:S(2)}, u32[]{:S(2)}) %collective-permute-start.6) | collective-permute-done | bytes 69664 | tf_op jit(solution)/shard_map/ppermute | solution.py:150
  78.0 0.7 add_select_fusion.inc_ref
  78.7 1.9 %broadcast_in_dim.8.inb_ref = f32[256,16,128]{2,1,0:T(8,128)} broadcast(f32[256,16]{1,0:T(8,128)S(1)} %copy.11), dimensions={0,1} | broadcast | bytes 2113536 | tf_op jit(solution)/shard_map/broadcast_in_dim | solution.py:175
  80.6 13.3 %shard_map.87 = (bf16[256,1024]{1,0:T(8,128)(2,1)}, f32[16,256]{1,0:T(8,128)}) custom-call(bf16[256,1024]{1,0:T(8,128)(2,1)} %g_ref.3, bf16[256,1024]{1,0:T(8,128)(2,1)} %s_ref.3, bf16[256,1024]{1,0:T(8,128)(2,1)} %x_ref.1, f32[256,16,128]{2,1,0:T(8,128)} %broadcast_in_dim.8.inb_ref, f32[256,16,128]{2,1,0:T(8,128)} %broadcast_in_dim.9.outb_ref, ...), custom_call_target="tpu_custom_call" | custom-call | flops 50331648 | bytes 10485760 | tf_op jit(solution)/shard_map/pallas_call | solution.py:106
  94.0 0.7 broadcast_multiply_fusion
  94.9 23.6 %all_to_all.5 = f32[8,1,512]{2,1,0:T(1,128)S(1)} all-to-all(f32[8,1,512]{2,1,0:T(1,128)S(1)} %reshape.10), channel_id=1, replica_groups=mesh['ctx'=128,'exp'=8] {'exp'}, dimensions={0} | all-to-all | bytes 32768 | tf_op jit(solution)/shard_map/all_to_all | solution.py:168
  (28 shorter events, 2.4 us)
Async XLA Ops:
  3.4 14.1 %copy-start = (f32[16,1024]{1,0:T(8,128)S(1)}, f32[16,1024]{1,0:T(8,128)}, u32[]{:S(2)}) copy-start(f32[16,1024]{1,0:T(8,128)} %a_ref.3) | copy-start | bytes 196612
  10.3 65.5 %copy-start.1 = (f32[256,16]{0,1:T(8,128)S(1)}, f32[256,16]{0,1:T(8,128)}, u32[]{:S(2)}) copy-start(f32[256,16]{0,1:T(8,128)} %param.10) | copy-start | bytes 49156
  10.3 6.4 %collective-permute-start = (f32[17,1024]{1,0:T(8,128)}, f32[17,1024]{1,0:T(8,128)S(1)}, u32[]{:S(2)}, u32[]{:S(2)}) collective-permute-start(f32[17,1024]{1,0:T(8,128)} %shard_map.86), channel_id=1, source_target_pairs={{0,8},{8,0},{16,24},{24,16},{32,40},{40,32},{48,56},{56,48},{64,72... | collective-permute-start | bytes 208904 | tf_op jit(solution)/shard_map/ppermute | solution.py:150
  18.4 6.4 %collective-permute-start.1 = (f32[17,1024]{1,0:T(8,128)S(1)}, f32[17,1024]{1,0:T(8,128)S(1)}, u32[]{:S(2)}, u32[]{:S(2)}) collective-permute-start(f32[17,1024]{1,0:T(8,128)S(1)} %pad_maximum_fusion), channel_id=1, source_target_pairs={{0,16},{8,24},{16,0},{24,8},{32,48},{40,56},{48,32},{56,40},{64,80... | collective-permute-start | bytes 208904 | tf_op jit(solution)/shard_map/ppermute | solution.py:150
  24.8 10.7 %collective-permute-start.2 = (f32[17,1024]{1,0:T(8,128)S(1)}, f32[17,1024]{1,0:T(8,128)S(1)}, u32[]{:S(2)}, u32[]{:S(2)}) collective-permute-start(f32[17,1024]{1,0:T(8,128)S(1)} %pad_maximum_fusion.1), channel_id=1, source_target_pairs={{0,32},{8,40},{16,48},{24,56},{32,0},{40,8},{48,16},{56,24},{64,96... | collective-permute-start | bytes 208904 | tf_op jit(solution)/shard_map/ppermute | solution.py:150
  35.5 6.0 %collective-permute-start.3 = (f32[17,1024]{1,0:T(8,128)S(1)}, f32[17,1024]{1,0:T(8,128)S(1)}, u32[]{:S(2)}, u32[]{:S(2)}) collective-permute-start(f32[17,1024]{1,0:T(8,128)S(1)} %pad_maximum_fusion.2), channel_id=1, source_target_pairs={{0,64},{8,72},{16,80},{24,88},{32,96},{40,104},{48,112},{56,120},{... | collective-permute-start | bytes 208904 | tf_op jit(solution)/shard_map/ppermute | solution.py:150
  41.5 8.1 %collective-permute-start.4 = (f32[17,1024]{1,0:T(8,128)S(1)}, f32[17,1024]{1,0:T(8,128)S(1)}, u32[]{:S(2)}, u32[]{:S(2)}) collective-permute-start(f32[17,1024]{1,0:T(8,128)S(1)} %pad_maximum_fusion.3), channel_id=1, source_target_pairs={{0,128},{8,136},{16,144},{24,152},{32,160},{40,168},{48,176},{56,1... | collective-permute-start | bytes 208904 | tf_op jit(solution)/shard_map/ppermute | solution.py:150
  49.7 12.9 %collective-permute-start.5 = (f32[17,1024]{1,0:T(8,128)S(1)}, f32[17,1024]{1,0:T(8,128)S(1)}, u32[]{:S(2)}, u32[]{:S(2)}) collective-permute-start(f32[17,1024]{1,0:T(8,128)S(1)} %pad_maximum_fusion.4), channel_id=1, source_target_pairs={{0,256},{8,264},{16,272},{24,280},{32,288},{40,296},{48,304},{56,3... | collective-permute-start | bytes 208904 | tf_op jit(solution)/shard_map/ppermute | solution.py:150
  62.7 15.3 %collective-permute-start.6 = (f32[17,1024]{1,0:T(8,128)S(1)}, f32[17,1024]{1,0:T(8,128)S(1)}, u32[]{:S(2)}, u32[]{:S(2)}) collective-permute-start(f32[17,1024]{1,0:T(8,128)S(1)} %pad_maximum_fusion.5), channel_id=1, source_target_pairs={{0,512},{8,520},{16,528},{24,536},{32,544},{40,552},{48,560},{56,5... | collective-permute-start | bytes 208904 | tf_op jit(solution)/shard_map/ppermute | solution.py:150

commit v10 on v9

--- a/solution.py
+++ b/solution.py
@@ -15,29 +15,41 @@
     return jnp.concatenate([column_block] * tiles, axis=1)
 
 
-def summary_kernel(g_ref, s_ref, outb_ref, a_ref, out_ref, gf, sf):
+def lane_column(block, j, channels):
+    lane = lax.broadcasted_iota(jnp.int32, block.shape, 1)
+    column = jnp.sum(jnp.where(lane == j, block, 0.0), axis=1, keepdims=True)
+    return jnp.broadcast_to(column, (block.shape[0], channels))
+
+
+def summary_kernel(g_ref, s_ref, outt_ref, a_ref, out_ref, gf, sf):
     rows, channels = g_ref.shape
     states = a_ref.shape[0]
-    tiles = channels // LANES
     gf[...] = g_ref[...].astype(jnp.float32)
     sf[...] = s_ref[...].astype(jnp.float32)
     out_ref[states:, :] = jnp.sum(sf[...], axis=0, keepdims=True)
     a = a_ref[...] * LOG2_E
 
-    def body(i, incoming):
-        t = rows - 1 - i
-        g_row = gf[pl.ds(t, 1), :]
-        s_row = sf[pl.ds(t, 1), :]
-        adjoint = tiled(outb_ref[t], tiles) * g_row + incoming
-        return jnp.exp2(s_row * a) * adjoint
-
-    out_ref[0:states, :] = lax.fori_loop(
-        0, rows, body, jnp.zeros(a.shape, jnp.float32), unroll=8
-    )
+    def run_block(base, incoming):
+        out_block = outt_ref[:, base:base + LANES]
+
+        def body(i, incoming):
+            j = LANES - 1 - i
+            t = base + j
+            g_row = gf[pl.ds(t, 1), :]
+            s_row = sf[pl.ds(t, 1), :]
+            adjoint = lane_column(out_block, j, channels) * g_row + incoming
+            return jnp.exp2(s_row * a) * adjoint
+
+        return lax.fori_loop(0, LANES, body, incoming, unroll=8)
+
+    incoming = jnp.zeros(a.shape, jnp.float32)
+    for block in range(rows // LANES - 1, -1, -1):
+        incoming = run_block(block * LANES, incoming)
+    out_ref[0:states, :] = incoming
 
 
 def sweep_kernel(
-    g_ref, s_ref, x_ref, inb_ref, outb_ref, a_ref, skip_ref, inc_ref,
+    g_ref, s_ref, x_ref, int_ref, outt_ref, a_ref, skip_ref, inc_ref,
     res_ref, bt_ref, gf, sf, wf, rf,
 ):
     rows, channels = g_ref.shape
@@ -51,21 +63,25 @@
     lane = lax.broadcasted_iota(jnp.int32, (states, LANES), 1)
 
     def run_block(base, incoming):
+        in_block = int_ref[:, base:base + LANES]
+        out_block = outt_ref[:, base:base + LANES]
+
         def body(i, carry):
             incoming, gathered = carry
-            t = base + LANES - 1 - i
+            j = LANES - 1 - i
+            t = base + j
             g_row = gf[pl.ds(t, 1), :]
             s_row = sf[pl.ds(t, 1), :]
             w_row = wf[pl.ds(t, 1), :]
-            adjoint = tiled(outb_ref[t], tiles) * g_row + incoming
-            mixed = jnp.sum(tiled(inb_ref[t], tiles) * adjoint, axis=0, keepdims=True)
+            adjoint = lane_column(out_block, j, channels) * g_row + incoming
+            mixed = jnp.sum(lane_column(in_block, j, channels) * adjoint, axis=0, keepdims=True)
             rf[pl.ds(t, 1), :] = s_row * mixed + skip * g_row
             weighted = adjoint * w_row
             part = weighted[:, 0:LANES]
             for k in range(1, tiles):
                 part = part + weighted[:, k * LANES:(k + 1) * LANES]
             column = jnp.sum(part, axis=1, keepdims=True)
-            gathered = jnp.where(lane == LANES - 1 - i, column, gathered)
+            gathered = jnp.where(lane == j, column, gathered)
             return (jnp.exp2(s_row * a) * adjoint, gathered)
 
         start = (incoming, jnp.zeros((states, LANES), jnp.float32))
@@ -172,8 +188,8 @@
 def shards(scan_grad, step_size, scan_input, state_in, state_out, decay_rate, skip_gain):
     rows = scan_grad.shape[0]
     states = state_in.shape[1]
-    in_b = jnp.broadcast_to(state_in[:, :, None], (rows, states, LANES))
-    out_b = jnp.broadcast_to(state_out[:, :, None], (rows, states, LANES))
+    in_b = jnp.transpose(state_in)
+    out_b = jnp.transpose(state_out)
     packed = shard_summary(scan_grad, step_size, out_b, decay_rate)
     carried = carry_in(packed, decay_rate)
     scan_input_grad, b_t = shard_sweep(

time: 121 us -> 118 us (0.975)
  local copies, waits for them, and re-layouts: 5.57 us -> 0.78 us
  Pallas kernels: 20.3 us -> 21.7 us
    broadcast_in_dim x2 -> x0, local copies, waits for them, and re-layouts: 3.87 us -> none  [the longest x1 1.94 us: shards(): in_b = jnp.broadcast_to(state_in[:, :, None], (rows, states, LANES))]
    pallas_call x1, Pallas kernels: 13.3 us -> 14.6 us  [shard_sweep(): pl.pallas_call(sweep_kernel, out_shape=(jax.ShapeDtypeStruct((rows, chann...]
where the time goes in v10:
time: 118 us; the launch traced here: 117 us
  starting transfers between devices  50.2 us (43%)
  blocking collectives  23.6 us (20%)
  Pallas kernels  21.7 us (18%)
  waiting for transfers between devices  15 us (13%)
  other arithmetic  4.6 us (4%)
    ppermute x7, starting transfers between devices, carry_in(): got = lax.ppermute(packed, 'ctx', [(q, q ^ bit) for q in range(size)])  50.2 us
    all_to_all x1, blocking collectives, exchange_sum(): got = lax.all_to_all(pieces, axis, 0, 0, tiled=True)  23.6 us
    ppermute x7, waiting for transfers between devices, carry_in(): got = lax.ppermute(packed, 'ctx', [(q, q ^ bit) for q in range(size)])  15 us
    pallas_call x1, Pallas kernels, shard_sweep(): pl.pallas_call(sweep_kernel, out_shape=(jax.ShapeDtypeStruct((rows, chann...  14.6 us
    pallas_call x1, Pallas kernels, shard_summary(): pl.pallas_call(summary_kernel, out_shape=jax.ShapeDtypeStruct((states + 1...  7.13 us
  transfers between devices with their start and end apart: 7, of which 7 were waited for; matrix products, arithmetic and copies ran while one was open for 0% of the time, Pallas kernels for 0%

profile of v10, /device:TPU:1, one launch (start us, length us, event | category | flops | bytes accessed | tf_op | source)
XLA Modules:
  0.0 117.0 jit_solution(3359158273927414372)
XLA Ops:
  0.6 7.1 %shard_map.86 = f32[17,1024]{1,0:T(8,128)} custom-call(bf16[256,1024]{1,0:T(8,128)(2,1)} %g_ref.3, bf16[256,1024]{1,0:T(8,128)(2,1)} %s_ref.3, f32[16,256]{1,0:T(8,128)} %bitcast.32, f32[16,1024]{1,0:T(8,128)} %a_ref.3), custom_call_target="tpu_custom_call" | custom-call | flops 25165824 | bytes 1064960 | tf_op jit(solution)/shard_map/pallas_call | solution.py:105
  7.8 4.0 %collective-permute-start = (f32[17,1024]{1,0:T(8,128)}, f32[17,1024]{1,0:T(8,128)S(1)}, u32[]{:S(2)}, u32[]{:S(2)}) collective-permute-start(f32[17,1024]{1,0:T(8,128)} %shard_map.86), channel_id=1, source_target_pairs={{0,8},{8,0},{16,24},{24,16},{32,40},{40,32},{48,56},{56,48},{64,72... | collective-permute-start | bytes 208904 | tf_op jit(solution)/shard_map/ppermute | solution.py:166
  11.8 2.2 %collective-permute-done = f32[17,1024]{1,0:T(8,128)S(1)} collective-permute-done((f32[17,1024]{1,0:T(8,128)}, f32[17,1024]{1,0:T(8,128)S(1)}, u32[]{:S(2)}, u32[]{:S(2)}) %collective-permute-start) | collective-permute-done | bytes 69664 | tf_op jit(solution)/shard_map/ppermute | solution.py:166
  14.0 0.8 broadcast_select_fusion.10
  14.8 0.9 multiply_add_fusion.5
  15.7 4.4 %collective-permute-start.1 = (f32[17,1024]{1,0:T(8,128)S(1)}, f32[17,1024]{1,0:T(8,128)S(1)}, u32[]{:S(2)}, u32[]{:S(2)}) collective-permute-start(f32[17,1024]{1,0:T(8,128)S(1)} %pad_maximum_fusion), channel_id=1, source_target_pairs={{0,16},{8,24},{16,0},{24,8},{32,48},{40,56},{48,32},{56,40},{64,80... | collective-permute-start | bytes 208904 | tf_op jit(solution)/shard_map/ppermute | solution.py:166
  20.1 2.0 %collective-permute-done.1 = f32[17,1024]{1,0:T(8,128)S(1)} collective-permute-done((f32[17,1024]{1,0:T(8,128)S(1)}, f32[17,1024]{1,0:T(8,128)S(1)}, u32[]{:S(2)}, u32[]{:S(2)}) %collective-permute-start.1) | collective-permute-done | bytes 69664 | tf_op jit(solution)/shard_map/ppermute | solution.py:166
  22.1 8.6 %collective-permute-start.2 = (f32[17,1024]{1,0:T(8,128)S(1)}, f32[17,1024]{1,0:T(8,128)S(1)}, u32[]{:S(2)}, u32[]{:S(2)}) collective-permute-start(f32[17,1024]{1,0:T(8,128)S(1)} %pad_maximum_fusion.1), channel_id=1, source_target_pairs={{0,32},{8,40},{16,48},{24,56},{32,0},{40,8},{48,16},{56,24},{64,96... | collective-permute-start | bytes 208904 | tf_op jit(solution)/shard_map/ppermute | solution.py:166
  30.7 2.1 %collective-permute-done.2 = f32[17,1024]{1,0:T(8,128)S(1)} collective-permute-done((f32[17,1024]{1,0:T(8,128)S(1)}, f32[17,1024]{1,0:T(8,128)S(1)}, u32[]{:S(2)}, u32[]{:S(2)}) %collective-permute-start.2) | collective-permute-done | bytes 69664 | tf_op jit(solution)/shard_map/ppermute | solution.py:166
  32.8 4.0 %collective-permute-start.3 = (f32[17,1024]{1,0:T(8,128)S(1)}, f32[17,1024]{1,0:T(8,128)S(1)}, u32[]{:S(2)}, u32[]{:S(2)}) collective-permute-start(f32[17,1024]{1,0:T(8,128)S(1)} %pad_maximum_fusion.2), channel_id=1, source_target_pairs={{0,64},{8,72},{16,80},{24,88},{32,96},{40,104},{48,112},{56,120},{... | collective-permute-start | bytes 208904 | tf_op jit(solution)/shard_map/ppermute | solution.py:166
  36.8 2.0 %collective-permute-done.3 = f32[17,1024]{1,0:T(8,128)S(1)} collective-permute-done((f32[17,1024]{1,0:T(8,128)S(1)}, f32[17,1024]{1,0:T(8,128)S(1)}, u32[]{:S(2)}, u32[]{:S(2)}) %collective-permute-start.3) | collective-permute-done | bytes 69664 | tf_op jit(solution)/shard_map/ppermute | solution.py:166
  38.8 5.8 %collective-permute-start.4 = (f32[17,1024]{1,0:T(8,128)S(1)}, f32[17,1024]{1,0:T(8,128)S(1)}, u32[]{:S(2)}, u32[]{:S(2)}) collective-permute-start(f32[17,1024]{1,0:T(8,128)S(1)} %pad_maximum_fusion.3), channel_id=1, source_target_pairs={{0,128},{8,136},{16,144},{24,152},{32,160},{40,168},{48,176},{56,1... | collective-permute-start | bytes 208904 | tf_op jit(solution)/shard_map/ppermute | solution.py:166
  44.7 2.3 %collective-permute-done.4 = f32[17,1024]{1,0:T(8,128)S(1)} collective-permute-done((f32[17,1024]{1,0:T(8,128)S(1)}, f32[17,1024]{1,0:T(8,128)S(1)}, u32[]{:S(2)}, u32[]{:S(2)}) %collective-permute-start.4) | collective-permute-done | bytes 69664 | tf_op jit(solution)/shard_map/ppermute | solution.py:166
  47.0 10.3 %collective-permute-start.5 = (f32[17,1024]{1,0:T(8,128)S(1)}, f32[17,1024]{1,0:T(8,128)S(1)}, u32[]{:S(2)}, u32[]{:S(2)}) collective-permute-start(f32[17,1024]{1,0:T(8,128)S(1)} %pad_maximum_fusion.4), channel_id=1, source_target_pairs={{0,256},{8,264},{16,272},{24,280},{32,288},{40,296},{48,304},{56,3... | collective-permute-start | bytes 208904 | tf_op jit(solution)/shard_map/ppermute | solution.py:166
  57.4 2.5 %collective-permute-done.5 = f32[17,1024]{1,0:T(8,128)S(1)} collective-permute-done((f32[17,1024]{1,0:T(8,128)S(1)}, f32[17,1024]{1,0:T(8,128)S(1)}, u32[]{:S(2)}, u32[]{:S(2)}) %collective-permute-start.5) | collective-permute-done | bytes 69664 | tf_op jit(solution)/shard_map/ppermute | solution.py:166
  60.0 13.2 %collective-permute-start.6 = (f32[17,1024]{1,0:T(8,128)S(1)}, f32[17,1024]{1,0:T(8,128)S(1)}, u32[]{:S(2)}, u32[]{:S(2)}) collective-permute-start(f32[17,1024]{1,0:T(8,128)S(1)} %pad_maximum_fusion.5), channel_id=1, source_target_pairs={{0,512},{8,520},{16,528},{24,536},{32,544},{40,552},{48,560},{56,5... | collective-permute-start | bytes 208904 | tf_op jit(solution)/shard_map/ppermute | solution.py:166
  73.2 2.1 %collective-permute-done.6 = f32[17,1024]{1,0:T(8,128)S(1)} collective-permute-done((f32[17,1024]{1,0:T(8,128)S(1)}, f32[17,1024]{1,0:T(8,128)S(1)}, u32[]{:S(2)}, u32[]{:S(2)}) %collective-permute-start.6) | collective-permute-done | bytes 69664 | tf_op jit(solution)/shard_map/ppermute | solution.py:166
  75.3 0.7 add_select_fusion.inc_ref
  76.0 14.6 %shard_map.87 = (bf16[256,1024]{1,0:T(8,128)(2,1)}, f32[16,256]{1,0:T(8,128)}) custom-call(bf16[256,1024]{1,0:T(8,128)(2,1)} %g_ref.3, bf16[256,1024]{1,0:T(8,128)(2,1)} %s_ref.3, bf16[256,1024]{1,0:T(8,128)(2,1)} %x_ref.1, f32[16,256]{1,0:T(8,128)} %bitcast.31, f32[16,256]{1,0:T(8,128)} %bitcast.33, f32[16,1024]{1,0:T(8,128)} %a_ref.3, f32[1,1024]{1,0:T(1,128)} %bitcast.34, ...), custom_call_target="tpu_custom_call" | custom-call | flops 50331648 | bytes 2162688 | tf_op jit(solution)/shard_map/pallas_call | solution.py:122
  90.6 0.7 broadcast_multiply_fusion
  91.5 23.6 %all_to_all.5 = f32[8,1,512]{2,1,0:T(1,128)S(1)} all-to-all(f32[8,1,512]{2,1,0:T(1,128)S(1)} %reshape.8), channel_id=1, replica_groups=mesh['ctx'=128,'exp'=8] {'exp'}, dimensions={0} | all-to-all | bytes 32768 | tf_op jit(solution)/shard_map/all_to_all | solution.py:184
  115.1 0.5 broadcast.19
  115.6 0.7 reduce
  116.4 0.6 reduce_sum.9
  (22 shorter events, 0.5 us)
Async XLA Ops:
  0.6 14.1 %copy-start = (f32[16,1024]{1,0:T(8,128)S(1)}, f32[16,1024]{1,0:T(8,128)}, u32[]{:S(2)}) copy-start(f32[16,1024]{1,0:T(8,128)} %a_ref.3) | copy-start | bytes 196612
  7.8 6.2 %collective-permute-start = (f32[17,1024]{1,0:T(8,128)}, f32[17,1024]{1,0:T(8,128)S(1)}, u32[]{:S(2)}, u32[]{:S(2)}) collective-permute-start(f32[17,1024]{1,0:T(8,128)} %shard_map.86), channel_id=1, source_target_pairs={{0,8},{8,0},{16,24},{24,16},{32,40},{40,32},{48,56},{56,48},{64,72... | collective-permute-start | bytes 208904 | tf_op jit(solution)/shard_map/ppermute | solution.py:166
  15.7 6.4 %collective-permute-start.1 = (f32[17,1024]{1,0:T(8,128)S(1)}, f32[17,1024]{1,0:T(8,128)S(1)}, u32[]{:S(2)}, u32[]{:S(2)}) collective-permute-start(f32[17,1024]{1,0:T(8,128)S(1)} %pad_maximum_fusion), channel_id=1, source_target_pairs={{0,16},{8,24},{16,0},{24,8},{32,48},{40,56},{48,32},{56,40},{64,80... | collective-permute-start | bytes 208904 | tf_op jit(solution)/shard_map/ppermute | solution.py:166
  22.1 10.7 %collective-permute-start.2 = (f32[17,1024]{1,0:T(8,128)S(1)}, f32[17,1024]{1,0:T(8,128)S(1)}, u32[]{:S(2)}, u32[]{:S(2)}) collective-permute-start(f32[17,1024]{1,0:T(8,128)S(1)} %pad_maximum_fusion.1), channel_id=1, source_target_pairs={{0,32},{8,40},{16,48},{24,56},{32,0},{40,8},{48,16},{56,24},{64,96... | collective-permute-start | bytes 208904 | tf_op jit(solution)/shard_map/ppermute | solution.py:166
  32.8 6.0 %collective-permute-start.3 = (f32[17,1024]{1,0:T(8,128)S(1)}, f32[17,1024]{1,0:T(8,128)S(1)}, u32[]{:S(2)}, u32[]{:S(2)}) collective-permute-start(f32[17,1024]{1,0:T(8,128)S(1)} %pad_maximum_fusion.2), channel_id=1, source_target_pairs={{0,64},{8,72},{16,80},{24,88},{32,96},{40,104},{48,112},{56,120},{... | collective-permute-start | bytes 208904 | tf_op jit(solution)/shard_map/ppermute | solution.py:166
  38.8 8.1 %collective-permute-start.4 = (f32[17,1024]{1,0:T(8,128)S(1)}, f32[17,1024]{1,0:T(8,128)S(1)}, u32[]{:S(2)}, u32[]{:S(2)}) collective-permute-start(f32[17,1024]{1,0:T(8,128)S(1)} %pad_maximum_fusion.3), channel_id=1, source_target_pairs={{0,128},{8,136},{16,144},{24,152},{32,160},{40,168},{48,176},{56,1... | collective-permute-start | bytes 208904 | tf_op jit(solution)/shard_map/ppermute | solution.py:166
  47.0 12.9 %collective-permute-start.5 = (f32[17,1024]{1,0:T(8,128)S(1)}, f32[17,1024]{1,0:T(8,128)S(1)}, u32[]{:S(2)}, u32[]{:S(2)}) collective-permute-start(f32[17,1024]{1,0:T(8,128)S(1)} %pad_maximum_fusion.4), channel_id=1, source_target_pairs={{0,256},{8,264},{16,272},{24,280},{32,288},{40,296},{48,304},{56,3... | collective-permute-start | bytes 208904 | tf_op jit(solution)/shard_map/ppermute | solution.py:166
  60.0 15.3 %collective-permute-start.6 = (f32[17,1024]{1,0:T(8,128)S(1)}, f32[17,1024]{1,0:T(8,128)S(1)}, u32[]{:S(2)}, u32[]{:S(2)}) collective-permute-start(f32[17,1024]{1,0:T(8,128)S(1)} %pad_maximum_fusion.5), channel_id=1, source_target_pairs={{0,512},{8,520},{16,528},{24,536},{32,544},{40,552},{48,560},{56,5... | collective-permute-start | bytes 208904 | tf_op jit(solution)/shard_map/ppermute | solution.py:166

commit v11 on v10

--- a/solution.py
+++ b/solution.py
@@ -40,7 +40,7 @@
             adjoint = lane_column(out_block, j, channels) * g_row + incoming
             return jnp.exp2(s_row * a) * adjoint
 
-        return lax.fori_loop(0, LANES, body, incoming, unroll=8)
+        return lax.fori_loop(0, LANES, body, incoming, unroll=16)
 
     incoming = jnp.zeros(a.shape, jnp.float32)
     for block in range(rows // LANES - 1, -1, -1):
@@ -85,7 +85,7 @@
             return (jnp.exp2(s_row * a) * adjoint, gathered)
 
         start = (incoming, jnp.zeros((states, LANES), jnp.float32))
-        incoming, gathered = lax.fori_loop(0, LANES, body, start, unroll=8)
+        incoming, gathered = lax.fori_loop(0, LANES, body, start, unroll=16)
         bt_ref[:, base:base + LANES] = gathered
         return incoming
 

time: 118 us -> 115 us (0.975)
  Pallas kernels: 21.7 us -> 19.3 us
    pallas_call x1, Pallas kernels: 14.6 us -> 12.5 us  [shard_sweep(): pl.pallas_call(sweep_kernel, out_shape=(jax.ShapeDtypeStruct((rows, chann...]
where the time goes in v11:
time: 115 us
  starting transfers between devices  50.2 us (44%)
  blocking collectives  23.6 us (21%)
  Pallas kernels  19.3 us (17%)
  waiting for transfers between devices  15 us (13%)
  other arithmetic  4.6 us (4%)
    ppermute x7, starting transfers between devices, carry_in(): got = lax.ppermute(packed, 'ctx', [(q, q ^ bit) for q in range(size)])  50.2 us
    all_to_all x1, blocking collectives, exchange_sum(): got = lax.all_to_all(pieces, axis, 0, 0, tiled=True)  23.6 us
    ppermute x7, waiting for transfers between devices, carry_in(): got = lax.ppermute(packed, 'ctx', [(q, q ^ bit) for q in range(size)])  15 us
    pallas_call x1, Pallas kernels, shard_sweep(): pl.pallas_call(sweep_kernel, out_shape=(jax.ShapeDtypeStruct((rows, chann...  12.5 us
    pallas_call x1, Pallas kernels, shard_summary(): pl.pallas_call(summary_kernel, out_shape=jax.ShapeDtypeStruct((states + 1...  6.81 us
  transfers between devices with their start and end apart: 7, of which 7 were waited for; matrix products, arithmetic and copies ran while one was open for 0% of the time, Pallas kernels for 0%

profile of v11, /device:TPU:1, one launch (start us, length us, event | category | flops | bytes accessed | tf_op | source)
XLA Modules:
  0.0 114.6 jit_solution(10091259623303204288)
XLA Ops:
  0.6 6.8 %shard_map.86 = f32[17,1024]{1,0:T(8,128)} custom-call(bf16[256,1024]{1,0:T(8,128)(2,1)} %g_ref.3, bf16[256,1024]{1,0:T(8,128)(2,1)} %s_ref.3, f32[16,256]{1,0:T(8,128)} %bitcast.32, f32[16,1024]{1,0:T(8,128)} %a_ref.3), custom_call_target="tpu_custom_call" | custom-call | flops 25165824 | bytes 1064960 | tf_op jit(solution)/shard_map/pallas_call | solution.py:105
  7.5 4.0 %collective-permute-start = (f32[17,1024]{1,0:T(8,128)}, f32[17,1024]{1,0:T(8,128)S(1)}, u32[]{:S(2)}, u32[]{:S(2)}) collective-permute-start(f32[17,1024]{1,0:T(8,128)} %shard_map.86), channel_id=1, source_target_pairs={{0,8},{8,0},{16,24},{24,16},{32,40},{40,32},{48,56},{56,48},{64,72... | collective-permute-start | bytes 208904 | tf_op jit(solution)/shard_map/ppermute | solution.py:166
  11.5 2.2 %collective-permute-done = f32[17,1024]{1,0:T(8,128)S(1)} collective-permute-done((f32[17,1024]{1,0:T(8,128)}, f32[17,1024]{1,0:T(8,128)S(1)}, u32[]{:S(2)}, u32[]{:S(2)}) %collective-permute-start) | collective-permute-done | bytes 69664 | tf_op jit(solution)/shard_map/ppermute | solution.py:166
  13.7 0.8 broadcast_select_fusion.10
  14.5 0.9 multiply_add_fusion.5
  15.3 4.4 %collective-permute-start.1 = (f32[17,1024]{1,0:T(8,128)S(1)}, f32[17,1024]{1,0:T(8,128)S(1)}, u32[]{:S(2)}, u32[]{:S(2)}) collective-permute-start(f32[17,1024]{1,0:T(8,128)S(1)} %pad_maximum_fusion), channel_id=1, source_target_pairs={{0,16},{8,24},{16,0},{24,8},{32,48},{40,56},{48,32},{56,40},{64,80... | collective-permute-start | bytes 208904 | tf_op jit(solution)/shard_map/ppermute | solution.py:166
  19.8 2.0 %collective-permute-done.1 = f32[17,1024]{1,0:T(8,128)S(1)} collective-permute-done((f32[17,1024]{1,0:T(8,128)S(1)}, f32[17,1024]{1,0:T(8,128)S(1)}, u32[]{:S(2)}, u32[]{:S(2)}) %collective-permute-start.1) | collective-permute-done | bytes 69664 | tf_op jit(solution)/shard_map/ppermute | solution.py:166
  21.8 8.6 %collective-permute-start.2 = (f32[17,1024]{1,0:T(8,128)S(1)}, f32[17,1024]{1,0:T(8,128)S(1)}, u32[]{:S(2)}, u32[]{:S(2)}) collective-permute-start(f32[17,1024]{1,0:T(8,128)S(1)} %pad_maximum_fusion.1), channel_id=1, source_target_pairs={{0,32},{8,40},{16,48},{24,56},{32,0},{40,8},{48,16},{56,24},{64,96... | collective-permute-start | bytes 208904 | tf_op jit(solution)/shard_map/ppermute | solution.py:166
  30.4 2.1 %collective-permute-done.2 = f32[17,1024]{1,0:T(8,128)S(1)} collective-permute-done((f32[17,1024]{1,0:T(8,128)S(1)}, f32[17,1024]{1,0:T(8,128)S(1)}, u32[]{:S(2)}, u32[]{:S(2)}) %collective-permute-start.2) | collective-permute-done | bytes 69664 | tf_op jit(solution)/shard_map/ppermute | solution.py:166
  32.5 4.0 %collective-permute-start.3 = (f32[17,1024]{1,0:T(8,128)S(1)}, f32[17,1024]{1,0:T(8,128)S(1)}, u32[]{:S(2)}, u32[]{:S(2)}) collective-permute-start(f32[17,1024]{1,0:T(8,128)S(1)} %pad_maximum_fusion.2), channel_id=1, source_target_pairs={{0,64},{8,72},{16,80},{24,88},{32,96},{40,104},{48,112},{56,120},{... | collective-permute-start | bytes 208904 | tf_op jit(solution)/shard_map/ppermute | solution.py:166
  36.5 2.0 %collective-permute-done.3 = f32[17,1024]{1,0:T(8,128)S(1)} collective-permute-done((f32[17,1024]{1,0:T(8,128)S(1)}, f32[17,1024]{1,0:T(8,128)S(1)}, u32[]{:S(2)}, u32[]{:S(2)}) %collective-permute-start.3) | collective-permute-done | bytes 69664 | tf_op jit(solution)/shard_map/ppermute | solution.py:166
  38.5 5.8 %collective-permute-start.4 = (f32[17,1024]{1,0:T(8,128)S(1)}, f32[17,1024]{1,0:T(8,128)S(1)}, u32[]{:S(2)}, u32[]{:S(2)}) collective-permute-start(f32[17,1024]{1,0:T(8,128)S(1)} %pad_maximum_fusion.3), channel_id=1, source_target_pairs={{0,128},{8,136},{16,144},{24,152},{32,160},{40,168},{48,176},{56,1... | collective-permute-start | bytes 208904 | tf_op jit(solution)/shard_map/ppermute | solution.py:166
  44.4 2.3 %collective-permute-done.4 = f32[17,1024]{1,0:T(8,128)S(1)} collective-permute-done((f32[17,1024]{1,0:T(8,128)S(1)}, f32[17,1024]{1,0:T(8,128)S(1)}, u32[]{:S(2)}, u32[]{:S(2)}) %collective-permute-start.4) | collective-permute-done | bytes 69664 | tf_op jit(solution)/shard_map/ppermute | solution.py:166
  46.7 10.3 %collective-permute-start.5 = (f32[17,1024]{1,0:T(8,128)S(1)}, f32[17,1024]{1,0:T(8,128)S(1)}, u32[]{:S(2)}, u32[]{:S(2)}) collective-permute-start(f32[17,1024]{1,0:T(8,128)S(1)} %pad_maximum_fusion.4), channel_id=1, source_target_pairs={{0,256},{8,264},{16,272},{24,280},{32,288},{40,296},{48,304},{56,3... | collective-permute-start | bytes 208904 | tf_op jit(solution)/shard_map/ppermute | solution.py:166
  57.1 2.5 %collective-permute-done.5 = f32[17,1024]{1,0:T(8,128)S(1)} collective-permute-done((f32[17,1024]{1,0:T(8,128)S(1)}, f32[17,1024]{1,0:T(8,128)S(1)}, u32[]{:S(2)}, u32[]{:S(2)}) %collective-permute-start.5) | collective-permute-done | bytes 69664 | tf_op jit(solution)/shard_map/ppermute | solution.py:166
  59.7 13.2 %collective-permute-start.6 = (f32[17,1024]{1,0:T(8,128)S(1)}, f32[17,1024]{1,0:T(8,128)S(1)}, u32[]{:S(2)}, u32[]{:S(2)}) collective-permute-start(f32[17,1024]{1,0:T(8,128)S(1)} %pad_maximum_fusion.5), channel_id=1, source_target_pairs={{0,512},{8,520},{16,528},{24,536},{32,544},{40,552},{48,560},{56,5... | collective-permute-start | bytes 208904 | tf_op jit(solution)/shard_map/ppermute | solution.py:166
  72.8 2.1 %collective-permute-done.6 = f32[17,1024]{1,0:T(8,128)S(1)} collective-permute-done((f32[17,1024]{1,0:T(8,128)S(1)}, f32[17,1024]{1,0:T(8,128)S(1)}, u32[]{:S(2)}, u32[]{:S(2)}) %collective-permute-start.6) | collective-permute-done | bytes 69664 | tf_op jit(solution)/shard_map/ppermute | solution.py:166
  74.9 0.7 add_select_fusion.inc_ref
  75.7 12.5 %shard_map.87 = (bf16[256,1024]{1,0:T(8,128)(2,1)}, f32[16,256]{1,0:T(8,128)}) custom-call(bf16[256,1024]{1,0:T(8,128)(2,1)} %g_ref.3, bf16[256,1024]{1,0:T(8,128)(2,1)} %s_ref.3, bf16[256,1024]{1,0:T(8,128)(2,1)} %x_ref.1, f32[16,256]{1,0:T(8,128)} %bitcast.31, f32[16,256]{1,0:T(8,128)} %bitcast.33, f32[16,1024]{1,0:T(8,128)} %a_ref.3, f32[1,1024]{1,0:T(1,128)} %bitcast.34, ...), custom_call_target="tpu_custom_call" | custom-call | flops 50331648 | bytes 2162688 | tf_op jit(solution)/shard_map/pallas_call | solution.py:122
  88.2 0.7 broadcast_multiply_fusion
  89.1 23.6 %all_to_all.5 = f32[8,1,512]{2,1,0:T(1,128)S(1)} all-to-all(f32[8,1,512]{2,1,0:T(1,128)S(1)} %reshape.8), channel_id=1, replica_groups=mesh['ctx'=128,'exp'=8] {'exp'}, dimensions={0} | all-to-all | bytes 32768 | tf_op jit(solution)/shard_map/all_to_all | solution.py:184
  112.7 0.5 broadcast.19
  113.2 0.7 reduce
  114.0 0.6 reduce_sum.9
  (22 shorter events, 0.5 us)
Async XLA Ops:
  0.6 13.8 %copy-start = (f32[16,1024]{1,0:T(8,128)S(1)}, f32[16,1024]{1,0:T(8,128)}, u32[]{:S(2)}) copy-start(f32[16,1024]{1,0:T(8,128)} %a_ref.3) | copy-start | bytes 196612
  7.5 6.2 %collective-permute-start = (f32[17,1024]{1,0:T(8,128)}, f32[17,1024]{1,0:T(8,128)S(1)}, u32[]{:S(2)}, u32[]{:S(2)}) collective-permute-start(f32[17,1024]{1,0:T(8,128)} %shard_map.86), channel_id=1, source_target_pairs={{0,8},{8,0},{16,24},{24,16},{32,40},{40,32},{48,56},{56,48},{64,72... | collective-permute-start | bytes 208904 | tf_op jit(solution)/shard_map/ppermute | solution.py:166
  15.3 6.4 %collective-permute-start.1 = (f32[17,1024]{1,0:T(8,128)S(1)}, f32[17,1024]{1,0:T(8,128)S(1)}, u32[]{:S(2)}, u32[]{:S(2)}) collective-permute-start(f32[17,1024]{1,0:T(8,128)S(1)} %pad_maximum_fusion), channel_id=1, source_target_pairs={{0,16},{8,24},{16,0},{24,8},{32,48},{40,56},{48,32},{56,40},{64,80... | collective-permute-start | bytes 208904 | tf_op jit(solution)/shard_map/ppermute | solution.py:166
  21.8 10.7 %collective-permute-start.2 = (f32[17,1024]{1,0:T(8,128)S(1)}, f32[17,1024]{1,0:T(8,128)S(1)}, u32[]{:S(2)}, u32[]{:S(2)}) collective-permute-start(f32[17,1024]{1,0:T(8,128)S(1)} %pad_maximum_fusion.1), channel_id=1, source_target_pairs={{0,32},{8,40},{16,48},{24,56},{32,0},{40,8},{48,16},{56,24},{64,96... | collective-permute-start | bytes 208904 | tf_op jit(solution)/shard_map/ppermute | solution.py:166
  32.5 6.0 %collective-permute-start.3 = (f32[17,1024]{1,0:T(8,128)S(1)}, f32[17,1024]{1,0:T(8,128)S(1)}, u32[]{:S(2)}, u32[]{:S(2)}) collective-permute-start(f32[17,1024]{1,0:T(8,128)S(1)} %pad_maximum_fusion.2), channel_id=1, source_target_pairs={{0,64},{8,72},{16,80},{24,88},{32,96},{40,104},{48,112},{56,120},{... | collective-permute-start | bytes 208904 | tf_op jit(solution)/shard_map/ppermute | solution.py:166
  38.5 8.1 %collective-permute-start.4 = (f32[17,1024]{1,0:T(8,128)S(1)}, f32[17,1024]{1,0:T(8,128)S(1)}, u32[]{:S(2)}, u32[]{:S(2)}) collective-permute-start(f32[17,1024]{1,0:T(8,128)S(1)} %pad_maximum_fusion.3), channel_id=1, source_target_pairs={{0,128},{8,136},{16,144},{24,152},{32,160},{40,168},{48,176},{56,1... | collective-permute-start | bytes 208904 | tf_op jit(solution)/shard_map/ppermute | solution.py:166
  46.7 12.9 %collective-permute-start.5 = (f32[17,1024]{1,0:T(8,128)S(1)}, f32[17,1024]{1,0:T(8,128)S(1)}, u32[]{:S(2)}, u32[]{:S(2)}) collective-permute-start(f32[17,1024]{1,0:T(8,128)S(1)} %pad_maximum_fusion.4), channel_id=1, source_target_pairs={{0,256},{8,264},{16,272},{24,280},{32,288},{40,296},{48,304},{56,3... | collective-permute-start | bytes 208904 | tf_op jit(solution)/shard_map/ppermute | solution.py:166
  59.7 15.3 %collective-permute-start.6 = (f32[17,1024]{1,0:T(8,128)S(1)}, f32[17,1024]{1,0:T(8,128)S(1)}, u32[]{:S(2)}, u32[]{:S(2)}) collective-permute-start(f32[17,1024]{1,0:T(8,128)S(1)} %pad_maximum_fusion.5), channel_id=1, source_target_pairs={{0,512},{8,520},{16,528},{24,536},{32,544},{40,552},{48,560},{56,5... | collective-permute-start | bytes 208904 | tf_op jit(solution)/shard_map/ppermute | solution.py:166

commit v12 on v11

--- a/solution.py
+++ b/solution.py
@@ -40,7 +40,7 @@
             adjoint = lane_column(out_block, j, channels) * g_row + incoming
             return jnp.exp2(s_row * a) * adjoint
 
-        return lax.fori_loop(0, LANES, body, incoming, unroll=16)
+        return lax.fori_loop(0, LANES, body, incoming, unroll=32)
 
     incoming = jnp.zeros(a.shape, jnp.float32)
     for block in range(rows // LANES - 1, -1, -1):
@@ -85,7 +85,7 @@
             return (jnp.exp2(s_row * a) * adjoint, gathered)
 
         start = (incoming, jnp.zeros((states, LANES), jnp.float32))
-        incoming, gathered = lax.fori_loop(0, LANES, body, start, unroll=16)
+        incoming, gathered = lax.fori_loop(0, LANES, body, start, unroll=32)
         bt_ref[:, base:base + LANES] = gathered
         return incoming
 

time: 115 us -> 115 us (level)
  no operation moved by 1% of the time
where the time goes in v12:
time: 115 us; the launch traced here: 114 us
  starting transfers between devices  50.2 us (44%)
  blocking collectives  23.6 us (21%)
  Pallas kernels  19.1 us (17%)
  waiting for transfers between devices  15 us (13%)
  other arithmetic  4.6 us (4%)
    ppermute x7, starting transfers between devices, carry_in(): got = lax.ppermute(packed, 'ctx', [(q, q ^ bit) for q in range(size)])  50.2 us
    all_to_all x1, blocking collectives, exchange_sum(): got = lax.all_to_all(pieces, axis, 0, 0, tiled=True)  23.6 us
    ppermute x7, waiting for transfers between devices, carry_in(): got = lax.ppermute(packed, 'ctx', [(q, q ^ bit) for q in range(size)])  15 us
    pallas_call x1, Pallas kernels, shard_sweep(): pl.pallas_call(sweep_kernel, out_shape=(jax.ShapeDtypeStruct((rows, chann...  12.4 us
    pallas_call x1, Pallas kernels, shard_summary(): pl.pallas_call(summary_kernel, out_shape=jax.ShapeDtypeStruct((states + 1...  6.73 us
  transfers between devices with their start and end apart: 7, of which 7 were waited for; matrix products, arithmetic and copies ran while one was open for 0% of the time, Pallas kernels for 0%

profile of v12, /device:TPU:1, one launch (start us, length us, event | category | flops | bytes accessed | tf_op | source)
XLA Modules:
  0.0 114.4 jit_solution(1159448659225576235)
XLA Ops:
  0.6 6.7 %shard_map.86 = f32[17,1024]{1,0:T(8,128)} custom-call(bf16[256,1024]{1,0:T(8,128)(2,1)} %g_ref.3, bf16[256,1024]{1,0:T(8,128)(2,1)} %s_ref.3, f32[16,256]{1,0:T(8,128)} %bitcast.32, f32[16,1024]{1,0:T(8,128)} %a_ref.3), custom_call_target="tpu_custom_call" | custom-call | flops 25165824 | bytes 1064960 | tf_op jit(solution)/shard_map/pallas_call | solution.py:105
  7.4 4.0 %collective-permute-start = (f32[17,1024]{1,0:T(8,128)}, f32[17,1024]{1,0:T(8,128)S(1)}, u32[]{:S(2)}, u32[]{:S(2)}) collective-permute-start(f32[17,1024]{1,0:T(8,128)} %shard_map.86), channel_id=1, source_target_pairs={{0,8},{8,0},{16,24},{24,16},{32,40},{40,32},{48,56},{56,48},{64,72... | collective-permute-start | bytes 208904 | tf_op jit(solution)/shard_map/ppermute | solution.py:166
  11.4 2.2 %collective-permute-done = f32[17,1024]{1,0:T(8,128)S(1)} collective-permute-done((f32[17,1024]{1,0:T(8,128)}, f32[17,1024]{1,0:T(8,128)S(1)}, u32[]{:S(2)}, u32[]{:S(2)}) %collective-permute-start) | collective-permute-done | bytes 69664 | tf_op jit(solution)/shard_map/ppermute | solution.py:166
  13.6 0.8 broadcast_select_fusion.10
  14.4 0.9 multiply_add_fusion.5
  15.3 4.4 %collective-permute-start.1 = (f32[17,1024]{1,0:T(8,128)S(1)}, f32[17,1024]{1,0:T(8,128)S(1)}, u32[]{:S(2)}, u32[]{:S(2)}) collective-permute-start(f32[17,1024]{1,0:T(8,128)S(1)} %pad_maximum_fusion), channel_id=1, source_target_pairs={{0,16},{8,24},{16,0},{24,8},{32,48},{40,56},{48,32},{56,40},{64,80... | collective-permute-start | bytes 208904 | tf_op jit(solution)/shard_map/ppermute | solution.py:166
  19.7 2.0 %collective-permute-done.1 = f32[17,1024]{1,0:T(8,128)S(1)} collective-permute-done((f32[17,1024]{1,0:T(8,128)S(1)}, f32[17,1024]{1,0:T(8,128)S(1)}, u32[]{:S(2)}, u32[]{:S(2)}) %collective-permute-start.1) | collective-permute-done | bytes 69664 | tf_op jit(solution)/shard_map/ppermute | solution.py:166
  21.7 8.6 %collective-permute-start.2 = (f32[17,1024]{1,0:T(8,128)S(1)}, f32[17,1024]{1,0:T(8,128)S(1)}, u32[]{:S(2)}, u32[]{:S(2)}) collective-permute-start(f32[17,1024]{1,0:T(8,128)S(1)} %pad_maximum_fusion.1), channel_id=1, source_target_pairs={{0,32},{8,40},{16,48},{24,56},{32,0},{40,8},{48,16},{56,24},{64,96... | collective-permute-start | bytes 208904 | tf_op jit(solution)/shard_map/ppermute | solution.py:166
  30.3 2.1 %collective-permute-done.2 = f32[17,1024]{1,0:T(8,128)S(1)} collective-permute-done((f32[17,1024]{1,0:T(8,128)S(1)}, f32[17,1024]{1,0:T(8,128)S(1)}, u32[]{:S(2)}, u32[]{:S(2)}) %collective-permute-start.2) | collective-permute-done | bytes 69664 | tf_op jit(solution)/shard_map/ppermute | solution.py:166
  32.4 4.0 %collective-permute-start.3 = (f32[17,1024]{1,0:T(8,128)S(1)}, f32[17,1024]{1,0:T(8,128)S(1)}, u32[]{:S(2)}, u32[]{:S(2)}) collective-permute-start(f32[17,1024]{1,0:T(8,128)S(1)} %pad_maximum_fusion.2), channel_id=1, source_target_pairs={{0,64},{8,72},{16,80},{24,88},{32,96},{40,104},{48,112},{56,120},{... | collective-permute-start | bytes 208904 | tf_op jit(solution)/shard_map/ppermute | solution.py:166
  36.4 2.0 %collective-permute-done.3 = f32[17,1024]{1,0:T(8,128)S(1)} collective-permute-done((f32[17,1024]{1,0:T(8,128)S(1)}, f32[17,1024]{1,0:T(8,128)S(1)}, u32[]{:S(2)}, u32[]{:S(2)}) %collective-permute-start.3) | collective-permute-done | bytes 69664 | tf_op jit(solution)/shard_map/ppermute | solution.py:166
  38.4 5.8 %collective-permute-start.4 = (f32[17,1024]{1,0:T(8,128)S(1)}, f32[17,1024]{1,0:T(8,128)S(1)}, u32[]{:S(2)}, u32[]{:S(2)}) collective-permute-start(f32[17,1024]{1,0:T(8,128)S(1)} %pad_maximum_fusion.3), channel_id=1, source_target_pairs={{0,128},{8,136},{16,144},{24,152},{32,160},{40,168},{48,176},{56,1... | collective-permute-start | bytes 208904 | tf_op jit(solution)/shard_map/ppermute | solution.py:166
  44.3 2.3 %collective-permute-done.4 = f32[17,1024]{1,0:T(8,128)S(1)} collective-permute-done((f32[17,1024]{1,0:T(8,128)S(1)}, f32[17,1024]{1,0:T(8,128)S(1)}, u32[]{:S(2)}, u32[]{:S(2)}) %collective-permute-start.4) | collective-permute-done | bytes 69664 | tf_op jit(solution)/shard_map/ppermute | solution.py:166
  46.6 10.3 %collective-permute-start.5 = (f32[17,1024]{1,0:T(8,128)S(1)}, f32[17,1024]{1,0:T(8,128)S(1)}, u32[]{:S(2)}, u32[]{:S(2)}) collective-permute-start(f32[17,1024]{1,0:T(8,128)S(1)} %pad_maximum_fusion.4), channel_id=1, source_target_pairs={{0,256},{8,264},{16,272},{24,280},{32,288},{40,296},{48,304},{56,3... | collective-permute-start | bytes 208904 | tf_op jit(solution)/shard_map/ppermute | solution.py:166
  57.0 2.5 %collective-permute-done.5 = f32[17,1024]{1,0:T(8,128)S(1)} collective-permute-done((f32[17,1024]{1,0:T(8,128)S(1)}, f32[17,1024]{1,0:T(8,128)S(1)}, u32[]{:S(2)}, u32[]{:S(2)}) %collective-permute-start.5) | collective-permute-done | bytes 69664 | tf_op jit(solution)/shard_map/ppermute | solution.py:166
  59.6 13.2 %collective-permute-start.6 = (f32[17,1024]{1,0:T(8,128)S(1)}, f32[17,1024]{1,0:T(8,128)S(1)}, u32[]{:S(2)}, u32[]{:S(2)}) collective-permute-start(f32[17,1024]{1,0:T(8,128)S(1)} %pad_maximum_fusion.5), channel_id=1, source_target_pairs={{0,512},{8,520},{16,528},{24,536},{32,544},{40,552},{48,560},{56,5... | collective-permute-start | bytes 208904 | tf_op jit(solution)/shard_map/ppermute | solution.py:166
  72.8 2.1 %collective-permute-done.6 = f32[17,1024]{1,0:T(8,128)S(1)} collective-permute-done((f32[17,1024]{1,0:T(8,128)S(1)}, f32[17,1024]{1,0:T(8,128)S(1)}, u32[]{:S(2)}, u32[]{:S(2)}) %collective-permute-start.6) | collective-permute-done | bytes 69664 | tf_op jit(solution)/shard_map/ppermute | solution.py:166
  74.9 0.7 add_select_fusion.inc_ref
  75.6 12.4 %shard_map.87 = (bf16[256,1024]{1,0:T(8,128)(2,1)}, f32[16,256]{1,0:T(8,128)}) custom-call(bf16[256,1024]{1,0:T(8,128)(2,1)} %g_ref.3, bf16[256,1024]{1,0:T(8,128)(2,1)} %s_ref.3, bf16[256,1024]{1,0:T(8,128)(2,1)} %x_ref.1, f32[16,256]{1,0:T(8,128)} %bitcast.31, f32[16,256]{1,0:T(8,128)} %bitcast.33, f32[16,1024]{1,0:T(8,128)} %a_ref.3, f32[1,1024]{1,0:T(1,128)} %bitcast.34, ...), custom_call_target="tpu_custom_call" | custom-call | flops 50331648 | bytes 2162688 | tf_op jit(solution)/shard_map/pallas_call | solution.py:122
  88.0 0.7 broadcast_multiply_fusion
  88.9 23.6 %all_to_all.5 = f32[8,1,512]{2,1,0:T(1,128)S(1)} all-to-all(f32[8,1,512]{2,1,0:T(1,128)S(1)} %reshape.8), channel_id=1, replica_groups=mesh['ctx'=128,'exp'=8] {'exp'}, dimensions={0} | all-to-all | bytes 32768 | tf_op jit(solution)/shard_map/all_to_all | solution.py:184
  112.5 0.5 broadcast.19
  113.0 0.7 reduce
  113.8 0.6 reduce_sum.9
  (22 shorter events, 0.5 us)
Async XLA Ops:
  0.6 13.7 %copy-start = (f32[16,1024]{1,0:T(8,128)S(1)}, f32[16,1024]{1,0:T(8,128)}, u32[]{:S(2)}) copy-start(f32[16,1024]{1,0:T(8,128)} %a_ref.3) | copy-start | bytes 196612
  7.4 6.2 %collective-permute-start = (f32[17,1024]{1,0:T(8,128)}, f32[17,1024]{1,0:T(8,128)S(1)}, u32[]{:S(2)}, u32[]{:S(2)}) collective-permute-start(f32[17,1024]{1,0:T(8,128)} %shard_map.86), channel_id=1, source_target_pairs={{0,8},{8,0},{16,24},{24,16},{32,40},{40,32},{48,56},{56,48},{64,72... | collective-permute-start | bytes 208904 | tf_op jit(solution)/shard_map/ppermute | solution.py:166
  15.3 6.4 %collective-permute-start.1 = (f32[17,1024]{1,0:T(8,128)S(1)}, f32[17,1024]{1,0:T(8,128)S(1)}, u32[]{:S(2)}, u32[]{:S(2)}) collective-permute-start(f32[17,1024]{1,0:T(8,128)S(1)} %pad_maximum_fusion), channel_id=1, source_target_pairs={{0,16},{8,24},{16,0},{24,8},{32,48},{40,56},{48,32},{56,40},{64,80... | collective-permute-start | bytes 208904 | tf_op jit(solution)/shard_map/ppermute | solution.py:166
  21.7 10.7 %collective-permute-start.2 = (f32[17,1024]{1,0:T(8,128)S(1)}, f32[17,1024]{1,0:T(8,128)S(1)}, u32[]{:S(2)}, u32[]{:S(2)}) collective-permute-start(f32[17,1024]{1,0:T(8,128)S(1)} %pad_maximum_fusion.1), channel_id=1, source_target_pairs={{0,32},{8,40},{16,48},{24,56},{32,0},{40,8},{48,16},{56,24},{64,96... | collective-permute-start | bytes 208904 | tf_op jit(solution)/shard_map/ppermute | solution.py:166
  32.4 6.0 %collective-permute-start.3 = (f32[17,1024]{1,0:T(8,128)S(1)}, f32[17,1024]{1,0:T(8,128)S(1)}, u32[]{:S(2)}, u32[]{:S(2)}) collective-permute-start(f32[17,1024]{1,0:T(8,128)S(1)} %pad_maximum_fusion.2), channel_id=1, source_target_pairs={{0,64},{8,72},{16,80},{24,88},{32,96},{40,104},{48,112},{56,120},{... | collective-permute-start | bytes 208904 | tf_op jit(solution)/shard_map/ppermute | solution.py:166
  38.4 8.1 %collective-permute-start.4 = (f32[17,1024]{1,0:T(8,128)S(1)}, f32[17,1024]{1,0:T(8,128)S(1)}, u32[]{:S(2)}, u32[]{:S(2)}) collective-permute-start(f32[17,1024]{1,0:T(8,128)S(1)} %pad_maximum_fusion.3), channel_id=1, source_target_pairs={{0,128},{8,136},{16,144},{24,152},{32,160},{40,168},{48,176},{56,1... | collective-permute-start | bytes 208904 | tf_op jit(solution)/shard_map/ppermute | solution.py:166
  46.6 12.9 %collective-permute-start.5 = (f32[17,1024]{1,0:T(8,128)S(1)}, f32[17,1024]{1,0:T(8,128)S(1)}, u32[]{:S(2)}, u32[]{:S(2)}) collective-permute-start(f32[17,1024]{1,0:T(8,128)S(1)} %pad_maximum_fusion.4), channel_id=1, source_target_pairs={{0,256},{8,264},{16,272},{24,280},{32,288},{40,296},{48,304},{56,3... | collective-permute-start | bytes 208904 | tf_op jit(solution)/shard_map/ppermute | solution.py:166
  59.6 15.3 %collective-permute-start.6 = (f32[17,1024]{1,0:T(8,128)S(1)}, f32[17,1024]{1,0:T(8,128)S(1)}, u32[]{:S(2)}, u32[]{:S(2)}) collective-permute-start(f32[17,1024]{1,0:T(8,128)S(1)} %pad_maximum_fusion.5), channel_id=1, source_target_pairs={{0,512},{8,520},{16,528},{24,536},{32,544},{40,552},{48,560},{56,5... | collective-permute-start | bytes 208904 | tf_op jit(solution)/shard_map/ppermute | solution.py:166

commit v13 on v12

--- a/solution.py
+++ b/solution.py
@@ -1,3 +1,4 @@
+import functools
 import math
 
 import jax
@@ -50,7 +51,7 @@
 
 def sweep_kernel(
     g_ref, s_ref, x_ref, int_ref, outt_ref, a_ref, skip_ref, inc_ref,
-    res_ref, bt_ref, gf, sf, wf, rf,
+    res_ref, bt_ref, gf, sf, wf, rf, *, scale,
 ):
     rows, channels = g_ref.shape
     states = a_ref.shape[0]
@@ -86,7 +87,7 @@
 
         start = (incoming, jnp.zeros((states, LANES), jnp.float32))
         incoming, gathered = lax.fori_loop(0, LANES, body, start, unroll=32)
-        bt_ref[:, base:base + LANES] = gathered
+        bt_ref[:, base:base + LANES] = gathered * scale
         return incoming
 
     incoming = inc_ref[...]
@@ -116,11 +117,11 @@
     )(scan_grad, step_size, out_b, decay_rate)
 
 
-def shard_sweep(scan_grad, step_size, scan_input, in_b, out_b, decay_rate, skip_gain, incoming):
+def shard_sweep(scan_grad, step_size, scan_input, in_b, out_b, decay_rate, skip_gain, incoming, scale):
     rows, channels = scan_grad.shape
     states = decay_rate.shape[0]
     return pl.pallas_call(
-        sweep_kernel,
+        functools.partial(sweep_kernel, scale=scale),
         out_shape=(
             jax.ShapeDtypeStruct((rows, channels), jnp.bfloat16),
             jax.ShapeDtypeStruct((states, rows), jnp.float32),
@@ -193,10 +194,10 @@
     packed = shard_summary(scan_grad, step_size, out_b, decay_rate)
     carried = carry_in(packed, decay_rate)
     scan_input_grad, b_t = shard_sweep(
-        scan_grad, step_size, scan_input, in_b, out_b, decay_rate, skip_gain[None, :], carried
+        scan_grad, step_size, scan_input, in_b, out_b, decay_rate, skip_gain[None, :], carried,
+        1.0 / math.sqrt(scan_grad.shape[1] * lax.axis_size("exp")),
     )
-    all_channels = scan_grad.shape[1] * lax.axis_size("exp")
-    b_term = b_t * (1.0 / math.sqrt(all_channels))
+    b_term = b_t
     state_in_grad = exchange_sum(b_term, "exp")
     return (scan_input_grad, state_in_grad)
 

time: 115 us -> 115 us (level)
  no operation moved by 1% of the time
where the time goes in v13:
time: 115 us; the launch traced here: 114 us
  starting transfers between devices  50.2 us (44%)
  blocking collectives  23.6 us (21%)
  Pallas kernels  19.1 us (17%)
  waiting for transfers between devices  15 us (13%)
  other arithmetic  3.88 us (3%)
  local copies, waits for them, and re-layouts  1.5 us (1%)
    ppermute x7, starting transfers between devices, carry_in(): got = lax.ppermute(packed, 'ctx', [(q, q ^ bit) for q in range(size)])  50.2 us
    all_to_all x1, blocking collectives, exchange_sum(): got = lax.all_to_all(pieces, axis, 0, 0, tiled=True)  23.6 us
    ppermute x7, waiting for transfers between devices, carry_in(): got = lax.ppermute(packed, 'ctx', [(q, q ^ bit) for q in range(size)])  15 us
    pallas_call x1, Pallas kernels, shard_sweep(): pl.pallas_call(functools.partial(sweep_kernel, scale=scale), out_shape=(j...  12.4 us
    pallas_call x1, Pallas kernels, shard_summary(): pl.pallas_call(summary_kernel, out_shape=jax.ShapeDtypeStruct((states + 1...  6.73 us
  transfers between devices with their start and end apart: 7, of which 7 were waited for; matrix products, arithmetic and copies ran while one was open for 0% of the time, Pallas kernels for 0%

profile of v13, /device:TPU:1, one launch (start us, length us, event | category | flops | bytes accessed | tf_op | source)
XLA Modules:
  0.0 114.4 jit_solution(1212127487003864825)
XLA Ops:
  0.6 6.7 %shard_map.86 = f32[17,1024]{1,0:T(8,128)} custom-call(bf16[256,1024]{1,0:T(8,128)(2,1)} %g_ref.3, bf16[256,1024]{1,0:T(8,128)(2,1)} %s_ref.3, f32[16,256]{1,0:T(8,128)} %bitcast.32, f32[16,1024]{1,0:T(8,128)} %a_ref.3), custom_call_target="tpu_custom_call" | custom-call | flops 25165824 | bytes 1064960 | tf_op jit(solution)/shard_map/pallas_call | solution.py:106
  7.4 4.0 %collective-permute-start = (f32[17,1024]{1,0:T(8,128)}, f32[17,1024]{1,0:T(8,128)S(1)}, u32[]{:S(2)}, u32[]{:S(2)}) collective-permute-start(f32[17,1024]{1,0:T(8,128)} %shard_map.86), channel_id=1, source_target_pairs={{0,8},{8,0},{16,24},{24,16},{32,40},{40,32},{48,56},{56,48},{64,72... | collective-permute-start | bytes 208904 | tf_op jit(solution)/shard_map/ppermute | solution.py:167
  11.4 2.2 %collective-permute-done = f32[17,1024]{1,0:T(8,128)S(1)} collective-permute-done((f32[17,1024]{1,0:T(8,128)}, f32[17,1024]{1,0:T(8,128)S(1)}, u32[]{:S(2)}, u32[]{:S(2)}) %collective-permute-start) | collective-permute-done | bytes 69664 | tf_op jit(solution)/shard_map/ppermute | solution.py:167
  13.6 0.8 broadcast_select_fusion.10
  14.4 0.9 multiply_add_fusion.5
  15.3 4.4 %collective-permute-start.1 = (f32[17,1024]{1,0:T(8,128)S(1)}, f32[17,1024]{1,0:T(8,128)S(1)}, u32[]{:S(2)}, u32[]{:S(2)}) collective-permute-start(f32[17,1024]{1,0:T(8,128)S(1)} %pad_maximum_fusion), channel_id=1, source_target_pairs={{0,16},{8,24},{16,0},{24,8},{32,48},{40,56},{48,32},{56,40},{64,80... | collective-permute-start | bytes 208904 | tf_op jit(solution)/shard_map/ppermute | solution.py:167
  19.7 2.0 %collective-permute-done.1 = f32[17,1024]{1,0:T(8,128)S(1)} collective-permute-done((f32[17,1024]{1,0:T(8,128)S(1)}, f32[17,1024]{1,0:T(8,128)S(1)}, u32[]{:S(2)}, u32[]{:S(2)}) %collective-permute-start.1) | collective-permute-done | bytes 69664 | tf_op jit(solution)/shard_map/ppermute | solution.py:167
  21.7 8.6 %collective-permute-start.2 = (f32[17,1024]{1,0:T(8,128)S(1)}, f32[17,1024]{1,0:T(8,128)S(1)}, u32[]{:S(2)}, u32[]{:S(2)}) collective-permute-start(f32[17,1024]{1,0:T(8,128)S(1)} %pad_maximum_fusion.1), channel_id=1, source_target_pairs={{0,32},{8,40},{16,48},{24,56},{32,0},{40,8},{48,16},{56,24},{64,96... | collective-permute-start | bytes 208904 | tf_op jit(solution)/shard_map/ppermute | solution.py:167
  30.3 2.1 %collective-permute-done.2 = f32[17,1024]{1,0:T(8,128)S(1)} collective-permute-done((f32[17,1024]{1,0:T(8,128)S(1)}, f32[17,1024]{1,0:T(8,128)S(1)}, u32[]{:S(2)}, u32[]{:S(2)}) %collective-permute-start.2) | collective-permute-done | bytes 69664 | tf_op jit(solution)/shard_map/ppermute | solution.py:167
  32.4 4.0 %collective-permute-start.3 = (f32[17,1024]{1,0:T(8,128)S(1)}, f32[17,1024]{1,0:T(8,128)S(1)}, u32[]{:S(2)}, u32[]{:S(2)}) collective-permute-start(f32[17,1024]{1,0:T(8,128)S(1)} %pad_maximum_fusion.2), channel_id=1, source_target_pairs={{0,64},{8,72},{16,80},{24,88},{32,96},{40,104},{48,112},{56,120},{... | collective-permute-start | bytes 208904 | tf_op jit(solution)/shard_map/ppermute | solution.py:167
  36.4 2.0 %collective-permute-done.3 = f32[17,1024]{1,0:T(8,128)S(1)} collective-permute-done((f32[17,1024]{1,0:T(8,128)S(1)}, f32[17,1024]{1,0:T(8,128)S(1)}, u32[]{:S(2)}, u32[]{:S(2)}) %collective-permute-start.3) | collective-permute-done | bytes 69664 | tf_op jit(solution)/shard_map/ppermute | solution.py:167
  38.4 5.8 %collective-permute-start.4 = (f32[17,1024]{1,0:T(8,128)S(1)}, f32[17,1024]{1,0:T(8,128)S(1)}, u32[]{:S(2)}, u32[]{:S(2)}) collective-permute-start(f32[17,1024]{1,0:T(8,128)S(1)} %pad_maximum_fusion.3), channel_id=1, source_target_pairs={{0,128},{8,136},{16,144},{24,152},{32,160},{40,168},{48,176},{56,1... | collective-permute-start | bytes 208904 | tf_op jit(solution)/shard_map/ppermute | solution.py:167
  44.3 2.3 %collective-permute-done.4 = f32[17,1024]{1,0:T(8,128)S(1)} collective-permute-done((f32[17,1024]{1,0:T(8,128)S(1)}, f32[17,1024]{1,0:T(8,128)S(1)}, u32[]{:S(2)}, u32[]{:S(2)}) %collective-permute-start.4) | collective-permute-done | bytes 69664 | tf_op jit(solution)/shard_map/ppermute | solution.py:167
  46.6 10.3 %collective-permute-start.5 = (f32[17,1024]{1,0:T(8,128)S(1)}, f32[17,1024]{1,0:T(8,128)S(1)}, u32[]{:S(2)}, u32[]{:S(2)}) collective-permute-start(f32[17,1024]{1,0:T(8,128)S(1)} %pad_maximum_fusion.4), channel_id=1, source_target_pairs={{0,256},{8,264},{16,272},{24,280},{32,288},{40,296},{48,304},{56,3... | collective-permute-start | bytes 208904 | tf_op jit(solution)/shard_map/ppermute | solution.py:167
  57.0 2.5 %collective-permute-done.5 = f32[17,1024]{1,0:T(8,128)S(1)} collective-permute-done((f32[17,1024]{1,0:T(8,128)S(1)}, f32[17,1024]{1,0:T(8,128)S(1)}, u32[]{:S(2)}, u32[]{:S(2)}) %collective-permute-start.5) | collective-permute-done | bytes 69664 | tf_op jit(solution)/shard_map/ppermute | solution.py:167
  59.6 13.2 %collective-permute-start.6 = (f32[17,1024]{1,0:T(8,128)S(1)}, f32[17,1024]{1,0:T(8,128)S(1)}, u32[]{:S(2)}, u32[]{:S(2)}) collective-permute-start(f32[17,1024]{1,0:T(8,128)S(1)} %pad_maximum_fusion.5), channel_id=1, source_target_pairs={{0,512},{8,520},{16,528},{24,536},{32,544},{40,552},{48,560},{56,5... | collective-permute-start | bytes 208904 | tf_op jit(solution)/shard_map/ppermute | solution.py:167
  72.8 2.1 %collective-permute-done.6 = f32[17,1024]{1,0:T(8,128)S(1)} collective-permute-done((f32[17,1024]{1,0:T(8,128)S(1)}, f32[17,1024]{1,0:T(8,128)S(1)}, u32[]{:S(2)}, u32[]{:S(2)}) %collective-permute-start.6) | collective-permute-done | bytes 69664 | tf_op jit(solution)/shard_map/ppermute | solution.py:167
  74.9 0.7 add_select_fusion.inc_ref
  75.6 12.4 %shard_map.87 = (bf16[256,1024]{1,0:T(8,128)(2,1)}, f32[16,256]{1,0:T(8,128)}) custom-call(bf16[256,1024]{1,0:T(8,128)(2,1)} %g_ref.3, bf16[256,1024]{1,0:T(8,128)(2,1)} %s_ref.3, bf16[256,1024]{1,0:T(8,128)(2,1)} %x_ref.1, f32[16,256]{1,0:T(8,128)} %bitcast.31, f32[16,256]{1,0:T(8,128)} %bitcast.33, f32[16,1024]{1,0:T(8,128)} %a_ref.3, f32[1,1024]{1,0:T(1,128)} %bitcast.34, ...), custom_call_target="tpu_custom_call" | custom-call | flops 50331648 | bytes 2162688 | tf_op jit(solution)/shard_map/pallas_call | solution.py:123
  88.0 0.8 reshape.7
  88.9 23.6 %all_to_all.5 = f32[8,1,512]{2,1,0:T(1,128)S(1)} all-to-all(f32[8,1,512]{2,1,0:T(1,128)S(1)} %reshape.8), channel_id=1, replica_groups=mesh['ctx'=128,'exp'=8] {'exp'}, dimensions={0} | all-to-all | bytes 32768 | tf_op jit(solution)/shard_map/all_to_all | solution.py:185
  112.5 0.5 broadcast.19
  113.0 0.7 reduce
  113.8 0.6 reduce_sum.9
  (21 shorter events, 0.4 us)
Async XLA Ops:
  0.6 13.7 %copy-start = (f32[16,1024]{1,0:T(8,128)S(1)}, f32[16,1024]{1,0:T(8,128)}, u32[]{:S(2)}) copy-start(f32[16,1024]{1,0:T(8,128)} %a_ref.3) | copy-start | bytes 196612
  7.4 6.2 %collective-permute-start = (f32[17,1024]{1,0:T(8,128)}, f32[17,1024]{1,0:T(8,128)S(1)}, u32[]{:S(2)}, u32[]{:S(2)}) collective-permute-start(f32[17,1024]{1,0:T(8,128)} %shard_map.86), channel_id=1, source_target_pairs={{0,8},{8,0},{16,24},{24,16},{32,40},{40,32},{48,56},{56,48},{64,72... | collective-permute-start | bytes 208904 | tf_op jit(solution)/shard_map/ppermute | solution.py:167
  15.3 6.4 %collective-permute-start.1 = (f32[17,1024]{1,0:T(8,128)S(1)}, f32[17,1024]{1,0:T(8,128)S(1)}, u32[]{:S(2)}, u32[]{:S(2)}) collective-permute-start(f32[17,1024]{1,0:T(8,128)S(1)} %pad_maximum_fusion), channel_id=1, source_target_pairs={{0,16},{8,24},{16,0},{24,8},{32,48},{40,56},{48,32},{56,40},{64,80... | collective-permute-start | bytes 208904 | tf_op jit(solution)/shard_map/ppermute | solution.py:167
  21.7 10.7 %collective-permute-start.2 = (f32[17,1024]{1,0:T(8,128)S(1)}, f32[17,1024]{1,0:T(8,128)S(1)}, u32[]{:S(2)}, u32[]{:S(2)}) collective-permute-start(f32[17,1024]{1,0:T(8,128)S(1)} %pad_maximum_fusion.1), channel_id=1, source_target_pairs={{0,32},{8,40},{16,48},{24,56},{32,0},{40,8},{48,16},{56,24},{64,96... | collective-permute-start | bytes 208904 | tf_op jit(solution)/shard_map/ppermute | solution.py:167
  32.4 6.0 %collective-permute-start.3 = (f32[17,1024]{1,0:T(8,128)S(1)}, f32[17,1024]{1,0:T(8,128)S(1)}, u32[]{:S(2)}, u32[]{:S(2)}) collective-permute-start(f32[17,1024]{1,0:T(8,128)S(1)} %pad_maximum_fusion.2), channel_id=1, source_target_pairs={{0,64},{8,72},{16,80},{24,88},{32,96},{40,104},{48,112},{56,120},{... | collective-permute-start | bytes 208904 | tf_op jit(solution)/shard_map/ppermute | solution.py:167
  38.4 8.1 %collective-permute-start.4 = (f32[17,1024]{1,0:T(8,128)S(1)}, f32[17,1024]{1,0:T(8,128)S(1)}, u32[]{:S(2)}, u32[]{:S(2)}) collective-permute-start(f32[17,1024]{1,0:T(8,128)S(1)} %pad_maximum_fusion.3), channel_id=1, source_target_pairs={{0,128},{8,136},{16,144},{24,152},{32,160},{40,168},{48,176},{56,1... | collective-permute-start | bytes 208904 | tf_op jit(solution)/shard_map/ppermute | solution.py:167
  46.6 12.9 %collective-permute-start.5 = (f32[17,1024]{1,0:T(8,128)S(1)}, f32[17,1024]{1,0:T(8,128)S(1)}, u32[]{:S(2)}, u32[]{:S(2)}) collective-permute-start(f32[17,1024]{1,0:T(8,128)S(1)} %pad_maximum_fusion.4), channel_id=1, source_target_pairs={{0,256},{8,264},{16,272},{24,280},{32,288},{40,296},{48,304},{56,3... | collective-permute-start | bytes 208904 | tf_op jit(solution)/shard_map/ppermute | solution.py:167
  59.6 15.3 %collective-permute-start.6 = (f32[17,1024]{1,0:T(8,128)S(1)}, f32[17,1024]{1,0:T(8,128)S(1)}, u32[]{:S(2)}, u32[]{:S(2)}) collective-permute-start(f32[17,1024]{1,0:T(8,128)S(1)} %pad_maximum_fusion.5), channel_id=1, source_target_pairs={{0,512},{8,520},{16,528},{24,536},{32,544},{40,552},{48,560},{56,5... | collective-permute-start | bytes 208904 | tf_op jit(solution)/shard_map/ppermute | solution.py:167

commit v14 on v12

--- a/solution.py
+++ b/solution.py
@@ -166,8 +166,12 @@
         got = lax.ppermute(packed, "ctx", [(q, q ^ bit) for q in range(size)])
         got_s, got_r = got[:states], got[states:]
         lower = (me // bit) % 2 == 0
-        after_s = jnp.where(lower, after_s + jnp.exp(decay_rate * after_r) * got_s, after_s)
-        after_r = jnp.where(lower, after_r + got_r, after_r)
+        if bit == 1:
+            after_s = jnp.where(lower, got_s, after_s)
+            after_r = jnp.where(lower, got_r, after_r)
+        else:
+            after_s = jnp.where(lower, after_s + jnp.exp(decay_rate * after_r) * got_s, after_s)
+            after_r = jnp.where(lower, after_r + got_r, after_r)
         first_s = jnp.where(lower, block_s, got_s)
         first_r = jnp.where(lower, block_r, got_r)
         second_s = jnp.where(lower, got_s, block_s)

time: 115 us -> 115 us (level)
  no operation moved by 1% of the time
where the time goes in v14:
time: 115 us; the launch traced here: 114 us
  starting transfers between devices  50.2 us (44%)
  blocking collectives  23.6 us (21%)
  Pallas kernels  19.1 us (17%)
  waiting for transfers between devices  15 us (13%)
  other arithmetic  4.59 us (4%)
    ppermute x7, starting transfers between devices, carry_in(): got = lax.ppermute(packed, 'ctx', [(q, q ^ bit) for q in range(size)])  50.2 us
    all_to_all x1, blocking collectives, exchange_sum(): got = lax.all_to_all(pieces, axis, 0, 0, tiled=True)  23.6 us
    ppermute x7, waiting for transfers between devices, carry_in(): got = lax.ppermute(packed, 'ctx', [(q, q ^ bit) for q in range(size)])  15 us
    pallas_call x1, Pallas kernels, shard_sweep(): pl.pallas_call(sweep_kernel, out_shape=(jax.ShapeDtypeStruct((rows, chann...  12.4 us
    pallas_call x1, Pallas kernels, shard_summary(): pl.pallas_call(summary_kernel, out_shape=jax.ShapeDtypeStruct((states + 1...  6.73 us
  transfers between devices with their start and end apart: 7, of which 7 were waited for; matrix products, arithmetic and copies ran while one was open for 0% of the time, Pallas kernels for 0%

profile of v14, /device:TPU:1, one launch (start us, length us, event | category | flops | bytes accessed | tf_op | source)
XLA Modules:
  0.0 114.4 jit_solution(14162670465303674703)
XLA Ops:
  0.6 6.7 %shard_map.86 = f32[17,1024]{1,0:T(8,128)} custom-call(bf16[256,1024]{1,0:T(8,128)(2,1)} %g_ref.3, bf16[256,1024]{1,0:T(8,128)(2,1)} %s_ref.3, f32[16,256]{1,0:T(8,128)} %bitcast.32, f32[16,1024]{1,0:T(8,128)} %a_ref.3), custom_call_target="tpu_custom_call" | custom-call | flops 25165824 | bytes 1064960 | tf_op jit(solution)/shard_map/pallas_call | solution.py:105
  7.4 4.0 %collective-permute-start = (f32[17,1024]{1,0:T(8,128)}, f32[17,1024]{1,0:T(8,128)S(1)}, u32[]{:S(2)}, u32[]{:S(2)}) collective-permute-start(f32[17,1024]{1,0:T(8,128)} %shard_map.86), channel_id=1, source_target_pairs={{0,8},{8,0},{16,24},{24,16},{32,40},{40,32},{48,56},{56,48},{64,72... | collective-permute-start | bytes 208904 | tf_op jit(solution)/shard_map/ppermute | solution.py:166
  11.4 2.2 %collective-permute-done = f32[17,1024]{1,0:T(8,128)S(1)} collective-permute-done((f32[17,1024]{1,0:T(8,128)}, f32[17,1024]{1,0:T(8,128)S(1)}, u32[]{:S(2)}, u32[]{:S(2)}) %collective-permute-start) | collective-permute-done | bytes 69664 | tf_op jit(solution)/shard_map/ppermute | solution.py:166
  13.6 0.8 broadcast_select_fusion.10
  14.4 0.9 multiply_add_fusion.5
  15.3 4.4 %collective-permute-start.1 = (f32[17,1024]{1,0:T(8,128)S(1)}, f32[17,1024]{1,0:T(8,128)S(1)}, u32[]{:S(2)}, u32[]{:S(2)}) collective-permute-start(f32[17,1024]{1,0:T(8,128)S(1)} %pad_maximum_fusion), channel_id=1, source_target_pairs={{0,16},{8,24},{16,0},{24,8},{32,48},{40,56},{48,32},{56,40},{64,80... | collective-permute-start | bytes 208904 | tf_op jit(solution)/shard_map/ppermute | solution.py:166
  19.7 2.0 %collective-permute-done.1 = f32[17,1024]{1,0:T(8,128)S(1)} collective-permute-done((f32[17,1024]{1,0:T(8,128)S(1)}, f32[17,1024]{1,0:T(8,128)S(1)}, u32[]{:S(2)}, u32[]{:S(2)}) %collective-permute-start.1) | collective-permute-done | bytes 69664 | tf_op jit(solution)/shard_map/ppermute | solution.py:166
  21.7 8.6 %collective-permute-start.2 = (f32[17,1024]{1,0:T(8,128)S(1)}, f32[17,1024]{1,0:T(8,128)S(1)}, u32[]{:S(2)}, u32[]{:S(2)}) collective-permute-start(f32[17,1024]{1,0:T(8,128)S(1)} %pad_maximum_fusion.1), channel_id=1, source_target_pairs={{0,32},{8,40},{16,48},{24,56},{32,0},{40,8},{48,16},{56,24},{64,96... | collective-permute-start | bytes 208904 | tf_op jit(solution)/shard_map/ppermute | solution.py:166
  30.3 2.1 %collective-permute-done.2 = f32[17,1024]{1,0:T(8,128)S(1)} collective-permute-done((f32[17,1024]{1,0:T(8,128)S(1)}, f32[17,1024]{1,0:T(8,128)S(1)}, u32[]{:S(2)}, u32[]{:S(2)}) %collective-permute-start.2) | collective-permute-done | bytes 69664 | tf_op jit(solution)/shard_map/ppermute | solution.py:166
  32.4 4.0 %collective-permute-start.3 = (f32[17,1024]{1,0:T(8,128)S(1)}, f32[17,1024]{1,0:T(8,128)S(1)}, u32[]{:S(2)}, u32[]{:S(2)}) collective-permute-start(f32[17,1024]{1,0:T(8,128)S(1)} %pad_maximum_fusion.2), channel_id=1, source_target_pairs={{0,64},{8,72},{16,80},{24,88},{32,96},{40,104},{48,112},{56,120},{... | collective-permute-start | bytes 208904 | tf_op jit(solution)/shard_map/ppermute | solution.py:166
  36.4 2.0 %collective-permute-done.3 = f32[17,1024]{1,0:T(8,128)S(1)} collective-permute-done((f32[17,1024]{1,0:T(8,128)S(1)}, f32[17,1024]{1,0:T(8,128)S(1)}, u32[]{:S(2)}, u32[]{:S(2)}) %collective-permute-start.3) | collective-permute-done | bytes 69664 | tf_op jit(solution)/shard_map/ppermute | solution.py:166
  38.4 5.8 %collective-permute-start.4 = (f32[17,1024]{1,0:T(8,128)S(1)}, f32[17,1024]{1,0:T(8,128)S(1)}, u32[]{:S(2)}, u32[]{:S(2)}) collective-permute-start(f32[17,1024]{1,0:T(8,128)S(1)} %pad_maximum_fusion.3), channel_id=1, source_target_pairs={{0,128},{8,136},{16,144},{24,152},{32,160},{40,168},{48,176},{56,1... | collective-permute-start | bytes 208904 | tf_op jit(solution)/shard_map/ppermute | solution.py:166
  44.3 2.3 %collective-permute-done.4 = f32[17,1024]{1,0:T(8,128)S(1)} collective-permute-done((f32[17,1024]{1,0:T(8,128)S(1)}, f32[17,1024]{1,0:T(8,128)S(1)}, u32[]{:S(2)}, u32[]{:S(2)}) %collective-permute-start.4) | collective-permute-done | bytes 69664 | tf_op jit(solution)/shard_map/ppermute | solution.py:166
  46.6 10.3 %collective-permute-start.5 = (f32[17,1024]{1,0:T(8,128)S(1)}, f32[17,1024]{1,0:T(8,128)S(1)}, u32[]{:S(2)}, u32[]{:S(2)}) collective-permute-start(f32[17,1024]{1,0:T(8,128)S(1)} %pad_maximum_fusion.4), channel_id=1, source_target_pairs={{0,256},{8,264},{16,272},{24,280},{32,288},{40,296},{48,304},{56,3... | collective-permute-start | bytes 208904 | tf_op jit(solution)/shard_map/ppermute | solution.py:166
  57.0 2.5 %collective-permute-done.5 = f32[17,1024]{1,0:T(8,128)S(1)} collective-permute-done((f32[17,1024]{1,0:T(8,128)S(1)}, f32[17,1024]{1,0:T(8,128)S(1)}, u32[]{:S(2)}, u32[]{:S(2)}) %collective-permute-start.5) | collective-permute-done | bytes 69664 | tf_op jit(solution)/shard_map/ppermute | solution.py:166
  59.6 13.2 %collective-permute-start.6 = (f32[17,1024]{1,0:T(8,128)S(1)}, f32[17,1024]{1,0:T(8,128)S(1)}, u32[]{:S(2)}, u32[]{:S(2)}) collective-permute-start(f32[17,1024]{1,0:T(8,128)S(1)} %pad_maximum_fusion.5), channel_id=1, source_target_pairs={{0,512},{8,520},{16,528},{24,536},{32,544},{40,552},{48,560},{56,5... | collective-permute-start | bytes 208904 | tf_op jit(solution)/shard_map/ppermute | solution.py:166
  72.8 2.1 %collective-permute-done.6 = f32[17,1024]{1,0:T(8,128)S(1)} collective-permute-done((f32[17,1024]{1,0:T(8,128)S(1)}, f32[17,1024]{1,0:T(8,128)S(1)}, u32[]{:S(2)}, u32[]{:S(2)}) %collective-permute-start.6) | collective-permute-done | bytes 69664 | tf_op jit(solution)/shard_map/ppermute | solution.py:166
  74.9 0.7 add_select_fusion.inc_ref
  75.6 12.4 %shard_map.87 = (bf16[256,1024]{1,0:T(8,128)(2,1)}, f32[16,256]{1,0:T(8,128)}) custom-call(bf16[256,1024]{1,0:T(8,128)(2,1)} %g_ref.3, bf16[256,1024]{1,0:T(8,128)(2,1)} %s_ref.3, bf16[256,1024]{1,0:T(8,128)(2,1)} %x_ref.1, f32[16,256]{1,0:T(8,128)} %bitcast.31, f32[16,256]{1,0:T(8,128)} %bitcast.33, f32[16,1024]{1,0:T(8,128)} %a_ref.3, f32[1,1024]{1,0:T(1,128)} %bitcast.34, ...), custom_call_target="tpu_custom_call" | custom-call | flops 50331648 | bytes 2162688 | tf_op jit(solution)/shard_map/pallas_call | solution.py:122
  87.9 0.7 broadcast_multiply_fusion
  88.9 23.6 %all_to_all.5 = f32[8,1,512]{2,1,0:T(1,128)S(1)} all-to-all(f32[8,1,512]{2,1,0:T(1,128)S(1)} %reshape.8), channel_id=1, replica_groups=mesh['ctx'=128,'exp'=8] {'exp'}, dimensions={0} | all-to-all | bytes 32768 | tf_op jit(solution)/shard_map/all_to_all | solution.py:188
  112.5 0.5 broadcast.14
  113.0 0.7 reduce
  113.8 0.6 reduce_sum.9
  (22 shorter events, 0.5 us)
Async XLA Ops:
  0.6 13.7 %copy-start = (f32[16,1024]{1,0:T(8,128)S(1)}, f32[16,1024]{1,0:T(8,128)}, u32[]{:S(2)}) copy-start(f32[16,1024]{1,0:T(8,128)} %a_ref.3) | copy-start | bytes 196612
  7.4 6.2 %collective-permute-start = (f32[17,1024]{1,0:T(8,128)}, f32[17,1024]{1,0:T(8,128)S(1)}, u32[]{:S(2)}, u32[]{:S(2)}) collective-permute-start(f32[17,1024]{1,0:T(8,128)} %shard_map.86), channel_id=1, source_target_pairs={{0,8},{8,0},{16,24},{24,16},{32,40},{40,32},{48,56},{56,48},{64,72... | collective-permute-start | bytes 208904 | tf_op jit(solution)/shard_map/ppermute | solution.py:166
  15.3 6.4 %collective-permute-start.1 = (f32[17,1024]{1,0:T(8,128)S(1)}, f32[17,1024]{1,0:T(8,128)S(1)}, u32[]{:S(2)}, u32[]{:S(2)}) collective-permute-start(f32[17,1024]{1,0:T(8,128)S(1)} %pad_maximum_fusion), channel_id=1, source_target_pairs={{0,16},{8,24},{16,0},{24,8},{32,48},{40,56},{48,32},{56,40},{64,80... | collective-permute-start | bytes 208904 | tf_op jit(solution)/shard_map/ppermute | solution.py:166
  21.7 10.7 %collective-permute-start.2 = (f32[17,1024]{1,0:T(8,128)S(1)}, f32[17,1024]{1,0:T(8,128)S(1)}, u32[]{:S(2)}, u32[]{:S(2)}) collective-permute-start(f32[17,1024]{1,0:T(8,128)S(1)} %pad_maximum_fusion.1), channel_id=1, source_target_pairs={{0,32},{8,40},{16,48},{24,56},{32,0},{40,8},{48,16},{56,24},{64,96... | collective-permute-start | bytes 208904 | tf_op jit(solution)/shard_map/ppermute | solution.py:166
  32.4 6.0 %collective-permute-start.3 = (f32[17,1024]{1,0:T(8,128)S(1)}, f32[17,1024]{1,0:T(8,128)S(1)}, u32[]{:S(2)}, u32[]{:S(2)}) collective-permute-start(f32[17,1024]{1,0:T(8,128)S(1)} %pad_maximum_fusion.2), channel_id=1, source_target_pairs={{0,64},{8,72},{16,80},{24,88},{32,96},{40,104},{48,112},{56,120},{... | collective-permute-start | bytes 208904 | tf_op jit(solution)/shard_map/ppermute | solution.py:166
  38.4 8.1 %collective-permute-start.4 = (f32[17,1024]{1,0:T(8,128)S(1)}, f32[17,1024]{1,0:T(8,128)S(1)}, u32[]{:S(2)}, u32[]{:S(2)}) collective-permute-start(f32[17,1024]{1,0:T(8,128)S(1)} %pad_maximum_fusion.3), channel_id=1, source_target_pairs={{0,128},{8,136},{16,144},{24,152},{32,160},{40,168},{48,176},{56,1... | collective-permute-start | bytes 208904 | tf_op jit(solution)/shard_map/ppermute | solution.py:166
  46.6 12.9 %collective-permute-start.5 = (f32[17,1024]{1,0:T(8,128)S(1)}, f32[17,1024]{1,0:T(8,128)S(1)}, u32[]{:S(2)}, u32[]{:S(2)}) collective-permute-start(f32[17,1024]{1,0:T(8,128)S(1)} %pad_maximum_fusion.4), channel_id=1, source_target_pairs={{0,256},{8,264},{16,272},{24,280},{32,288},{40,296},{48,304},{56,3... | collective-permute-start | bytes 208904 | tf_op jit(solution)/shard_map/ppermute | solution.py:166
  59.6 15.3 %collective-permute-start.6 = (f32[17,1024]{1,0:T(8,128)S(1)}, f32[17,1024]{1,0:T(8,128)S(1)}, u32[]{:S(2)}, u32[]{:S(2)}) collective-permute-start(f32[17,1024]{1,0:T(8,128)S(1)} %pad_maximum_fusion.5), channel_id=1, source_target_pairs={{0,512},{8,520},{16,528},{24,536},{32,544},{40,552},{48,560},{56,5... | collective-permute-start | bytes 208904 | tf_op jit(solution)/shard_map/ppermute | solution.py:166

commit v15 on v14

--- a/solution.py
+++ b/solution.py
@@ -40,7 +40,7 @@
             adjoint = lane_column(out_block, j, channels) * g_row + incoming
             return jnp.exp2(s_row * a) * adjoint
 
-        return lax.fori_loop(0, LANES, body, incoming, unroll=32)
+        return lax.fori_loop(0, LANES, body, incoming, unroll=LANES)
 
     incoming = jnp.zeros(a.shape, jnp.float32)
     for block in range(rows // LANES - 1, -1, -1):

time: 115 us -> 114 us (level)
  no operation moved by 1% of the time
where the time goes in v15:
time: 114 us
  starting transfers between devices  50.2 us (44%)
  blocking collectives  23.6 us (21%)
  Pallas kernels  18.6 us (16%)
  waiting for transfers between devices  15 us (13%)
  other arithmetic  4.59 us (4%)
    ppermute x7, starting transfers between devices, carry_in(): got = lax.ppermute(packed, 'ctx', [(q, q ^ bit) for q in range(size)])  50.2 us
    all_to_all x1, blocking collectives, exchange_sum(): got = lax.all_to_all(pieces, axis, 0, 0, tiled=True)  23.6 us
    ppermute x7, waiting for transfers between devices, carry_in(): got = lax.ppermute(packed, 'ctx', [(q, q ^ bit) for q in range(size)])  15 us
    pallas_call x1, Pallas kernels, shard_sweep(): pl.pallas_call(sweep_kernel, out_shape=(jax.ShapeDtypeStruct((rows, chann...  12.4 us
    pallas_call x1, Pallas kernels, shard_summary(): pl.pallas_call(summary_kernel, out_shape=jax.ShapeDtypeStruct((states + 1...  6.27 us
  transfers between devices with their start and end apart: 7, of which 7 were waited for; matrix products, arithmetic and copies ran while one was open for 0% of the time, Pallas kernels for 0%

profile of v15, /device:TPU:1, one launch (start us, length us, event | category | flops | bytes accessed | tf_op | source)
XLA Modules:
  0.0 113.9 jit_solution(4291318464296792762)
XLA Ops:
  0.6 6.3 %shard_map.86 = f32[17,1024]{1,0:T(8,128)} custom-call(bf16[256,1024]{1,0:T(8,128)(2,1)} %g_ref.3, bf16[256,1024]{1,0:T(8,128)(2,1)} %s_ref.3, f32[16,256]{1,0:T(8,128)} %bitcast.32, f32[16,1024]{1,0:T(8,128)} %a_ref.3), custom_call_target="tpu_custom_call" | custom-call | flops 25165824 | bytes 1064960 | tf_op jit(solution)/shard_map/pallas_call | solution.py:105
  6.9 4.0 %collective-permute-start = (f32[17,1024]{1,0:T(8,128)}, f32[17,1024]{1,0:T(8,128)S(1)}, u32[]{:S(2)}, u32[]{:S(2)}) collective-permute-start(f32[17,1024]{1,0:T(8,128)} %shard_map.86), channel_id=1, source_target_pairs={{0,8},{8,0},{16,24},{24,16},{32,40},{40,32},{48,56},{56,48},{64,72... | collective-permute-start | bytes 208904 | tf_op jit(solution)/shard_map/ppermute | solution.py:166
  11.0 2.2 %collective-permute-done = f32[17,1024]{1,0:T(8,128)S(1)} collective-permute-done((f32[17,1024]{1,0:T(8,128)}, f32[17,1024]{1,0:T(8,128)S(1)}, u32[]{:S(2)}, u32[]{:S(2)}) %collective-permute-start) | collective-permute-done | bytes 69664 | tf_op jit(solution)/shard_map/ppermute | solution.py:166
  13.1 0.8 broadcast_select_fusion.10
  13.9 0.9 multiply_add_fusion.5
  14.8 4.4 %collective-permute-start.1 = (f32[17,1024]{1,0:T(8,128)S(1)}, f32[17,1024]{1,0:T(8,128)S(1)}, u32[]{:S(2)}, u32[]{:S(2)}) collective-permute-start(f32[17,1024]{1,0:T(8,128)S(1)} %pad_maximum_fusion), channel_id=1, source_target_pairs={{0,16},{8,24},{16,0},{24,8},{32,48},{40,56},{48,32},{56,40},{64,80... | collective-permute-start | bytes 208904 | tf_op jit(solution)/shard_map/ppermute | solution.py:166
  19.2 2.0 %collective-permute-done.1 = f32[17,1024]{1,0:T(8,128)S(1)} collective-permute-done((f32[17,1024]{1,0:T(8,128)S(1)}, f32[17,1024]{1,0:T(8,128)S(1)}, u32[]{:S(2)}, u32[]{:S(2)}) %collective-permute-start.1) | collective-permute-done | bytes 69664 | tf_op jit(solution)/shard_map/ppermute | solution.py:166
  21.2 8.6 %collective-permute-start.2 = (f32[17,1024]{1,0:T(8,128)S(1)}, f32[17,1024]{1,0:T(8,128)S(1)}, u32[]{:S(2)}, u32[]{:S(2)}) collective-permute-start(f32[17,1024]{1,0:T(8,128)S(1)} %pad_maximum_fusion.1), channel_id=1, source_target_pairs={{0,32},{8,40},{16,48},{24,56},{32,0},{40,8},{48,16},{56,24},{64,96... | collective-permute-start | bytes 208904 | tf_op jit(solution)/shard_map/ppermute | solution.py:166
  29.8 2.1 %collective-permute-done.2 = f32[17,1024]{1,0:T(8,128)S(1)} collective-permute-done((f32[17,1024]{1,0:T(8,128)S(1)}, f32[17,1024]{1,0:T(8,128)S(1)}, u32[]{:S(2)}, u32[]{:S(2)}) %collective-permute-start.2) | collective-permute-done | bytes 69664 | tf_op jit(solution)/shard_map/ppermute | solution.py:166
  31.9 4.0 %collective-permute-start.3 = (f32[17,1024]{1,0:T(8,128)S(1)}, f32[17,1024]{1,0:T(8,128)S(1)}, u32[]{:S(2)}, u32[]{:S(2)}) collective-permute-start(f32[17,1024]{1,0:T(8,128)S(1)} %pad_maximum_fusion.2), channel_id=1, source_target_pairs={{0,64},{8,72},{16,80},{24,88},{32,96},{40,104},{48,112},{56,120},{... | collective-permute-start | bytes 208904 | tf_op jit(solution)/shard_map/ppermute | solution.py:166
  36.0 2.0 %collective-permute-done.3 = f32[17,1024]{1,0:T(8,128)S(1)} collective-permute-done((f32[17,1024]{1,0:T(8,128)S(1)}, f32[17,1024]{1,0:T(8,128)S(1)}, u32[]{:S(2)}, u32[]{:S(2)}) %collective-permute-start.3) | collective-permute-done | bytes 69664 | tf_op jit(solution)/shard_map/ppermute | solution.py:166
  38.0 5.8 %collective-permute-start.4 = (f32[17,1024]{1,0:T(8,128)S(1)}, f32[17,1024]{1,0:T(8,128)S(1)}, u32[]{:S(2)}, u32[]{:S(2)}) collective-permute-start(f32[17,1024]{1,0:T(8,128)S(1)} %pad_maximum_fusion.3), channel_id=1, source_target_pairs={{0,128},{8,136},{16,144},{24,152},{32,160},{40,168},{48,176},{56,1... | collective-permute-start | bytes 208904 | tf_op jit(solution)/shard_map/ppermute | solution.py:166
  43.8 2.3 %collective-permute-done.4 = f32[17,1024]{1,0:T(8,128)S(1)} collective-permute-done((f32[17,1024]{1,0:T(8,128)S(1)}, f32[17,1024]{1,0:T(8,128)S(1)}, u32[]{:S(2)}, u32[]{:S(2)}) %collective-permute-start.4) | collective-permute-done | bytes 69664 | tf_op jit(solution)/shard_map/ppermute | solution.py:166
  46.1 10.3 %collective-permute-start.5 = (f32[17,1024]{1,0:T(8,128)S(1)}, f32[17,1024]{1,0:T(8,128)S(1)}, u32[]{:S(2)}, u32[]{:S(2)}) collective-permute-start(f32[17,1024]{1,0:T(8,128)S(1)} %pad_maximum_fusion.4), channel_id=1, source_target_pairs={{0,256},{8,264},{16,272},{24,280},{32,288},{40,296},{48,304},{56,3... | collective-permute-start | bytes 208904 | tf_op jit(solution)/shard_map/ppermute | solution.py:166
  56.5 2.5 %collective-permute-done.5 = f32[17,1024]{1,0:T(8,128)S(1)} collective-permute-done((f32[17,1024]{1,0:T(8,128)S(1)}, f32[17,1024]{1,0:T(8,128)S(1)}, u32[]{:S(2)}, u32[]{:S(2)}) %collective-permute-start.5) | collective-permute-done | bytes 69664 | tf_op jit(solution)/shard_map/ppermute | solution.py:166
  59.1 13.2 %collective-permute-start.6 = (f32[17,1024]{1,0:T(8,128)S(1)}, f32[17,1024]{1,0:T(8,128)S(1)}, u32[]{:S(2)}, u32[]{:S(2)}) collective-permute-start(f32[17,1024]{1,0:T(8,128)S(1)} %pad_maximum_fusion.5), channel_id=1, source_target_pairs={{0,512},{8,520},{16,528},{24,536},{32,544},{40,552},{48,560},{56,5... | collective-permute-start | bytes 208904 | tf_op jit(solution)/shard_map/ppermute | solution.py:166
  72.3 2.1 %collective-permute-done.6 = f32[17,1024]{1,0:T(8,128)S(1)} collective-permute-done((f32[17,1024]{1,0:T(8,128)S(1)}, f32[17,1024]{1,0:T(8,128)S(1)}, u32[]{:S(2)}, u32[]{:S(2)}) %collective-permute-start.6) | collective-permute-done | bytes 69664 | tf_op jit(solution)/shard_map/ppermute | solution.py:166
  74.4 0.7 add_select_fusion.inc_ref
  75.1 12.4 %shard_map.87 = (bf16[256,1024]{1,0:T(8,128)(2,1)}, f32[16,256]{1,0:T(8,128)}) custom-call(bf16[256,1024]{1,0:T(8,128)(2,1)} %g_ref.3, bf16[256,1024]{1,0:T(8,128)(2,1)} %s_ref.3, bf16[256,1024]{1,0:T(8,128)(2,1)} %x_ref.1, f32[16,256]{1,0:T(8,128)} %bitcast.31, f32[16,256]{1,0:T(8,128)} %bitcast.33, f32[16,1024]{1,0:T(8,128)} %a_ref.3, f32[1,1024]{1,0:T(1,128)} %bitcast.34, ...), custom_call_target="tpu_custom_call" | custom-call | flops 50331648 | bytes 2162688 | tf_op jit(solution)/shard_map/pallas_call | solution.py:122
  87.5 0.7 broadcast_multiply_fusion
  88.4 23.6 %all_to_all.5 = f32[8,1,512]{2,1,0:T(1,128)S(1)} all-to-all(f32[8,1,512]{2,1,0:T(1,128)S(1)} %reshape.8), channel_id=1, replica_groups=mesh['ctx'=128,'exp'=8] {'exp'}, dimensions={0} | all-to-all | bytes 32768 | tf_op jit(solution)/shard_map/all_to_all | solution.py:188
  112.0 0.5 broadcast.14
  112.5 0.7 reduce
  113.3 0.6 reduce_sum.9
  (22 shorter events, 0.5 us)
Async XLA Ops:
  0.6 13.3 %copy-start = (f32[16,1024]{1,0:T(8,128)S(1)}, f32[16,1024]{1,0:T(8,128)}, u32[]{:S(2)}) copy-start(f32[16,1024]{1,0:T(8,128)} %a_ref.3) | copy-start | bytes 196612
  6.9 6.2 %collective-permute-start = (f32[17,1024]{1,0:T(8,128)}, f32[17,1024]{1,0:T(8,128)S(1)}, u32[]{:S(2)}, u32[]{:S(2)}) collective-permute-start(f32[17,1024]{1,0:T(8,128)} %shard_map.86), channel_id=1, source_target_pairs={{0,8},{8,0},{16,24},{24,16},{32,40},{40,32},{48,56},{56,48},{64,72... | collective-permute-start | bytes 208904 | tf_op jit(solution)/shard_map/ppermute | solution.py:166
  14.8 6.4 %collective-permute-start.1 = (f32[17,1024]{1,0:T(8,128)S(1)}, f32[17,1024]{1,0:T(8,128)S(1)}, u32[]{:S(2)}, u32[]{:S(2)}) collective-permute-start(f32[17,1024]{1,0:T(8,128)S(1)} %pad_maximum_fusion), channel_id=1, source_target_pairs={{0,16},{8,24},{16,0},{24,8},{32,48},{40,56},{48,32},{56,40},{64,80... | collective-permute-start | bytes 208904 | tf_op jit(solution)/shard_map/ppermute | solution.py:166
  21.2 10.7 %collective-permute-start.2 = (f32[17,1024]{1,0:T(8,128)S(1)}, f32[17,1024]{1,0:T(8,128)S(1)}, u32[]{:S(2)}, u32[]{:S(2)}) collective-permute-start(f32[17,1024]{1,0:T(8,128)S(1)} %pad_maximum_fusion.1), channel_id=1, source_target_pairs={{0,32},{8,40},{16,48},{24,56},{32,0},{40,8},{48,16},{56,24},{64,96... | collective-permute-start | bytes 208904 | tf_op jit(solution)/shard_map/ppermute | solution.py:166
  31.9 6.0 %collective-permute-start.3 = (f32[17,1024]{1,0:T(8,128)S(1)}, f32[17,1024]{1,0:T(8,128)S(1)}, u32[]{:S(2)}, u32[]{:S(2)}) collective-permute-start(f32[17,1024]{1,0:T(8,128)S(1)} %pad_maximum_fusion.2), channel_id=1, source_target_pairs={{0,64},{8,72},{16,80},{24,88},{32,96},{40,104},{48,112},{56,120},{... | collective-permute-start | bytes 208904 | tf_op jit(solution)/shard_map/ppermute | solution.py:166
  38.0 8.1 %collective-permute-start.4 = (f32[17,1024]{1,0:T(8,128)S(1)}, f32[17,1024]{1,0:T(8,128)S(1)}, u32[]{:S(2)}, u32[]{:S(2)}) collective-permute-start(f32[17,1024]{1,0:T(8,128)S(1)} %pad_maximum_fusion.3), channel_id=1, source_target_pairs={{0,128},{8,136},{16,144},{24,152},{32,160},{40,168},{48,176},{56,1... | collective-permute-start | bytes 208904 | tf_op jit(solution)/shard_map/ppermute | solution.py:166
  46.1 12.9 %collective-permute-start.5 = (f32[17,1024]{1,0:T(8,128)S(1)}, f32[17,1024]{1,0:T(8,128)S(1)}, u32[]{:S(2)}, u32[]{:S(2)}) collective-permute-start(f32[17,1024]{1,0:T(8,128)S(1)} %pad_maximum_fusion.4), channel_id=1, source_target_pairs={{0,256},{8,264},{16,272},{24,280},{32,288},{40,296},{48,304},{56,3... | collective-permute-start | bytes 208904 | tf_op jit(solution)/shard_map/ppermute | solution.py:166
  59.1 15.3 %collective-permute-start.6 = (f32[17,1024]{1,0:T(8,128)S(1)}, f32[17,1024]{1,0:T(8,128)S(1)}, u32[]{:S(2)}, u32[]{:S(2)}) collective-permute-start(f32[17,1024]{1,0:T(8,128)S(1)} %pad_maximum_fusion.5), channel_id=1, source_target_pairs={{0,512},{8,520},{16,528},{24,536},{32,544},{40,552},{48,560},{56,5... | collective-permute-start | bytes 208904 | tf_op jit(solution)/shard_map/ppermute | solution.py:166

commit v16 on v14

--- a/solution.py
+++ b/solution.py
@@ -85,7 +85,7 @@
             return (jnp.exp2(s_row * a) * adjoint, gathered)
 
         start = (incoming, jnp.zeros((states, LANES), jnp.float32))
-        incoming, gathered = lax.fori_loop(0, LANES, body, start, unroll=32)
+        incoming, gathered = lax.fori_loop(0, LANES, body, start, unroll=64)
         bt_ref[:, base:base + LANES] = gathered
         return incoming
 

time: 115 us -> 119 us (1.035)
  Pallas kernels: 19.1 us -> 23.6 us
    pallas_call x1, Pallas kernels: 12.4 us -> 16.9 us  [shard_sweep(): pl.pallas_call(sweep_kernel, out_shape=(jax.ShapeDtypeStruct((rows, chann...]
where the time goes in v16:
time: 119 us
  starting transfers between devices  50.2 us (42%)
  Pallas kernels  23.6 us (20%)
  blocking collectives  23.6 us (20%)
  waiting for transfers between devices  15 us (13%)
  other arithmetic  4.59 us (4%)
    ppermute x7, starting transfers between devices, carry_in(): got = lax.ppermute(packed, 'ctx', [(q, q ^ bit) for q in range(size)])  50.2 us
    all_to_all x1, blocking collectives, exchange_sum(): got = lax.all_to_all(pieces, axis, 0, 0, tiled=True)  23.6 us
    pallas_call x1, Pallas kernels, shard_sweep(): pl.pallas_call(sweep_kernel, out_shape=(jax.ShapeDtypeStruct((rows, chann...  16.9 us
    ppermute x7, waiting for transfers between devices, carry_in(): got = lax.ppermute(packed, 'ctx', [(q, q ^ bit) for q in range(size)])  15 us
    pallas_call x1, Pallas kernels, shard_summary(): pl.pallas_call(summary_kernel, out_shape=jax.ShapeDtypeStruct((states + 1...  6.73 us
  transfers between devices with their start and end apart: 7, of which 7 were waited for; matrix products, arithmetic and copies ran while one was open for 0% of the time, Pallas kernels for 0%

profile of v16, /device:TPU:1, one launch (start us, length us, event | category | flops | bytes accessed | tf_op | source)
XLA Modules:
  0.0 118.9 jit_solution(13449498716165001523)
XLA Ops:
  0.6 6.7 %shard_map.86 = f32[17,1024]{1,0:T(8,128)} custom-call(bf16[256,1024]{1,0:T(8,128)(2,1)} %g_ref.3, bf16[256,1024]{1,0:T(8,128)(2,1)} %s_ref.3, f32[16,256]{1,0:T(8,128)} %bitcast.32, f32[16,1024]{1,0:T(8,128)} %a_ref.3), custom_call_target="tpu_custom_call" | custom-call | flops 25165824 | bytes 1064960 | tf_op jit(solution)/shard_map/pallas_call | solution.py:105
  7.4 4.0 %collective-permute-start = (f32[17,1024]{1,0:T(8,128)}, f32[17,1024]{1,0:T(8,128)S(1)}, u32[]{:S(2)}, u32[]{:S(2)}) collective-permute-start(f32[17,1024]{1,0:T(8,128)} %shard_map.86), channel_id=1, source_target_pairs={{0,8},{8,0},{16,24},{24,16},{32,40},{40,32},{48,56},{56,48},{64,72... | collective-permute-start | bytes 208904 | tf_op jit(solution)/shard_map/ppermute | solution.py:166
  11.4 2.2 %collective-permute-done = f32[17,1024]{1,0:T(8,128)S(1)} collective-permute-done((f32[17,1024]{1,0:T(8,128)}, f32[17,1024]{1,0:T(8,128)S(1)}, u32[]{:S(2)}, u32[]{:S(2)}) %collective-permute-start) | collective-permute-done | bytes 69664 | tf_op jit(solution)/shard_map/ppermute | solution.py:166
  13.6 0.8 broadcast_select_fusion.10
  14.4 0.9 multiply_add_fusion.5
  15.3 4.4 %collective-permute-start.1 = (f32[17,1024]{1,0:T(8,128)S(1)}, f32[17,1024]{1,0:T(8,128)S(1)}, u32[]{:S(2)}, u32[]{:S(2)}) collective-permute-start(f32[17,1024]{1,0:T(8,128)S(1)} %pad_maximum_fusion), channel_id=1, source_target_pairs={{0,16},{8,24},{16,0},{24,8},{32,48},{40,56},{48,32},{56,40},{64,80... | collective-permute-start | bytes 208904 | tf_op jit(solution)/shard_map/ppermute | solution.py:166
  19.7 2.0 %collective-permute-done.1 = f32[17,1024]{1,0:T(8,128)S(1)} collective-permute-done((f32[17,1024]{1,0:T(8,128)S(1)}, f32[17,1024]{1,0:T(8,128)S(1)}, u32[]{:S(2)}, u32[]{:S(2)}) %collective-permute-start.1) | collective-permute-done | bytes 69664 | tf_op jit(solution)/shard_map/ppermute | solution.py:166
  21.7 8.6 %collective-permute-start.2 = (f32[17,1024]{1,0:T(8,128)S(1)}, f32[17,1024]{1,0:T(8,128)S(1)}, u32[]{:S(2)}, u32[]{:S(2)}) collective-permute-start(f32[17,1024]{1,0:T(8,128)S(1)} %pad_maximum_fusion.1), channel_id=1, source_target_pairs={{0,32},{8,40},{16,48},{24,56},{32,0},{40,8},{48,16},{56,24},{64,96... | collective-permute-start | bytes 208904 | tf_op jit(solution)/shard_map/ppermute | solution.py:166
  30.3 2.1 %collective-permute-done.2 = f32[17,1024]{1,0:T(8,128)S(1)} collective-permute-done((f32[17,1024]{1,0:T(8,128)S(1)}, f32[17,1024]{1,0:T(8,128)S(1)}, u32[]{:S(2)}, u32[]{:S(2)}) %collective-permute-start.2) | collective-permute-done | bytes 69664 | tf_op jit(solution)/shard_map/ppermute | solution.py:166
  32.4 4.0 %collective-permute-start.3 = (f32[17,1024]{1,0:T(8,128)S(1)}, f32[17,1024]{1,0:T(8,128)S(1)}, u32[]{:S(2)}, u32[]{:S(2)}) collective-permute-start(f32[17,1024]{1,0:T(8,128)S(1)} %pad_maximum_fusion.2), channel_id=1, source_target_pairs={{0,64},{8,72},{16,80},{24,88},{32,96},{40,104},{48,112},{56,120},{... | collective-permute-start | bytes 208904 | tf_op jit(solution)/shard_map/ppermute | solution.py:166
  36.4 2.0 %collective-permute-done.3 = f32[17,1024]{1,0:T(8,128)S(1)} collective-permute-done((f32[17,1024]{1,0:T(8,128)S(1)}, f32[17,1024]{1,0:T(8,128)S(1)}, u32[]{:S(2)}, u32[]{:S(2)}) %collective-permute-start.3) | collective-permute-done | bytes 69664 | tf_op jit(solution)/shard_map/ppermute | solution.py:166
  38.4 5.8 %collective-permute-start.4 = (f32[17,1024]{1,0:T(8,128)S(1)}, f32[17,1024]{1,0:T(8,128)S(1)}, u32[]{:S(2)}, u32[]{:S(2)}) collective-permute-start(f32[17,1024]{1,0:T(8,128)S(1)} %pad_maximum_fusion.3), channel_id=1, source_target_pairs={{0,128},{8,136},{16,144},{24,152},{32,160},{40,168},{48,176},{56,1... | collective-permute-start | bytes 208904 | tf_op jit(solution)/shard_map/ppermute | solution.py:166
  44.3 2.3 %collective-permute-done.4 = f32[17,1024]{1,0:T(8,128)S(1)} collective-permute-done((f32[17,1024]{1,0:T(8,128)S(1)}, f32[17,1024]{1,0:T(8,128)S(1)}, u32[]{:S(2)}, u32[]{:S(2)}) %collective-permute-start.4) | collective-permute-done | bytes 69664 | tf_op jit(solution)/shard_map/ppermute | solution.py:166
  46.6 10.3 %collective-permute-start.5 = (f32[17,1024]{1,0:T(8,128)S(1)}, f32[17,1024]{1,0:T(8,128)S(1)}, u32[]{:S(2)}, u32[]{:S(2)}) collective-permute-start(f32[17,1024]{1,0:T(8,128)S(1)} %pad_maximum_fusion.4), channel_id=1, source_target_pairs={{0,256},{8,264},{16,272},{24,280},{32,288},{40,296},{48,304},{56,3... | collective-permute-start | bytes 208904 | tf_op jit(solution)/shard_map/ppermute | solution.py:166
  57.0 2.5 %collective-permute-done.5 = f32[17,1024]{1,0:T(8,128)S(1)} collective-permute-done((f32[17,1024]{1,0:T(8,128)S(1)}, f32[17,1024]{1,0:T(8,128)S(1)}, u32[]{:S(2)}, u32[]{:S(2)}) %collective-permute-start.5) | collective-permute-done | bytes 69664 | tf_op jit(solution)/shard_map/ppermute | solution.py:166
  59.6 13.2 %collective-permute-start.6 = (f32[17,1024]{1,0:T(8,128)S(1)}, f32[17,1024]{1,0:T(8,128)S(1)}, u32[]{:S(2)}, u32[]{:S(2)}) collective-permute-start(f32[17,1024]{1,0:T(8,128)S(1)} %pad_maximum_fusion.5), channel_id=1, source_target_pairs={{0,512},{8,520},{16,528},{24,536},{32,544},{40,552},{48,560},{56,5... | collective-permute-start | bytes 208904 | tf_op jit(solution)/shard_map/ppermute | solution.py:166
  72.8 2.1 %collective-permute-done.6 = f32[17,1024]{1,0:T(8,128)S(1)} collective-permute-done((f32[17,1024]{1,0:T(8,128)S(1)}, f32[17,1024]{1,0:T(8,128)S(1)}, u32[]{:S(2)}, u32[]{:S(2)}) %collective-permute-start.6) | collective-permute-done | bytes 69664 | tf_op jit(solution)/shard_map/ppermute | solution.py:166
  74.9 0.7 add_select_fusion.inc_ref
  75.6 16.9 %shard_map.87 = (bf16[256,1024]{1,0:T(8,128)(2,1)}, f32[16,256]{1,0:T(8,128)}) custom-call(bf16[256,1024]{1,0:T(8,128)(2,1)} %g_ref.3, bf16[256,1024]{1,0:T(8,128)(2,1)} %s_ref.3, bf16[256,1024]{1,0:T(8,128)(2,1)} %x_ref.1, f32[16,256]{1,0:T(8,128)} %bitcast.31, f32[16,256]{1,0:T(8,128)} %bitcast.33, f32[16,1024]{1,0:T(8,128)} %a_ref.3, f32[1,1024]{1,0:T(1,128)} %bitcast.34, ...), custom_call_target="tpu_custom_call" | custom-call | flops 50331648 | bytes 2162688 | tf_op jit(solution)/shard_map/pallas_call | solution.py:122
  92.5 0.7 broadcast_multiply_fusion
  93.4 23.6 %all_to_all.5 = f32[8,1,512]{2,1,0:T(1,128)S(1)} all-to-all(f32[8,1,512]{2,1,0:T(1,128)S(1)} %reshape.8), channel_id=1, replica_groups=mesh['ctx'=128,'exp'=8] {'exp'}, dimensions={0} | all-to-all | bytes 32768 | tf_op jit(solution)/shard_map/all_to_all | solution.py:188
  117.0 0.5 broadcast.14
  117.5 0.7 reduce
  118.3 0.6 reduce_sum.9
  (22 shorter events, 0.5 us)
Async XLA Ops:
  0.6 13.7 %copy-start = (f32[16,1024]{1,0:T(8,128)S(1)}, f32[16,1024]{1,0:T(8,128)}, u32[]{:S(2)}) copy-start(f32[16,1024]{1,0:T(8,128)} %a_ref.3) | copy-start | bytes 196612
  7.4 6.2 %collective-permute-start = (f32[17,1024]{1,0:T(8,128)}, f32[17,1024]{1,0:T(8,128)S(1)}, u32[]{:S(2)}, u32[]{:S(2)}) collective-permute-start(f32[17,1024]{1,0:T(8,128)} %shard_map.86), channel_id=1, source_target_pairs={{0,8},{8,0},{16,24},{24,16},{32,40},{40,32},{48,56},{56,48},{64,72... | collective-permute-start | bytes 208904 | tf_op jit(solution)/shard_map/ppermute | solution.py:166
  15.3 6.4 %collective-permute-start.1 = (f32[17,1024]{1,0:T(8,128)S(1)}, f32[17,1024]{1,0:T(8,128)S(1)}, u32[]{:S(2)}, u32[]{:S(2)}) collective-permute-start(f32[17,1024]{1,0:T(8,128)S(1)} %pad_maximum_fusion), channel_id=1, source_target_pairs={{0,16},{8,24},{16,0},{24,8},{32,48},{40,56},{48,32},{56,40},{64,80... | collective-permute-start | bytes 208904 | tf_op jit(solution)/shard_map/ppermute | solution.py:166
  21.7 10.7 %collective-permute-start.2 = (f32[17,1024]{1,0:T(8,128)S(1)}, f32[17,1024]{1,0:T(8,128)S(1)}, u32[]{:S(2)}, u32[]{:S(2)}) collective-permute-start(f32[17,1024]{1,0:T(8,128)S(1)} %pad_maximum_fusion.1), channel_id=1, source_target_pairs={{0,32},{8,40},{16,48},{24,56},{32,0},{40,8},{48,16},{56,24},{64,96... | collective-permute-start | bytes 208904 | tf_op jit(solution)/shard_map/ppermute | solution.py:166
  32.4 6.0 %collective-permute-start.3 = (f32[17,1024]{1,0:T(8,128)S(1)}, f32[17,1024]{1,0:T(8,128)S(1)}, u32[]{:S(2)}, u32[]{:S(2)}) collective-permute-start(f32[17,1024]{1,0:T(8,128)S(1)} %pad_maximum_fusion.2), channel_id=1, source_target_pairs={{0,64},{8,72},{16,80},{24,88},{32,96},{40,104},{48,112},{56,120},{... | collective-permute-start | bytes 208904 | tf_op jit(solution)/shard_map/ppermute | solution.py:166
  38.4 8.1 %collective-permute-start.4 = (f32[17,1024]{1,0:T(8,128)S(1)}, f32[17,1024]{1,0:T(8,128)S(1)}, u32[]{:S(2)}, u32[]{:S(2)}) collective-permute-start(f32[17,1024]{1,0:T(8,128)S(1)} %pad_maximum_fusion.3), channel_id=1, source_target_pairs={{0,128},{8,136},{16,144},{24,152},{32,160},{40,168},{48,176},{56,1... | collective-permute-start | bytes 208904 | tf_op jit(solution)/shard_map/ppermute | solution.py:166
  46.6 12.9 %collective-permute-start.5 = (f32[17,1024]{1,0:T(8,128)S(1)}, f32[17,1024]{1,0:T(8,128)S(1)}, u32[]{:S(2)}, u32[]{:S(2)}) collective-permute-start(f32[17,1024]{1,0:T(8,128)S(1)} %pad_maximum_fusion.4), channel_id=1, source_target_pairs={{0,256},{8,264},{16,272},{24,280},{32,288},{40,296},{48,304},{56,3... | collective-permute-start | bytes 208904 | tf_op jit(solution)/shard_map/ppermute | solution.py:166
  59.6 15.3 %collective-permute-start.6 = (f32[17,1024]{1,0:T(8,128)S(1)}, f32[17,1024]{1,0:T(8,128)S(1)}, u32[]{:S(2)}, u32[]{:S(2)}) collective-permute-start(f32[17,1024]{1,0:T(8,128)S(1)} %pad_maximum_fusion.5), channel_id=1, source_target_pairs={{0,512},{8,520},{16,528},{24,536},{32,544},{40,552},{48,560},{56,5... | collective-permute-start | bytes 208904 | tf_op jit(solution)/shard_map/ppermute | solution.py:166
